TPU v7x, 256 devices: a whole 4x4x8 slice. The times are simulated.
256 devices in a mesh: tm: 8 (over z), owner: 32 (over y, x, core).
Axes of the slice: x: 4, y: 4, z: 8, core: 2. Of those that a mesh axis runs over, the one named last changes fastest.
Arguments:
- pressure: bfloat16 [512, 262144], P('tm', 'owner'), may hold values from -6 to 6
- proj_weight: bfloat16 [32, 64, 4, 128, 128], P('owner', 'tm'), may hold values from -0.1875 to 0.1875
- pattern: int32 [32, 64, 4], P('owner', 'tm'), may hold values from 0 to 31, as said below
- panel_list: int32 [32, 32], replicated, may hold values from 0 to 767, as said below
- owner_list: int32 [32, 36], replicated, may hold values from -1 to 767, as said below
- owner_count: int32 [32], replicated, may hold values from 12 to 36, as said below
Outputs:
- panel_field: float32 [1152, 512, 128], P('owner', 'tm')
Inputs may be any that keep to these rules, and one draw needn't show every extreme that they name: `pattern`: the 4 entries of one face block are different. `panel_list`: each row names different panel blocks, owned by 16 different owners, exactly 2 of each. `owner_list`: slots below an owner's count hold its panel blocks; every panel block stands in exactly one such slot; slots from the count on hold -1. `owner_count`: the counts sum to 768.
All inputs are finite; a program needn't handle non-finite values.
Results may differ from a plain program's by a relative error of at most 0.0003.
Values may be sent and summed in bfloat16 or wider, within the bound.
No kernel may reach another device: no remote copies, remote signals or barrier semaphores. Data moves between devices by JAX's collectives and lax.ppermute only.
A program may use at most 128 MiB of HBM per device.

v0:
```python
import jax
import jax.numpy as jnp
from jax import lax
from jax.sharding import PartitionSpec as P


def routing_tables(panel_list, owner_list, owner_count, slot_count):
    owner_size, list_len = panel_list.shape
    capacity = owner_list.shape[1]
    owners = jnp.arange(owner_size, dtype=jnp.int32)
    owned_slots = jnp.arange(capacity, dtype=jnp.int32)[None, :] < owner_count[:, None]
    matches = (panel_list[:, :, None, None] == owner_list[None, None, :, :]) & owned_slots[
        None, None, :, :
    ]
    target = jnp.sum(jnp.where(matches, owners[None, None, :, None], 0), axis=(2, 3))
    position = jnp.arange(list_len, dtype=jnp.int32)
    earlier = (target[:, :, None] == target[:, None, :]) & (
        position[None, None, :] < position[None, :, None]
    )
    order_rank = jnp.sum(earlier.astype(jnp.int32), axis=2)
    slot_ids = jnp.arange(slot_count, dtype=jnp.int32)
    placed = (target[:, :, None, None] == owners[None, None, :, None]) & (
        order_rank[:, :, None, None] == slot_ids[None, None, None, :]
    )
    filled = jnp.sum(placed.astype(jnp.int32), axis=1)
    source_row = jnp.sum(jnp.where(placed, position[None, :, None, None], 0), axis=1) + list_len * (
        1 - filled
    )
    carried = jnp.sum(jnp.where(placed, panel_list[:, :, None, None], 0), axis=1) - (1 - filled)
    return (source_row, carried)


def pack_rows(values, outgoing, owner_size, slot_count):
    padded = jnp.concatenate([values, jnp.zeros((1,) + values.shape[1:], jnp.float32)], axis=0)
    packed = jnp.take(padded, outgoing, axis=0)
    return packed.reshape((owner_size, slot_count) + values.shape[1:])


def collect(received, slot_panels, owner_list, owner_count, own_index):
    capacity = owner_list.shape[1]
    wanted = owner_list[own_index]
    live_count = owner_count[own_index]
    slot_ids = jnp.arange(capacity, dtype=jnp.int32)
    live_slots = slot_ids < live_count
    incoming = slot_panels.reshape(-1)
    match = (incoming[:, None] == wanted[None, :]) & live_slots[None, :]
    found = jnp.sum(match.astype(jnp.int32), axis=1)
    dest = jnp.sum(jnp.where(match, slot_ids[None, :], 0), axis=1) + capacity * (1 - found)
    flat_rows = received.reshape((incoming.shape[0],) + received.shape[2:])
    combined = jax.ops.segment_sum(flat_rows, dest, num_segments=capacity + 1)
    return combined[:capacity]


def body(pressure, proj_weight, pattern, panel_list, owner_list, owner_count):
    owner_size = lax.axis_size("owner")
    own_index = lax.axis_index("owner")
    series = lax.all_to_all(pressure, "tm", split_axis=1, concat_axis=0, tiled=True)
    time_len = series.shape[0]
    fb_dev = pattern.shape[1]
    block_len = proj_weight.shape[-1]
    list_len = panel_list.shape[1]
    slot_count = max(2, list_len // owner_size)
    series = series.reshape(time_len, fb_dev, block_len)
    contrib = jnp.einsum(
        "tia,ikab->iktb", series, proj_weight[0], preferred_element_type=jnp.float32
    )
    flat_contrib = contrib.reshape((-1, time_len, block_len))
    partial_value = (
        jnp.zeros((list_len, time_len, block_len), jnp.float32)
        .at[pattern[0].reshape(-1)]
        .add(flat_contrib)
    )
    source_row, carried = routing_tables(panel_list, owner_list, owner_count, slot_count)
    outgoing = jnp.take(source_row, own_index, axis=0).reshape(-1)
    slot_panels = jnp.take(carried, own_index, axis=1)
    packed = pack_rows(partial_value, outgoing, owner_size, slot_count)
    received = lax.all_to_all(packed, "owner", split_axis=0, concat_axis=0, tiled=True)
    combined = collect(received, slot_panels, owner_list, owner_count, own_index)
    return lax.psum_scatter(combined, "tm", scatter_dimension=1, tiled=True)


def solution(mesh):
    placed = (
        P("tm", "owner"),
        P("owner", "tm", None, None, None),
        P("owner", "tm", None),
        P(),
        P(),
        P(),
    )
    return jax.shard_map(
        body, mesh=mesh, in_specs=placed, out_specs=P("owner", "tm", None), check_vma=False
    )
```

profile of v0, /device:TPU:1, one launch (start us, length us, event | category | flops | bytes accessed | tf_op | source)
XLA Modules:
  0.0 490.4 jit_solution(2496817232864158563)
XLA Ops:
  6.5 0.0 copy-start
  6.5 2.4 copy.34
  8.9 9.0 %all-to-all-start = ((bf16[64,8,1024]{2,0,1:T(8,128)(2,1)}), bf16[64,8,1024]{2,0,1:T(8,128)(2,1)S(1)}, u32[]{:S(2)}, u32[]{:S(2)}) async-start(bf16[64,8,1024]{2,0,1:T(8,128)(2,1)} %bitcast.26), calls=%async_computation | async-start | bytes 2097152 | tf_op jit(solution)/shard_map/all_to_all | solution.py:57
  17.9 0.7 iota_compare_fusion.3
  18.6 20.8 %select_reduce_fusion = s32[32,32]{1,0:T(8,128)S(1)} fusion(s32[32,36]{1,0:T(8,128)} %param.10, s32[32,32]{1,0:T(8,128)} %param.9, pred[32,36]{1,0:T(8,128)(4,1)S(1)} %iota_compare_fusion.3), kind=kLoop, calls=%fused_computation.3 | loop fusion | flops 4717568 | bytes 13952 | tf_op jit(solution)/shard_map/reduce_sum | solution.py:15
  39.4 0.8 copy.19
  40.2 0.1 reshape_squeeze.3
  40.3 0.8 convert_reduce_fusion
  41.1 0.2 iota_compare_fusion
  41.3 1.7 fusion.2
  43.0 0.1 copy.18
  43.2 0.1 copy.24
  43.2 0.1 select_n.96
  43.4 3.7 all-to-all-done
  47.1 0.3 copy.30
  47.4 0.0 copy-done
  47.4 4.5 fusion.3
  51.9 9.0 %copy.23 = f32[32,512,128]{2,1,0:T(8,128)} copy(f32[32,512,128]{1,2,0:T(8,128)} %bitcast.28) | data formatting | bytes 16777216 | tf_op jit(solution)/shard_map/reshape | solution.py:67
  60.9 4.2 broadcast_in_dim.113
  65.0 18.8 %scatter_fusion = f32[32,512,128]{2,1,0:T(8,128)} fusion(f32[32,512,128]{2,1,0:T(8,128)} %broadcast_in_dim.113, s32[32]{0:T(128)S(1)} %fusion.12, f32[32,512,128]{2,1,0:T(8,128)} %copy.23), kind=kCustom, calls=%fused_computation.1 | custom fusion | flops 2097152 | bytes 25165952 | tf_op jit(solution)/shard_map/scatter-add | solution.py:71
  83.9 7.7 %concatenate.3 = f32[33,512,128]{2,1,0:T(8,128)} pad(f32[32,512,128]{2,1,0:T(8,128)} %scatter_fusion, f32[]{:T(128)} %constant.25.clone.1), padding=0_1x0_0x0_0 | pad | bytes 17039364 | tf_op jit(solution)/shard_map/concatenate | solution.py:34
  91.6 12.3 %gather_fusion = f32[64,512,128]{2,1,0:T(8,128)} fusion(f32[33,512,128]{2,1,0:T(8,128)} %concatenate.3, s32[1024]{0:T(1024)S(1)} %pad_clamp_fusion), kind=kCustom, calls=%fused_computation | custom fusion | bytes 33554688 | tf_op jit(solution)/shard_map/jit(_take)/gather | solution.py:35
  103.8 11.6 %broadcast_select_fusion = f32[32,2,512,128]{3,2,1,0:T(8,128)} fusion(f32[32,2,512,128]{3,2,1,0:T(8,128)} %bitcast.27, pred[32,2]{1,0:T(8,128)(4,1)S(1)} %copy.18), kind=kLoop, calls=%fused_computation.4 | loop fusion | flops 4194304 | bytes 33554496 | tf_op jit(solution)/shard_map/jit(_take)/select_n | solution.py:35
  115.4 0.0 copy-start.2
  115.4 7.5 %all-to-all-start.1 = ((f32[32,2,512,128]{3,2,1,0:T(8,128)}), f32[32,2,512,128]{3,2,1,0:T(8,128)}, u32[]{:S(2)}, u32[]{:S(2)}) async-start(f32[32,2,512,128]{3,2,1,0:T(8,128)} %broadcast_select_fusion), calls=%async_computation.1 | async-start | bytes 33554432 | tf_op jit(solution)/shard_map/all_to_all | solution.py:77
  122.9 0.0 reduce-scatter.2.cloned.1.call-start
  122.9 0.0 copy-done.2
  122.9 0.6 dynamic_slice.7
  123.5 0.7 fusion.7
  124.2 0.1 select_n.90
  124.3 0.7 fusion.11
  125.0 0.6 iota_compare_fusion.4
  125.7 0.1 convert_reduce_fusion.1
  125.8 199.1 %all-to-all-done.1 = f32[32,2,512,128]{3,2,1,0:T(8,128)} async-done(((f32[32,2,512,128]{3,2,1,0:T(8,128)}), f32[32,2,512,128]{3,2,1,0:T(8,128)}, u32[]{:S(2)}, u32[]{:S(2)}) %all-to-all-start.1) | async-done | bytes 16777248 | tf_op jit(solution)/shard_map/all_to_all | solution.py:77
  324.9 4.9 broadcast_in_dim.101
  329.8 0.0 copy-start.1
  329.8 35.9 %scatter_fusion.1 = f32[37,512,128]{2,1,0:T(8,128)} fusion(f32[37,512,128]{2,1,0:T(8,128)} %broadcast_in_dim.101, s32[64]{0:T(128)S(1)} %multiply_add_fusion, f32[64,512,128]{2,1,0:T(8,128)} %bitcast.11), kind=kCustom, calls=%fused_computation.2 | custom fusion | flops 4194304 | bytes 50331904 | tf_op jit(solution)/shard_map/scatter-add | solution.py:50
  365.7 8.3 %slice.24 = f32[36,512,128]{2,1,0:T(8,128)} slice(f32[37,512,128]{2,1,0:T(8,128)} %scatter_fusion.1), slice={[0:36], [0:512], [0:128]} | slice | bytes 18874368 | tf_op jit(solution)/shard_map/slice | solution.py:51
  374.0 0.0 reduce-scatter.2.cloned.1.call-update
  374.0 109.5 %reduce-scatter.2.cloned.1.call-done = f32[36,64,128]{2,1,0:T(8,128)} async-done(((f32[36,512,128]{2,1,0:T(8,128)}), f32[36,64,128]{2,1,0:T(8,128)}) %reduce-scatter.2.cloned.1.call-update) | async-done | bytes 1179664 | tf_op jit(solution)/shard_map/reduce_scatter | solution.py:79
  483.5 0.0 copy-done.1
  (8 shorter events, 0.1 us)
Async XLA Ops:
  6.5 40.8 %copy-start = (bf16[1,8,4,128,128]{4,3,2,1,0:T(8,128)(2,1)S(1)}, bf16[1,8,4,128,128]{4,3,2,1,0:T(8,128)(2,1)}, u32[]{:S(2)}) copy-start(bf16[1,8,4,128,128]{4,3,2,1,0:T(8,128)(2,1)} %param.7) | copy-start | bytes 3145732
  8.9 38.2 %all-to-all-start = ((bf16[64,8,1024]{2,0,1:T(8,128)(2,1)}), bf16[64,8,1024]{2,0,1:T(8,128)(2,1)S(1)}, u32[]{:S(2)}, u32[]{:S(2)}) async-start(bf16[64,8,1024]{2,0,1:T(8,128)(2,1)} %bitcast.26), calls=%async_computation | async-start | bytes 2097152 | tf_op jit(solution)/shard_map/all_to_all | solution.py:57
  115.4 7.5 %copy-start.2 = (s32[32]{0:T(128)S(1)}, s32[32]{0:T(128)}, u32[]{:S(2)}) copy-start(s32[32]{0:T(128)} %param.11) | copy-start | bytes 388
  115.4 209.5 %all-to-all-start.1 = ((f32[32,2,512,128]{3,2,1,0:T(8,128)}), f32[32,2,512,128]{3,2,1,0:T(8,128)}, u32[]{:S(2)}, u32[]{:S(2)}) async-start(f32[32,2,512,128]{3,2,1,0:T(8,128)} %broadcast_select_fusion), calls=%async_computation.1 | async-start | bytes 33554432 | tf_op jit(solution)/shard_map/all_to_all | solution.py:77
  122.9 360.6 %reduce-scatter.2.cloned.1.call-start = ((), (), s32[]{:S(2)}) async-start(), calls=%async_computation.3 | async-start | bytes 10616832 | tf_op jit(solution)/shard_map/reduce_scatter | solution.py:79
  329.8 153.7 %copy-start.1 = (bf16[1,8,4,128,128]{4,3,2,1,0:T(8,128)(2,1)S(1)}, bf16[1,8,4,128,128]{4,3,2,1,0:T(8,128)(2,1)}, u32[]{:S(2)}) copy-start(bf16[1,8,4,128,128]{4,3,2,1,0:T(8,128)(2,1)} %param.7) | copy-start | bytes 3145732
Sparse Core Ops, SparseCore 0:
  374.1 109.3 reduce-scatter.1
where the time goes:
time: 491 us; the launch traced here: 490 us
  waiting for transfers between devices  312 us (64%)
  other arithmetic  92 us (19%)
  local copies, waits for them, and re-layouts  51.5 us (10%)
  starting transfers between devices  16.5 us (3%)
  between operations  13.5 us (3%)
    all_to_all x1, waiting for transfers between devices, body(): lax.all_to_all(packed, 'owner', split_axis=0, concat_axis=0, tiled=True)  199 us
    reduce_scatter x1, waiting for transfers between devices, body(): return lax.psum_scatter(combined, 'tm', scatter_dimension=1, tiled=True)  110 us
    scatter-add x1, other arithmetic, collect(): combined = jax.ops.segment_sum(flat_rows, dest, num_segments=capacity + 1)  35.9 us
    reduce_sum x1, other arithmetic, routing_tables(): jnp.sum(jnp.where(matches, owners[None, None, :, None], 0), axis=(2, 3))  20.8 us
    scatter-add x1, other arithmetic, body(): partial_value = jnp.zeros((list_len, time_len, block_len), jnp.float32).a...  18.8 us
    gather x1, local copies, waits for them, and re-layouts, pack_rows(): packed = jnp.take(padded, outgoing, axis=0)  12.3 us
    select_n x2, other arithmetic, pack_rows(): packed = jnp.take(padded, outgoing, axis=0)  11.6 us
  transfers between devices with their start and end apart: 3, of which 3 were waited for; matrix products, arithmetic and copies ran while one was open for 6% of the time, Pallas kernels for 0%

commit v1 on v0

v1 whole, which is shorter than its diff:
```python
import functools

import jax
import jax.numpy as jnp
from jax import lax
from jax.experimental import pallas as pl
from jax.experimental.pallas import tpu as pltpu
from jax.sharding import PartitionSpec as P


def send_positions(panel_list, owner_list, owner_count, own_index, slot_count):
    owner_size, capacity = owner_list.shape
    row = panel_list[own_index]
    list_len = row.shape[0]
    live = jnp.arange(capacity, dtype=jnp.int32)[None, :] < owner_count[:, None]
    match = (row[:, None, None] == owner_list[None, :, :]) & live[None, :, :]
    owned_by = jnp.any(match, axis=2)
    owner_of = jnp.sum(jnp.where(owned_by, jnp.arange(owner_size, dtype=jnp.int32)[None, :], 0), axis=1)
    position = jnp.arange(list_len, dtype=jnp.int32)
    earlier = (owner_of[:, None] == owner_of[None, :]) & (position[None, :] < position[:, None])
    rank = jnp.sum(earlier.astype(jnp.int32), axis=1)
    return owner_of * slot_count + rank


def receive_slots(panel_list, owner_list, owner_count, own_index, slot_count):
    capacity = owner_list.shape[1]
    list_len = panel_list.shape[1]
    wanted = owner_list[own_index]
    live = jnp.arange(capacity, dtype=jnp.int32) < owner_count[own_index]
    match = (panel_list[:, :, None] == wanted[None, None, :]) & live[None, None, :]
    hit = jnp.any(match, axis=2)
    slot_of = jnp.sum(jnp.where(match, jnp.arange(capacity, dtype=jnp.int32)[None, None, :], 0), axis=2)
    position = jnp.arange(list_len, dtype=jnp.int32)
    earlier = hit[:, None, :] & (position[None, None, :] < position[None, :, None])
    rank = jnp.sum(earlier.astype(jnp.int32), axis=2)
    ranks = jnp.arange(slot_count, dtype=jnp.int32)
    chosen = hit[:, :, None] & (rank[:, :, None] == ranks[None, None, :])
    found = jnp.any(chosen, axis=1)
    dest = jnp.sum(jnp.where(chosen, slot_of[:, :, None], 0), axis=1)
    return jnp.where(found, dest, capacity).reshape(-1)


def project_kernel(group, kp, block_len, idx_ref, p_ref, w_ref, o_ref):
    step = pl.program_id(0)

    @pl.when(step == 0)
    def _():
        o_ref[...] = jnp.zeros_like(o_ref)

    for g in range(group):
        rows = p_ref[:, g * block_len:(g + 1) * block_len]
        for k in range(kp):
            pos = idx_ref[(step * group + g) * kp + k]
            o_ref[pos] += jnp.dot(rows, w_ref[g, k], preferred_element_type=jnp.float32)


def project(idx, pressure, weights, n_pos, group=8):
    fb, kp, block_len, _ = weights.shape
    time_len = pressure.shape[0]
    steps = fb // group
    return pl.pallas_call(
        functools.partial(project_kernel, group, kp, block_len),
        out_shape=jax.ShapeDtypeStruct((n_pos, time_len, block_len), jnp.float32),
        grid_spec=pltpu.PrefetchScalarGridSpec(
            num_scalar_prefetch=1,
            grid=(steps,),
            in_specs=[
                pl.BlockSpec((time_len, group * block_len), lambda c, idx: (0, c)),
                pl.BlockSpec((group, kp, block_len, block_len), lambda c, idx: (c, 0, 0, 0)),
            ],
            out_specs=pl.BlockSpec((n_pos, time_len, block_len), lambda c, idx: (0, 0, 0)),
        ),
        compiler_params=pltpu.CompilerParams(dimension_semantics=("arbitrary",)),
        cost_estimate=pl.CostEstimate(
            flops=2 * fb * kp * time_len * block_len * block_len,
            bytes_accessed=weights.size * 2 + pressure.size * 2 + n_pos * time_len * block_len * 4,
            transcendentals=0,
        ),
    )(idx, pressure, weights)


def collect_kernel(n_rows, dest_ref, r_ref, o_ref, acc_ref):
    acc_ref[...] = jnp.zeros_like(acc_ref)

    def add_row(e, carry):
        d = dest_ref[e]
        acc_ref[d] += r_ref[e]
        return carry

    lax.fori_loop(0, n_rows, add_row, 0)
    o_ref[...] = acc_ref[: o_ref.shape[0]]


def collect(dest, received, capacity):
    n_rows, time_len, block_len = received.shape
    return pl.pallas_call(
        functools.partial(collect_kernel, n_rows),
        out_shape=jax.ShapeDtypeStruct((capacity, time_len, block_len), jnp.float32),
        in_specs=[
            pl.BlockSpec(memory_space=pltpu.SMEM),
            pl.BlockSpec(memory_space=pltpu.VMEM),
        ],
        out_specs=pl.BlockSpec(memory_space=pltpu.VMEM),
        scratch_shapes=[pltpu.VMEM((capacity + 1, time_len, block_len), jnp.float32)],
    )(dest, received)


def body(pressure, proj_weight, pattern, panel_list, owner_list, owner_count):
    owner_size = lax.axis_size("owner")
    own_index = lax.axis_index("owner")
    list_len = panel_list.shape[1]
    capacity = owner_list.shape[1]
    slot_count = max(2, list_len // owner_size)
    n_pos = owner_size * slot_count

    weights = lax.all_gather(proj_weight[0], "tm", axis=0, tiled=True)
    positions = send_positions(panel_list, owner_list, owner_count, own_index, slot_count)
    local_idx = jnp.take(positions, pattern[0], axis=0)
    idx = lax.all_gather(local_idx, "tm", axis=0, tiled=True).reshape(-1)

    packed = project(idx, pressure, weights, n_pos)
    received = lax.all_to_all(packed, "owner", split_axis=0, concat_axis=0, tiled=True)
    dest = receive_slots(panel_list, owner_list, owner_count, own_index, slot_count)
    return collect(dest, received, capacity)


def solution(mesh):
    placed = (
        P("tm", "owner"),
        P("owner", "tm", None, None, None),
        P("owner", "tm", None),
        P(),
        P(),
        P(),
    )
    return jax.shard_map(
        body, mesh=mesh, in_specs=placed, out_specs=P("owner", "tm", None), check_vma=False
    )
```

time: 491 us -> 165 us (0.34)
  waiting for transfers between devices: 312 us -> 96.2 us
  other arithmetic: 92 us -> 6.23 us
  local copies, waits for them, and re-layouts: 51.5 us -> 5.88 us
  blocking collectives: 0 us -> 22 us
  Pallas kernels: 0 us -> 13 us
  starting transfers between devices: 16.5 us -> 7.83 us
    all_to_all x1, waiting for transfers between devices: 199 us -> 23.4 us  [body(): lax.all_to_all(packed, 'owner', split_axis=0, concat_axis=0, tiled=True)]
    reduce_scatter x1 -> x0, waiting for transfers between devices: 110 us -> none  [body(): return lax.psum_scatter(combined, 'tm', scatter_dimension=1, tiled=True)]
    all_gather x0 -> x1, waiting for transfers between devices: none -> 72 us  [body(): weights = lax.all_gather(proj_weight[0], 'tm', axis=0, tiled=True)]
    scatter-add x2 -> x0, other arithmetic: 54.7 us -> none  [the longest x1 35.9 us: collect(): combined = jax.ops.segment_sum(flat_rows, dest, num_segments=capacity + 1)]
    all_gather x0 -> x1, blocking collectives: none -> 22 us  [body(): idx = lax.all_gather(local_idx, 'tm', axis=0, tiled=True).reshape(-1)]
    reduce_sum x4 -> x5, other arithmetic: 23.3 us -> 1.81 us  [the longest x1 0.79 us: receive_slots(): jnp.sum(jnp.where(match, jnp.arange(capacity, dtype=jnp.int32)[None, None...]
    pallas_call x0 -> x2, Pallas kernels: none -> 13 us  [the longest x1 9.69 us: project(): pl.pallas_call(functools.partial(project_kernel, group, kp, block_len), o...]
    select_n x4 -> x2, other arithmetic: 12.3 us -> 0.69 us  [the longest x1 0.69 us: body(): local_idx = jnp.take(positions, pattern[0], axis=0)]
  transfers between devices with their start and end apart: 3 -> 2, of which waited for: 3 -> 2; matrix products, arithmetic and copies ran while one was open for 6% -> 7% of each run, Pallas kernels for 0% -> 0%
where the time goes in v1:
time: 165 us
  waiting for transfers between devices  96.2 us (58%)
  blocking collectives  22 us (13%)
  between operations  13.5 us (8%)
  Pallas kernels  13 us (8%)
  starting transfers between devices  7.83 us (5%)
  other arithmetic  6.23 us (4%)
  local copies, waits for them, and re-layouts  5.88 us (4%)
    all_gather x1, waiting for transfers between devices, body(): weights = lax.all_gather(proj_weight[0], 'tm', axis=0, tiled=True)  72 us
    all_to_all x1, waiting for transfers between devices, body(): lax.all_to_all(packed, 'owner', split_axis=0, concat_axis=0, tiled=True)  23.4 us
    all_gather x1, blocking collectives, body(): idx = lax.all_gather(local_idx, 'tm', axis=0, tiled=True).reshape(-1)  22 us
    pallas_call x1, Pallas kernels, project(): pl.pallas_call(functools.partial(project_kernel, group, kp, block_len), o...  9.69 us
    all_to_all x1, starting transfers between devices, body(): lax.all_to_all(packed, 'owner', split_axis=0, concat_axis=0, tiled=True)  7.83 us
  transfers between devices with their start and end apart: 2, of which 2 were waited for; matrix products, arithmetic and copies ran while one was open for 7% of the time, Pallas kernels for 0%

profile of v1, /device:TPU:1, one launch (start us, length us, event | category | flops | bytes accessed | tf_op | source)
XLA Modules:
  0.0 164.6 jit_solution(5571383856084114637)
XLA Ops:
  6.5 0.0 all-gather.4.cloned.1.call-start
  6.5 0.7 all-gather.4.cloned.1.call-update
  7.3 0.7 compare_select_fusion
  7.9 0.1 copy.17
  8.0 0.1 reshape.92
  8.1 0.7 dynamic-slice_bitcast_fusion
  8.8 0.7 iota_compare_fusion.1
  9.5 1.4 and_reduce_fusion
  11.0 0.1 select_reduce_fusion.2
  11.1 0.2 convert_reduce_fusion.1
  11.3 0.0 copy-start.2
  11.3 0.7 gather_fusion
  12.0 0.1 reshape.91
  12.1 0.1 copy.18
  12.1 0.0 copy-done.2
  12.2 22.0 %all-gather.1 = s32[8,8,4]{1,2,0:T(4,128)S(1)} all-gather(s32[1,8,4]{1,2,0:T(4,128)S(1)} %select_bitcast_fusion), channel_id=1, replica_groups=mesh['tm'=8,'owner'=32] {'tm'}, dimensions={0}, use_global_device_ids=true | all-gather | bytes 1152 | tf_op jit(solution)/shard_map/all_gather | solution.py:119
  34.2 0.1 copy.19
  34.3 0.7 reshape.89.idx_ref
  35.0 72.0 %all-gather.4.cloned.1.call-done = bf16[1,64,4,128,128]{4,3,2,0,1:T(8,128)(2,1)} async-done(((bf16[1,8,4,128,128]{4,3,2,0,1:T(8,128)(2,1)}), bf16[1,64,4,128,128]{4,3,2,0,1:T(8,128)(2,1)}) %all-gather.4.cloned.1.call-update) | async-done | bytes 8388624 | tf_op jit(solution)/shard_map/all_gather | solution.py:116
  107.0 9.7 %shard_map.64 = f32[64,64,128]{2,1,0:T(8,128)} custom-call(s32[256]{0:T(256)} %reshape.89.idx_ref, bf16[64,8192]{1,0:T(8,128)(2,1)} %p_ref.1, bf16[64,4,128,128]{3,2,1,0:T(8,128)(2,1)} %bitcast.17), custom_call_target="tpu_custom_call" | custom-call | flops 536870912 | bytes 11534336 | tf_op jit(solution)/shard_map/pallas_call | solution.py:61
  116.7 0.0 copy-start.3
  116.7 0.0 copy-start.1
  116.7 7.8 %all-to-all-start = ((f32[64,64,128]{2,1,0:T(8,128)}), f32[64,64,128]{2,1,0:T(8,128)S(1)}, u32[]{:S(2)}, u32[]{:S(2)}) async-start(f32[64,64,128]{2,1,0:T(8,128)} %shard_map.64), calls=%async_computation | async-start | bytes 4194304 | tf_op jit(solution)/shard_map/all_to_all | solution.py:122
  124.5 0.0 copy-done.3
  124.5 0.6 dynamic_slice.10
  125.1 0.7 dynamic-slice_bitcast_fusion.1
  125.8 0.6 iota_compare_fusion.3
  126.5 0.0 copy-done.1
  126.5 0.8 fusion
  127.3 0.6 convert_reduce_fusion
  127.9 0.1 fusion.2
  128.0 0.8 select_reduce_fusion
  128.8 0.1 select_reduce_fusion.1
  129.0 0.1 copy.16
  129.1 0.6 select_n.49.dest_ref
  129.7 23.4 %all-to-all-done.r_ref = f32[64,64,128]{2,1,0:T(8,128)S(1)} async-done(((f32[64,64,128]{2,1,0:T(8,128)}), f32[64,64,128]{2,1,0:T(8,128)S(1)}, u32[]{:S(2)}, u32[]{:S(2)}) %all-to-all-start) | async-done | bytes 2097184 | tf_op jit(solution)/shard_map/all_to_all | solution.py:122
  153.1 0.0 copy-start
  153.1 1.3 copy-done
  154.5 3.3 %shard_map.65 = f32[36,64,128]{2,1,0:T(8,128)} custom-call(s32[64]{0:T(128)} %select_n.49.dest_ref, f32[64,64,128]{2,1,0:T(8,128)} %copy-done), custom_call_target="tpu_custom_call" | custom-call | tf_op jit(solution)/shard_map/pallas_call | solution.py:96
  (5 shorter events, 0.0 us)
Async XLA Ops:
  6.5 100.5 %all-gather.4.cloned.1.call-start = ((), (), s32[]{:S(2)}) async-start(), calls=%async_computation.1 | async-start | bytes 9437184 | tf_op jit(solution)/shard_map/all_gather | solution.py:116
  11.3 0.9 copy-start.2
  116.7 7.8 %copy-start.3 = (s32[32]{0:T(128)S(1)}, s32[32]{0:T(128)}, u32[]{:S(2)}) copy-start(s32[32]{0:T(128)} %param.11) | copy-start | bytes 388
  116.7 9.8 %copy-start.1 = (s32[32,32]{1,0:T(8,128)S(1)}, s32[32,32]{1,0:T(8,128)}, u32[]{:S(2)}) copy-start(s32[32,32]{1,0:T(8,128)} %param.9) | copy-start | bytes 12292
  116.7 36.4 %all-to-all-start = ((f32[64,64,128]{2,1,0:T(8,128)}), f32[64,64,128]{2,1,0:T(8,128)S(1)}, u32[]{:S(2)}, u32[]{:S(2)}) async-start(f32[64,64,128]{2,1,0:T(8,128)} %shard_map.64), calls=%async_computation | async-start | bytes 4194304 | tf_op jit(solution)/shard_map/all_to_all | solution.py:122
  153.1 1.4 copy-start
Sparse Core Ops, SparseCore 0:
  9.1 97.8 all-gather.3

commit v2 on v1

--- a/solution.py
+++ b/solution.py
@@ -40,43 +40,52 @@
     return jnp.where(found, dest, capacity).reshape(-1)
 
 
-def project_kernel(group, kp, block_len, idx_ref, p_ref, w_ref, o_ref):
-    step = pl.program_id(0)
-
-    @pl.when(step == 0)
-    def _():
+def project_kernel(group, kp, block_len, first, idx_ref, off_ref, p_ref, w_ref, *refs):
+    if first:
+        (o_ref,) = refs
         o_ref[...] = jnp.zeros_like(o_ref)
-
+    else:
+        acc_ref, o_ref = refs
+        o_ref[...] = acc_ref[...]
     for g in range(group):
         rows = p_ref[:, g * block_len:(g + 1) * block_len]
         for k in range(kp):
-            pos = idx_ref[(step * group + g) * kp + k]
+            pos = idx_ref[g * kp + k]
             o_ref[pos] += jnp.dot(rows, w_ref[g, k], preferred_element_type=jnp.float32)
 
 
-def project(idx, pressure, weights, n_pos, group=8):
-    fb, kp, block_len, _ = weights.shape
+def project(idx, block_at, pressure, weights, acc, n_pos):
+    group, kp, block_len, _ = weights.shape
     time_len = pressure.shape[0]
-    steps = fb // group
+    first = acc is None
+    out_block = pl.BlockSpec((n_pos, time_len, block_len), lambda c, idx, off: (0, 0, 0))
+    in_specs = [
+        pl.BlockSpec((time_len, group * block_len), lambda c, idx, off: (0, off[0])),
+        pl.BlockSpec((group, kp, block_len, block_len), lambda c, idx, off: (0, 0, 0, 0)),
+    ]
+    operands = [idx, jnp.reshape(block_at, (1,)).astype(jnp.int32), pressure, weights]
+    aliases = {}
+    if not first:
+        in_specs.append(out_block)
+        operands.append(acc)
+        aliases = {4: 0}
     return pl.pallas_call(
-        functools.partial(project_kernel, group, kp, block_len),
+        functools.partial(project_kernel, group, kp, block_len, first),
         out_shape=jax.ShapeDtypeStruct((n_pos, time_len, block_len), jnp.float32),
         grid_spec=pltpu.PrefetchScalarGridSpec(
-            num_scalar_prefetch=1,
-            grid=(steps,),
-            in_specs=[
-                pl.BlockSpec((time_len, group * block_len), lambda c, idx: (0, c)),
-                pl.BlockSpec((group, kp, block_len, block_len), lambda c, idx: (c, 0, 0, 0)),
-            ],
-            out_specs=pl.BlockSpec((n_pos, time_len, block_len), lambda c, idx: (0, 0, 0)),
+            num_scalar_prefetch=2,
+            grid=(1,),
+            in_specs=in_specs,
+            out_specs=out_block,
         ),
-        compiler_params=pltpu.CompilerParams(dimension_semantics=("arbitrary",)),
+        input_output_aliases=aliases,
         cost_estimate=pl.CostEstimate(
-            flops=2 * fb * kp * time_len * block_len * block_len,
-            bytes_accessed=weights.size * 2 + pressure.size * 2 + n_pos * time_len * block_len * 4,
+            flops=2 * group * kp * time_len * block_len * block_len,
+            bytes_accessed=weights.size * 2 + time_len * group * block_len * 2
+            + 2 * n_pos * time_len * block_len * 4,
             transcendentals=0,
         ),
-    )(idx, pressure, weights)
+    )(*operands)
 
 
 def collect_kernel(n_rows, dest_ref, r_ref, o_ref, acc_ref):
@@ -113,12 +122,30 @@
     slot_count = max(2, list_len // owner_size)
     n_pos = owner_size * slot_count
 
-    weights = lax.all_gather(proj_weight[0], "tm", axis=0, tiled=True)
+    n_tm = lax.axis_size("tm")
+    t = lax.axis_index("tm")
     positions = send_positions(panel_list, owner_list, owner_count, own_index, slot_count)
-    local_idx = jnp.take(positions, pattern[0], axis=0)
-    idx = lax.all_gather(local_idx, "tm", axis=0, tiled=True).reshape(-1)
+    right = [(i, (i + 1) % n_tm) for i in range(n_tm)]
+    left = [(i, (i - 1) % n_tm) for i in range(n_tm)]
 
-    packed = project(idx, pressure, weights, n_pos)
+    def chunk(weights, pat, block_at, acc):
+        idx = jnp.take(positions, pat, axis=0).reshape(-1)
+        return project(idx, block_at, pressure, weights, acc, n_pos)
+
+    w_r = w_l = proj_weight[0]
+    p_r = p_l = pattern[0]
+    packed = chunk(w_r, p_r, t, None)
+    for s in range(1, n_tm // 2):
+        w_r, p_r = lax.ppermute((w_r, p_r), "tm", right)
+        w_l, p_l = lax.ppermute((w_l, p_l), "tm", left)
+        packed = chunk(w_r, p_r, (t - s) % n_tm, packed)
+        packed = chunk(w_l, p_l, (t + s) % n_tm, packed)
+    half = w_r.shape[0] // 2
+    far = (t + n_tm // 2) % n_tm
+    h_r, q_r = lax.ppermute((w_r[:half], p_r[:half]), "tm", right)
+    h_l, q_l = lax.ppermute((w_l[half:], p_l[half:]), "tm", left)
+    packed = chunk(h_r, q_r, 2 * far, packed)
+    packed = chunk(h_l, q_l, 2 * far + 1, packed)
     received = lax.all_to_all(packed, "owner", split_axis=0, concat_axis=0, tiled=True)
     dest = receive_slots(panel_list, owner_list, owner_count, own_index, slot_count)
     return collect(dest, received, capacity)

time: 165 us -> 172 us (1.042)
  waiting for transfers between devices: 96.2 us -> 64 us
  Pallas kernels: 13 us -> 41.6 us
  starting transfers between devices: 7.83 us -> 36.4 us
  blocking collectives: 22 us -> 0 us
  local copies, waits for them, and re-layouts: 5.88 us -> 23.1 us
  between operations: 13.5 us -> 0.23 us
    all_gather x1 -> x0, waiting for transfers between devices: 72 us -> none  [body(): weights = lax.all_gather(proj_weight[0], 'tm', axis=0, tiled=True)]
    ppermute x0 -> x16, waiting for transfers between devices: none -> 40.6 us  [the longest x6 24.2 us: body(): w_r, p_r = lax.ppermute((w_r, p_r), 'tm', right)]
    pallas_call x1 -> x9, Pallas kernels: 9.69 us -> 38.3 us  [project(): pl.pallas_call(functools.partial(project_kernel, group, kp, block_len, fi...]
    ppermute x0 -> x16, starting transfers between devices: none -> 25.1 us  [the longest x6 17.3 us: body(): w_l, p_l = lax.ppermute((w_l, p_l), 'tm', left)]
    all_gather x1 -> x0, blocking collectives: 22 us -> none  [body(): idx = lax.all_gather(local_idx, 'tm', axis=0, tiled=True).reshape(-1)]
    gather x3 -> x27, local copies, waits for them, and re-layouts: 0.86 us -> 7.71 us  [chunk(): idx = jnp.take(positions, pat, axis=0).reshape(-1)]
    reshape x1 -> x9, local copies, waits for them, and re-layouts: 0.67 us -> 5.61 us  [chunk(): idx = jnp.take(positions, pat, axis=0).reshape(-1)]
    all_to_all x1, starting transfers between devices: 7.83 us -> 11.3 us  [body(): lax.all_to_all(packed, 'owner', split_axis=0, concat_axis=0, tiled=True)]
  transfers between devices with their start and end apart: 2 -> 17, of which waited for: 2 -> 4; matrix products, arithmetic and copies ran while one was open for 7% -> 15% of each run, Pallas kernels for 0% -> 20%
where the time goes in v2:
time: 172 us
  waiting for transfers between devices  64 us (37%)
  Pallas kernels  41.6 us (24%)
  starting transfers between devices  36.4 us (21%)
  local copies, waits for them, and re-layouts  23.1 us (13%)
  other arithmetic  6.38 us (4%)
    pallas_call x9, Pallas kernels, project(): pl.pallas_call(functools.partial(project_kernel, group, kp, block_len, fi...  38.3 us
    ppermute x6, waiting for transfers between devices, body(): w_r, p_r = lax.ppermute((w_r, p_r), 'tm', right)  24.2 us
    all_to_all x1, waiting for transfers between devices, body(): lax.all_to_all(packed, 'owner', split_axis=0, concat_axis=0, tiled=True)  23.4 us
    ppermute x6, starting transfers between devices, body(): w_l, p_l = lax.ppermute((w_l, p_l), 'tm', left)  17.3 us
    ppermute x2, waiting for transfers between devices, body(): h_r, q_r = lax.ppermute((w_r[:half], p_r[:half]), 'tm', right)  16.4 us
    all_to_all x1, starting transfers between devices, body(): lax.all_to_all(packed, 'owner', split_axis=0, concat_axis=0, tiled=True)  11.3 us
    gather x27, local copies, waits for them, and re-layouts, chunk(): idx = jnp.take(positions, pat, axis=0).reshape(-1)  7.71 us
    reshape x9, local copies, waits for them, and re-layouts, chunk(): idx = jnp.take(positions, pat, axis=0).reshape(-1)  5.61 us
  transfers between devices with their start and end apart: 17, of which 4 were waited for; matrix products, arithmetic and copies ran while one was open for 15% of the time, Pallas kernels for 20%

profile of v2, /device:TPU:1, one launch (start us, length us, event | category | flops | bytes accessed | tf_op | source)
XLA Modules:
  0.0 171.7 jit_solution(10189474804105831441)
XLA Ops:
  0.0 2.5 %collective-permute-start.8 = (s32[8,4]{0,1:T(4,128)}, s32[8,4]{0,1:T(4,128)S(1)}, u32[]{:S(2)}, u32[]{:S(2)}) collective-permute-start(s32[8,4]{0,1:T(4,128)} %bitcast.23), channel_id=1, source_target_pairs={{0,32},{32,64},{64,96},{96,128},{128,160},{160,192},{192,224},{224... | collective-permute-start | bytes 392 | tf_op jit(solution)/shard_map/ppermute | solution.py:139
  2.5 3.9 %collective-permute-start = (s32[8,4]{0,1:T(4,128)}, s32[8,4]{0,1:T(4,128)S(1)}, u32[]{:S(2)}, u32[]{:S(2)}) collective-permute-start(s32[8,4]{0,1:T(4,128)} %bitcast.24), channel_id=1, source_target_pairs={{0,224},{32,0},{64,32},{96,64},{128,96},{160,128},{192,160},{224,1... | collective-permute-start | bytes 392 | tf_op jit(solution)/shard_map/ppermute | solution.py:140
  6.4 2.7 %collective-permute-start.4 = (bf16[8,4,128,128]{3,2,1,0:T(8,128)(2,1)}, bf16[8,4,128,128]{3,2,1,0:T(8,128)(2,1)S(1)}, u32[]{:S(2)}, u32[]{:S(2)}) collective-permute-start(bf16[8,4,128,128]{3,2,1,0:T(8,128)(2,1)} %bitcast.21), channel_id=1, source_target_pairs={{0,224},{32,0},{64,32},{96,64},{128,96},{160,128},{192,160},{224,1... | collective-permute-start | bytes 3145736 | tf_op jit(solution)/shard_map/ppermute | solution.py:140
  9.1 0.7 compare_select_fusion
  9.8 0.7 iota_compare_fusion.1
  10.5 0.7 dynamic-slice_bitcast_fusion
  11.2 1.4 and_reduce_fusion
  13.1 0.7 gather_fusion.8
  14.7 3.7 %shard_map.64.refs_0_ = f32[64,64,128]{2,1,0:T(8,128)} custom-call(s32[32]{0:T(128)} %reshape.132.idx_ref, s32[1]{0:T(128)} %bitcast.13.off_ref, bf16[64,8192]{1,0:T(8,128)(2,1)} %p_ref.17, bf16[8,4,128,128]{3,2,1,0:T(8,128)(2,1)} %bitcast.22), custom_call_target="tpu_custom_call" | custom-call | flops 67108864 | bytes 5373952 | tf_op jit(solution)/shard_map/pallas_call | solution.py:72
  18.6 0.7 gather_fusion.7
  20.4 0.7 gather_fusion.6
  21.9 2.7 %collective-permute-start.1 = (s32[8,4]{0,1:T(4,128)S(1)}, s32[8,4]{0,1:T(4,128)S(1)}, u32[]{:S(2)}, u32[]{:S(2)}) collective-permute-start(s32[8,4]{0,1:T(4,128)S(1)} %collective-permute-done), channel_id=1, source_target_pairs={{0,224},{32,0},{64,32},{96,64},{128,96},{160,128},{192,160},{224,1... | collective-permute-start | bytes 392 | tf_op jit(solution)/shard_map/ppermute | solution.py:140
  24.6 7.0 %collective-permute-done.9 = s32[8,4]{0,1:T(4,128)S(1)} collective-permute-done((s32[8,4]{0,1:T(4,128)S(1)}, s32[8,4]{0,1:T(4,128)S(1)}, u32[]{:S(2)}, u32[]{:S(2)}) %collective-permute-start.9) | collective-permute-done | bytes 160 | tf_op jit(solution)/shard_map/ppermute | solution.py:139
  31.8 0.7 gather_fusion.5
  33.4 2.7 %collective-permute-start.5 = (bf16[8,4,128,128]{3,2,1,0:T(8,128)(2,1)S(1)}, bf16[8,4,128,128]{3,2,1,0:T(8,128)(2,1)}, u32[]{:S(2)}, u32[]{:S(2)}) collective-permute-start(bf16[8,4,128,128]{3,2,1,0:T(8,128)(2,1)S(1)} %collective-permute-done.4.w_ref), channel_id=1, source_target_pairs={{0,224},{32,0},{64,32},{96,64},{128,96},{160,128},{192,160},{224,1... | collective-permute-start | bytes 3145736 | tf_op jit(solution)/shard_map/ppermute | solution.py:140
  36.2 0.7 gather_fusion.4
  37.8 2.7 %collective-permute-start.2 = (s32[8,4]{0,1:T(4,128)S(1)}, s32[8,4]{0,1:T(4,128)S(1)}, u32[]{:S(2)}, u32[]{:S(2)}) collective-permute-start(s32[8,4]{0,1:T(4,128)S(1)} %collective-permute-done.1), channel_id=1, source_target_pairs={{0,224},{32,0},{64,32},{96,64},{128,96},{160,128},{192,160},{224,1... | collective-permute-start | bytes 392 | tf_op jit(solution)/shard_map/ppermute | solution.py:140
  40.5 17.1 %collective-permute-done.10 = s32[8,4]{0,1:T(4,128)S(1)} collective-permute-done((s32[8,4]{0,1:T(4,128)S(1)}, s32[8,4]{0,1:T(4,128)S(1)}, u32[]{:S(2)}, u32[]{:S(2)}) %collective-permute-start.10) | collective-permute-done | bytes 160 | tf_op jit(solution)/shard_map/ppermute | solution.py:139
  57.8 0.7 gather_fusion.3
  58.8 0.7 reshape.122.idx_ref
  59.5 2.7 %collective-permute-start.6 = (bf16[8,4,128,128]{3,2,1,0:T(8,128)(2,1)}, bf16[8,4,128,128]{3,2,1,0:T(8,128)(2,1)S(1)}, u32[]{:S(2)}, u32[]{:S(2)}) collective-permute-start(bf16[8,4,128,128]{3,2,1,0:T(8,128)(2,1)} %collective-permute-done.5.w_ref), channel_id=1, source_target_pairs={{0,224},{32,0},{64,32},{96,64},{128,96},{160,128},{192,160},{224,1... | collective-permute-start | bytes 3145736 | tf_op jit(solution)/shard_map/ppermute | solution.py:140
  62.3 0.7 gather_fusion.2
  64.0 2.7 %collective-permute-start.3 = (s32[4,4]{0,1:T(4,128)S(1)}, s32[4,4]{0,1:T(4,128)S(1)}, u32[]{:S(2)}, u32[]{:S(2)}) collective-permute-start(s32[4,4]{0,1:T(4,128)S(1)} %slice.12), channel_id=1, source_target_pairs={{0,224},{32,0},{64,32},{96,64},{128,96},{160,128},{192,160},{224,1... | collective-permute-start | bytes 200 | tf_op jit(solution)/shard_map/ppermute | solution.py:146
  66.6 16.4 %collective-permute-done.11 = s32[4,4]{0,1:T(4,128)S(1)} collective-permute-done((s32[4,4]{0,1:T(4,128)S(1)}, s32[4,4]{0,1:T(4,128)S(1)}, u32[]{:S(2)}, u32[]{:S(2)}) %collective-permute-start.11) | collective-permute-done | bytes 96 | tf_op jit(solution)/shard_map/ppermute | solution.py:145
  83.2 0.7 gather_fusion.1
  84.1 0.7 reshape.118.idx_ref
  84.8 0.9 slice.35
  85.7 0.9 slice.34
  86.6 2.7 %collective-permute-start.7 = (bf16[4,4,128,128]{3,2,1,0:T(8,128)(2,1)}, bf16[4,4,128,128]{3,2,1,0:T(8,128)(2,1)S(1)}, u32[]{:S(2)}, u32[]{:S(2)}) collective-permute-start(bf16[4,4,128,128]{3,2,1,0:T(8,128)(2,1)} %slice.34), channel_id=1, source_target_pairs={{0,224},{32,0},{64,32},{96,64},{128,96},{160,128},{192,160},{224,1... | collective-permute-start | bytes 1572872 | tf_op jit(solution)/shard_map/ppermute | solution.py:146
  89.5 0.7 gather_fusion
  91.1 4.4 %shard_map.65.refs_0_ = f32[64,64,128]{2,1,0:T(8,128)} custom-call(s32[32]{0:T(128)} %reshape.130.idx_ref, s32[1]{0:T(128)} %bitcast.12.off_ref, bf16[64,8192]{1,0:T(8,128)(2,1)} %p_ref.17, bf16[8,4,128,128]{3,2,1,0:T(8,128)(2,1)} %copy-done.4, f32[64,64,128]{2,1,0:T(8,128)} %shard_map.64.refs_0_), custom_call_target="tpu_custom_call", output_to_operand_aliasing={{}: (4, {})} | custom-call | flops 67108864 | bytes 5373952 | tf_op jit(solution)/shard_map/pallas_call | solution.py:72
  95.5 4.4 %shard_map.66.refs_0_ = f32[64,64,128]{2,1,0:T(8,128)} custom-call(s32[32]{0:T(128)} %reshape.128.idx_ref, s32[1]{0:T(128)} %bitcast.11.off_ref, bf16[64,8192]{1,0:T(8,128)(2,1)} %p_ref.17, bf16[8,4,128,128]{3,2,1,0:T(8,128)(2,1)} %copy-done.3, f32[64,64,128]{2,1,0:T(8,128)} %shard_map.65.refs_0_), custom_call_target="tpu_custom_call", output_to_operand_aliasing={{}: (4, {})} | custom-call | flops 67108864 | bytes 5373952 | tf_op jit(solution)/shard_map/pallas_call | solution.py:72
  99.9 4.4 %shard_map.67.refs_0_ = f32[64,64,128]{2,1,0:T(8,128)} custom-call(s32[32]{0:T(128)} %reshape.126.idx_ref, s32[1]{0:T(128)} %bitcast.10.off_ref, bf16[64,8192]{1,0:T(8,128)(2,1)} %p_ref.17, bf16[8,4,128,128]{3,2,1,0:T(8,128)(2,1)} %collective-permute-done.13.w_ref, f32[64,64,128]{2,1,0:T(8,128)} %shard_map.66.refs_0_), custom_call_target="tpu_custom_call", output_to_operand_aliasing={{}: (4, {})} | custom-call | flops 67108864 | bytes 5373952 | tf_op jit(solution)/shard_map/pallas_call | solution.py:72
  104.3 4.4 %shard_map.68.refs_0_ = f32[64,64,128]{2,1,0:T(8,128)} custom-call(s32[32]{0:T(128)} %reshape.124.idx_ref, s32[1]{0:T(128)} %bitcast.9.off_ref, bf16[64,8192]{1,0:T(8,128)(2,1)} %p_ref.17, bf16[8,4,128,128]{3,2,1,0:T(8,128)(2,1)} %collective-permute-done.5.w_ref, f32[64,64,128]{2,1,0:T(8,128)} %shard_map.67.refs_0_), custom_call_target="tpu_custom_call", output_to_operand_aliasing={{}: (4, {})} | custom-call | flops 67108864 | bytes 5373952 | tf_op jit(solution)/shard_map/pallas_call | solution.py:72
  108.7 4.4 %shard_map.69.refs_0_ = f32[64,64,128]{2,1,0:T(8,128)} custom-call(s32[32]{0:T(128)} %reshape.122.idx_ref, s32[1]{0:T(128)} %bitcast.8.off_ref, bf16[64,8192]{1,0:T(8,128)(2,1)} %p_ref.17, bf16[8,4,128,128]{3,2,1,0:T(8,128)(2,1)} %copy-done.1, f32[64,64,128]{2,1,0:T(8,128)} %shard_map.68.refs_0_), custom_call_target="tpu_custom_call", output_to_operand_aliasing={{}: (4, {})} | custom-call | flops 67108864 | bytes 5373952 | tf_op jit(solution)/shard_map/pallas_call | solution.py:72
  113.1 4.4 %shard_map.70.refs_0_ = f32[64,64,128]{2,1,0:T(8,128)} custom-call(s32[32]{0:T(128)} %reshape.120.idx_ref, s32[1]{0:T(128)} %bitcast.7.off_ref, bf16[64,8192]{1,0:T(8,128)(2,1)} %p_ref.17, bf16[8,4,128,128]{3,2,1,0:T(8,128)(2,1)} %copy-done.2, f32[64,64,128]{2,1,0:T(8,128)} %shard_map.69.refs_0_), custom_call_target="tpu_custom_call", output_to_operand_aliasing={{}: (4, {})} | custom-call | flops 67108864 | bytes 5373952 | tf_op jit(solution)/shard_map/pallas_call | solution.py:72
  117.5 0.8 copy-done.5
  118.3 4.1 %shard_map.71.refs_0_ = f32[64,64,128]{2,1,0:T(8,128)} custom-call(s32[16]{0:T(128)} %reshape.118.idx_ref, s32[1]{0:T(128)} %bitcast.6.off_ref, bf16[64,8192]{1,0:T(8,128)(2,1)} %p_ref.17, bf16[4,4,128,128]{3,2,1,0:T(8,128)(2,1)} %copy-done.5, f32[64,64,128]{2,1,0:T(8,128)} %shard_map.70.refs_0_), custom_call_target="tpu_custom_call", output_to_operand_aliasing={{}: (4, {})} | custom-call | flops 33554432 | bytes 4784128 | tf_op jit(solution)/shard_map/pallas_call | solution.py:72
  122.4 0.8 copy-done.6
  123.2 4.1 %shard_map.72 = f32[64,64,128]{2,1,0:T(8,128)} custom-call(s32[16]{0:T(128)} %reshape.116.idx_ref, s32[1]{0:T(128)} %bitcast.4.off_ref, bf16[64,8192]{1,0:T(8,128)(2,1)} %p_ref.17, bf16[4,4,128,128]{3,2,1,0:T(8,128)(2,1)} %copy-done.6, f32[64,64,128]{2,1,0:T(8,128)} %shard_map.71.refs_0_), custom_call_target="tpu_custom_call", output_to_operand_aliasing={{}: (4, {})} | custom-call | flops 33554432 | bytes 4784128 | tf_op jit(solution)/shard_map/pallas_call | solution.py:72
  127.3 11.3 %all-to-all-start = ((f32[64,64,128]{2,1,0:T(8,128)}), f32[64,64,128]{2,1,0:T(8,128)S(1)}, u32[]{:S(2)}, u32[]{:S(2)}) async-start(f32[64,64,128]{2,1,0:T(8,128)} %shard_map.72), calls=%async_computation | async-start | bytes 4194304 | tf_op jit(solution)/shard_map/all_to_all | solution.py:149
  139.2 0.7 dynamic-slice_bitcast_fusion.1
  139.8 0.6 iota_compare_fusion.3
  140.5 0.8 fusion
  142.1 0.8 select_reduce_fusion
  143.7 23.4 %all-to-all-done.r_ref = f32[64,64,128]{2,1,0:T(8,128)S(1)} async-done(((f32[64,64,128]{2,1,0:T(8,128)}), f32[64,64,128]{2,1,0:T(8,128)S(1)}, u32[]{:S(2)}, u32[]{:S(2)}) %all-to-all-start) | async-done | bytes 2097184 | tf_op jit(solution)/shard_map/all_to_all | solution.py:149
  167.1 1.3 copy-done
  168.5 3.3 %shard_map.73 = f32[36,64,128]{2,1,0:T(8,128)} custom-call(s32[64]{0:T(128)} %select_n.74.dest_ref, f32[64,64,128]{2,1,0:T(8,128)} %copy-done), custom_call_target="tpu_custom_call" | custom-call | tf_op jit(solution)/shard_map/pallas_call | solution.py:105
  (127 shorter events, 10.9 us)
Async XLA Ops:
  0.0 18.4 %collective-permute-start.8 = (s32[8,4]{0,1:T(4,128)}, s32[8,4]{0,1:T(4,128)S(1)}, u32[]{:S(2)}, u32[]{:S(2)}) collective-permute-start(s32[8,4]{0,1:T(4,128)} %bitcast.23), channel_id=1, source_target_pairs={{0,32},{32,64},{64,96},{96,128},{128,160},{160,192},{192,224},{224... | collective-permute-start | bytes 392 | tf_op jit(solution)/shard_map/ppermute | solution.py:139
  2.5 17.7 %collective-permute-start = (s32[8,4]{0,1:T(4,128)}, s32[8,4]{0,1:T(4,128)S(1)}, u32[]{:S(2)}, u32[]{:S(2)}) collective-permute-start(s32[8,4]{0,1:T(4,128)} %bitcast.24), channel_id=1, source_target_pairs={{0,224},{32,0},{64,32},{96,64},{128,96},{160,128},{192,160},{224,1... | collective-permute-start | bytes 392 | tf_op jit(solution)/shard_map/ppermute | solution.py:140
  6.4 27.0 %collective-permute-start.12 = (bf16[8,4,128,128]{3,2,1,0:T(8,128)(2,1)}, bf16[8,4,128,128]{3,2,1,0:T(8,128)(2,1)S(1)}, u32[]{:S(2)}, u32[]{:S(2)}) collective-permute-start(bf16[8,4,128,128]{3,2,1,0:T(8,128)(2,1)} %bitcast.20), channel_id=1, source_target_pairs={{0,32},{32,64},{64,96},{96,128},{128,160},{160,192},{192,224},{224... | collective-permute-start | bytes 3145736 | tf_op jit(solution)/shard_map/ppermute | solution.py:139
  6.4 27.0 %collective-permute-start.4 = (bf16[8,4,128,128]{3,2,1,0:T(8,128)(2,1)}, bf16[8,4,128,128]{3,2,1,0:T(8,128)(2,1)S(1)}, u32[]{:S(2)}, u32[]{:S(2)}) collective-permute-start(bf16[8,4,128,128]{3,2,1,0:T(8,128)(2,1)} %bitcast.21), channel_id=1, source_target_pairs={{0,224},{32,0},{64,32},{96,64},{128,96},{160,128},{192,160},{224,1... | collective-permute-start | bytes 3145736 | tf_op jit(solution)/shard_map/ppermute | solution.py:140
  13.1 0.9 copy-start.8
  21.3 10.3 %collective-permute-start.9 = (s32[8,4]{0,1:T(4,128)S(1)}, s32[8,4]{0,1:T(4,128)S(1)}, u32[]{:S(2)}, u32[]{:S(2)}) collective-permute-start(s32[8,4]{0,1:T(4,128)S(1)} %collective-permute-done.8), channel_id=1, source_target_pairs={{0,32},{32,64},{64,96},{96,128},{128,160},{160,192},{192,224},{224... | collective-permute-start | bytes 392 | tf_op jit(solution)/shard_map/ppermute | solution.py:139
  21.9 14.1 %collective-permute-start.1 = (s32[8,4]{0,1:T(4,128)S(1)}, s32[8,4]{0,1:T(4,128)S(1)}, u32[]{:S(2)}, u32[]{:S(2)}) collective-permute-start(s32[8,4]{0,1:T(4,128)S(1)} %collective-permute-done), channel_id=1, source_target_pairs={{0,224},{32,0},{64,32},{96,64},{128,96},{160,128},{192,160},{224,1... | collective-permute-start | bytes 392 | tf_op jit(solution)/shard_map/ppermute | solution.py:140
  33.4 3.6 %copy-start.4 = (bf16[8,4,128,128]{3,2,1,0:T(8,128)(2,1)}, bf16[8,4,128,128]{3,2,1,0:T(8,128)(2,1)S(1)}, u32[]{:S(2)}) copy-start(bf16[8,4,128,128]{3,2,1,0:T(8,128)(2,1)S(1)} %collective-permute-done.12.w_ref) | copy-start | bytes 3145732
  33.4 26.1 %collective-permute-start.13 = (bf16[8,4,128,128]{3,2,1,0:T(8,128)(2,1)S(1)}, bf16[8,4,128,128]{3,2,1,0:T(8,128)(2,1)}, u32[]{:S(2)}, u32[]{:S(2)}) collective-permute-start(bf16[8,4,128,128]{3,2,1,0:T(8,128)(2,1)S(1)} %collective-permute-done.12.w_ref), channel_id=1, source_target_pairs={{0,32},{32,64},{64,96},{96,128},{128,160},{160,192},{192,224},{224... | collective-permute-start | bytes 3145736 | tf_op jit(solution)/shard_map/ppermute | solution.py:139
  33.4 3.6 %copy-start.3 = (bf16[8,4,128,128]{3,2,1,0:T(8,128)(2,1)}, bf16[8,4,128,128]{3,2,1,0:T(8,128)(2,1)S(1)}, u32[]{:S(2)}) copy-start(bf16[8,4,128,128]{3,2,1,0:T(8,128)(2,1)S(1)} %collective-permute-done.4.w_ref) | copy-start | bytes 3145732
  33.4 26.1 %collective-permute-start.5 = (bf16[8,4,128,128]{3,2,1,0:T(8,128)(2,1)S(1)}, bf16[8,4,128,128]{3,2,1,0:T(8,128)(2,1)}, u32[]{:S(2)}, u32[]{:S(2)}) collective-permute-start(bf16[8,4,128,128]{3,2,1,0:T(8,128)(2,1)S(1)} %collective-permute-done.4.w_ref), channel_id=1, source_target_pairs={{0,224},{32,0},{64,32},{96,64},{128,96},{160,128},{192,160},{224,1... | collective-permute-start | bytes 3145736 | tf_op jit(solution)/shard_map/ppermute | solution.py:140
  37.2 20.4 %collective-permute-start.10 = (s32[8,4]{0,1:T(4,128)S(1)}, s32[8,4]{0,1:T(4,128)S(1)}, u32[]{:S(2)}, u32[]{:S(2)}) collective-permute-start(s32[8,4]{0,1:T(4,128)S(1)} %collective-permute-done.9), channel_id=1, source_target_pairs={{0,32},{32,64},{64,96},{96,128},{128,160},{160,192},{192,224},{224... | collective-permute-start | bytes 392 | tf_op jit(solution)/shard_map/ppermute | solution.py:139
  37.8 24.3 %collective-permute-start.2 = (s32[8,4]{0,1:T(4,128)S(1)}, s32[8,4]{0,1:T(4,128)S(1)}, u32[]{:S(2)}, u32[]{:S(2)}) collective-permute-start(s32[8,4]{0,1:T(4,128)S(1)} %collective-permute-done.1), channel_id=1, source_target_pairs={{0,224},{32,0},{64,32},{96,64},{128,96},{160,128},{192,160},{224,1... | collective-permute-start | bytes 392 | tf_op jit(solution)/shard_map/ppermute | solution.py:140
  59.4 25.4 %collective-permute-start.14 = (bf16[8,4,128,128]{3,2,1,0:T(8,128)(2,1)}, bf16[8,4,128,128]{3,2,1,0:T(8,128)(2,1)S(1)}, u32[]{:S(2)}, u32[]{:S(2)}) collective-permute-start(bf16[8,4,128,128]{3,2,1,0:T(8,128)(2,1)} %collective-permute-done.13.w_ref), channel_id=1, source_target_pairs={{0,32},{32,64},{64,96},{96,128},{128,160},{160,192},{192,224},{224... | collective-permute-start | bytes 3145736 | tf_op jit(solution)/shard_map/ppermute | solution.py:139
  59.5 26.3 %collective-permute-start.6 = (bf16[8,4,128,128]{3,2,1,0:T(8,128)(2,1)}, bf16[8,4,128,128]{3,2,1,0:T(8,128)(2,1)S(1)}, u32[]{:S(2)}, u32[]{:S(2)}) collective-permute-start(bf16[8,4,128,128]{3,2,1,0:T(8,128)(2,1)} %collective-permute-done.5.w_ref), channel_id=1, source_target_pairs={{0,224},{32,0},{64,32},{96,64},{128,96},{160,128},{192,160},{224,1... | collective-permute-start | bytes 3145736 | tf_op jit(solution)/shard_map/ppermute | solution.py:140
  63.9 19.1 %collective-permute-start.11 = (s32[4,4]{0,1:T(4,128)S(1)}, s32[4,4]{0,1:T(4,128)S(1)}, u32[]{:S(2)}, u32[]{:S(2)}) collective-permute-start(s32[4,4]{0,1:T(4,128)S(1)} %bitcast.25), channel_id=1, source_target_pairs={{0,32},{32,64},{64,96},{96,128},{128,160},{160,192},{192,224},{224... | collective-permute-start | bytes 200 | tf_op jit(solution)/shard_map/ppermute | solution.py:145
  64.0 25.3 %collective-permute-start.3 = (s32[4,4]{0,1:T(4,128)S(1)}, s32[4,4]{0,1:T(4,128)S(1)}, u32[]{:S(2)}, u32[]{:S(2)}) collective-permute-start(s32[4,4]{0,1:T(4,128)S(1)} %slice.12), channel_id=1, source_target_pairs={{0,224},{32,0},{64,32},{96,64},{128,96},{160,128},{192,160},{224,1... | collective-permute-start | bytes 200 | tf_op jit(solution)/shard_map/ppermute | solution.py:146
  84.8 5.3 %copy-start.1 = (bf16[8,4,128,128]{3,2,1,0:T(8,128)(2,1)}, bf16[8,4,128,128]{3,2,1,0:T(8,128)(2,1)S(1)}, u32[]{:S(2)}) copy-start(bf16[8,4,128,128]{3,2,1,0:T(8,128)(2,1)S(1)} %collective-permute-done.14.w_ref) | copy-start | bytes 3145732
  85.7 31.8 %collective-permute-start.15 = (bf16[4,4,128,128]{3,2,1,0:T(8,128)(2,1)}, bf16[4,4,128,128]{3,2,1,0:T(8,128)(2,1)S(1)}, u32[]{:S(2)}, u32[]{:S(2)}) collective-permute-start(bf16[4,4,128,128]{3,2,1,0:T(8,128)(2,1)} %slice.35), channel_id=1, source_target_pairs={{0,32},{32,64},{64,96},{96,128},{128,160},{160,192},{192,224},{224... | collective-permute-start | bytes 1572872 | tf_op jit(solution)/shard_map/ppermute | solution.py:145
  85.7 9.7 %copy-start.2 = (bf16[8,4,128,128]{3,2,1,0:T(8,128)(2,1)}, bf16[8,4,128,128]{3,2,1,0:T(8,128)(2,1)S(1)}, u32[]{:S(2)}) copy-start(bf16[8,4,128,128]{3,2,1,0:T(8,128)(2,1)S(1)} %collective-permute-done.6.w_ref) | copy-start | bytes 3145732
  86.6 35.8 %collective-permute-start.7 = (bf16[4,4,128,128]{3,2,1,0:T(8,128)(2,1)}, bf16[4,4,128,128]{3,2,1,0:T(8,128)(2,1)S(1)}, u32[]{:S(2)}, u32[]{:S(2)}) collective-permute-start(bf16[4,4,128,128]{3,2,1,0:T(8,128)(2,1)} %slice.34), channel_id=1, source_target_pairs={{0,224},{32,0},{64,32},{96,64},{128,96},{160,128},{192,160},{224,1... | collective-permute-start | bytes 1572872 | tf_op jit(solution)/shard_map/ppermute | solution.py:146
  117.5 0.8 copy-start.5
  122.4 0.8 copy-start.6
  127.3 11.3 %copy-start.9 = (s32[32]{0:T(128)S(1)}, s32[32]{0:T(128)}, u32[]{:S(2)}) copy-start(s32[32]{0:T(128)} %param.15) | copy-start | bytes 388
  127.3 13.2 %copy-start.7 = (s32[32,32]{1,0:T(8,128)S(1)}, s32[32,32]{1,0:T(8,128)}, u32[]{:S(2)}) copy-start(s32[32,32]{1,0:T(8,128)} %param.13) | copy-start | bytes 12292
  127.3 39.9 %all-to-all-start = ((f32[64,64,128]{2,1,0:T(8,128)}), f32[64,64,128]{2,1,0:T(8,128)S(1)}, u32[]{:S(2)}, u32[]{:S(2)}) async-start(f32[64,64,128]{2,1,0:T(8,128)} %shard_map.72), calls=%async_computation | async-start | bytes 4194304 | tf_op jit(solution)/shard_map/all_to_all | solution.py:149
  167.1 1.3 copy-start

commit v3 on v1

--- a/solution.py
+++ b/solution.py
@@ -49,12 +49,14 @@
 
     for g in range(group):
         rows = p_ref[:, g * block_len:(g + 1) * block_len]
+        wide = jnp.concatenate([w_ref[g, k] for k in range(kp)], axis=1)
+        prod = jnp.dot(rows, wide, preferred_element_type=jnp.float32)
         for k in range(kp):
             pos = idx_ref[(step * group + g) * kp + k]
-            o_ref[pos] += jnp.dot(rows, w_ref[g, k], preferred_element_type=jnp.float32)
+            o_ref[pos] += prod[:, k * block_len:(k + 1) * block_len]
 
 
-def project(idx, pressure, weights, n_pos, group=8):
+def project(idx, pressure, weights, n_pos, group=32):
     fb, kp, block_len, _ = weights.shape
     time_len = pressure.shape[0]
     steps = fb // group

time: 165 us -> 162 us (0.982)
  Pallas kernels: 13 us -> 10.2 us
    pallas_call x1, Pallas kernels: 9.69 us -> 6.9 us  [project(): pl.pallas_call(functools.partial(project_kernel, group, kp, block_len), o...]
where the time goes in v3:
time: 162 us
  waiting for transfers between devices  96.2 us (59%)
  blocking collectives  22 us (14%)
  between operations  13.5 us (8%)
  Pallas kernels  10.2 us (6%)
  starting transfers between devices  7.83 us (5%)
  other arithmetic  6.23 us (4%)
  local copies, waits for them, and re-layouts  5.88 us (4%)
    all_gather x1, waiting for transfers between devices, body(): weights = lax.all_gather(proj_weight[0], 'tm', axis=0, tiled=True)  72 us
    all_to_all x1, waiting for transfers between devices, body(): lax.all_to_all(packed, 'owner', split_axis=0, concat_axis=0, tiled=True)  23.4 us
    all_gather x1, blocking collectives, body(): idx = lax.all_gather(local_idx, 'tm', axis=0, tiled=True).reshape(-1)  22 us
    all_to_all x1, starting transfers between devices, body(): lax.all_to_all(packed, 'owner', split_axis=0, concat_axis=0, tiled=True)  7.83 us
    pallas_call x1, Pallas kernels, project(): pl.pallas_call(functools.partial(project_kernel, group, kp, block_len), o...  6.9 us
    pallas_call x1, Pallas kernels, collect(): pl.pallas_call(functools.partial(collect_kernel, n_rows), out_shape=jax.S...  3.27 us
  transfers between devices with their start and end apart: 2, of which 2 were waited for; matrix products, arithmetic and copies ran while one was open for 7% of the time, Pallas kernels for 0%

profile of v3, /device:TPU:1, one launch (start us, length us, event | category | flops | bytes accessed | tf_op | source)
XLA Modules:
  0.0 161.8 jit_solution(13092193752164256281)
XLA Ops:
  6.5 0.0 all-gather.4.cloned.1.call-start
  6.5 0.7 all-gather.4.cloned.1.call-update
  7.3 0.7 compare_select_fusion
  7.9 0.1 copy.17
  8.0 0.1 reshape.92
  8.1 0.7 dynamic-slice_bitcast_fusion
  8.8 0.7 iota_compare_fusion.1
  9.5 1.4 and_reduce_fusion
  11.0 0.1 select_reduce_fusion.2
  11.1 0.2 convert_reduce_fusion.1
  11.3 0.0 copy-start.2
  11.3 0.7 gather_fusion
  12.0 0.1 reshape.91
  12.1 0.1 copy.18
  12.1 0.0 copy-done.2
  12.2 22.0 %all-gather.1 = s32[8,8,4]{1,2,0:T(4,128)S(1)} all-gather(s32[1,8,4]{1,2,0:T(4,128)S(1)} %select_bitcast_fusion), channel_id=1, replica_groups=mesh['tm'=8,'owner'=32] {'tm'}, dimensions={0}, use_global_device_ids=true | all-gather | bytes 1152 | tf_op jit(solution)/shard_map/all_gather | solution.py:121
  34.2 0.1 copy.19
  34.3 0.7 reshape.89.idx_ref
  35.0 72.0 %all-gather.4.cloned.1.call-done = bf16[1,64,4,128,128]{4,3,2,0,1:T(8,128)(2,1)} async-done(((bf16[1,8,4,128,128]{4,3,2,0,1:T(8,128)(2,1)}), bf16[1,64,4,128,128]{4,3,2,0,1:T(8,128)(2,1)}) %all-gather.4.cloned.1.call-update) | async-done | bytes 8388624 | tf_op jit(solution)/shard_map/all_gather | solution.py:118
  107.0 6.9 %shard_map.64 = f32[64,64,128]{2,1,0:T(8,128)} custom-call(s32[256]{0:T(256)} %reshape.89.idx_ref, bf16[64,8192]{1,0:T(8,128)(2,1)} %p_ref.1, bf16[64,4,128,128]{3,2,1,0:T(8,128)(2,1)} %bitcast.17), custom_call_target="tpu_custom_call" | custom-call | flops 536870912 | bytes 11534336 | tf_op jit(solution)/shard_map/pallas_call | solution.py:63
  113.9 0.0 copy-start.3
  113.9 0.0 copy-start.1
  113.9 7.8 %all-to-all-start = ((f32[64,64,128]{2,1,0:T(8,128)}), f32[64,64,128]{2,1,0:T(8,128)S(1)}, u32[]{:S(2)}, u32[]{:S(2)}) async-start(f32[64,64,128]{2,1,0:T(8,128)} %shard_map.64), calls=%async_computation | async-start | bytes 4194304 | tf_op jit(solution)/shard_map/all_to_all | solution.py:124
  121.8 0.0 copy-done.3
  121.8 0.6 dynamic_slice.10
  122.4 0.7 dynamic-slice_bitcast_fusion.1
  123.0 0.6 iota_compare_fusion.3
  123.7 0.0 copy-done.1
  123.7 0.8 fusion
  124.5 0.6 convert_reduce_fusion
  125.1 0.1 fusion.2
  125.3 0.8 select_reduce_fusion
  126.1 0.1 select_reduce_fusion.1
  126.2 0.1 copy.16
  126.3 0.6 select_n.49.dest_ref
  126.9 23.4 %all-to-all-done.r_ref = f32[64,64,128]{2,1,0:T(8,128)S(1)} async-done(((f32[64,64,128]{2,1,0:T(8,128)}), f32[64,64,128]{2,1,0:T(8,128)S(1)}, u32[]{:S(2)}, u32[]{:S(2)}) %all-to-all-start) | async-done | bytes 2097184 | tf_op jit(solution)/shard_map/all_to_all | solution.py:124
  150.3 0.0 copy-start
  150.3 1.3 copy-done
  151.7 3.3 %shard_map.65 = f32[36,64,128]{2,1,0:T(8,128)} custom-call(s32[64]{0:T(128)} %select_n.49.dest_ref, f32[64,64,128]{2,1,0:T(8,128)} %copy-done), custom_call_target="tpu_custom_call" | custom-call | tf_op jit(solution)/shard_map/pallas_call | solution.py:98
  (5 shorter events, 0.0 us)
Async XLA Ops:
  6.5 100.5 %all-gather.4.cloned.1.call-start = ((), (), s32[]{:S(2)}) async-start(), calls=%async_computation.1 | async-start | bytes 9437184 | tf_op jit(solution)/shard_map/all_gather | solution.py:118
  11.3 0.9 copy-start.2
  113.9 7.8 %copy-start.3 = (s32[32]{0:T(128)S(1)}, s32[32]{0:T(128)}, u32[]{:S(2)}) copy-start(s32[32]{0:T(128)} %param.11) | copy-start | bytes 388
  113.9 9.8 %copy-start.1 = (s32[32,32]{1,0:T(8,128)S(1)}, s32[32,32]{1,0:T(8,128)}, u32[]{:S(2)}) copy-start(s32[32,32]{1,0:T(8,128)} %param.9) | copy-start | bytes 12292
  113.9 36.4 %all-to-all-start = ((f32[64,64,128]{2,1,0:T(8,128)}), f32[64,64,128]{2,1,0:T(8,128)S(1)}, u32[]{:S(2)}, u32[]{:S(2)}) async-start(f32[64,64,128]{2,1,0:T(8,128)} %shard_map.64), calls=%async_computation | async-start | bytes 4194304 | tf_op jit(solution)/shard_map/all_to_all | solution.py:124
  150.3 1.4 copy-start
Sparse Core Ops, SparseCore 0:
  9.1 97.8 all-gather.3

commit v4 on v1

--- a/solution.py
+++ b/solution.py
@@ -40,43 +40,62 @@
     return jnp.where(found, dest, capacity).reshape(-1)
 
 
-def project_kernel(group, kp, block_len, idx_ref, p_ref, w_ref, o_ref):
-    step = pl.program_id(0)
+def project_kernel(sizes, kp, block_len, idx_ref, blk_ref, p_ref, *refs):
+    n = len(sizes)
+    w_refs = refs[:n]
+    o_ref, buf, sem = refs[n:]
+    o_ref[...] = jnp.zeros_like(o_ref)
 
-    @pl.when(step == 0)
-    def _():
-        o_ref[...] = jnp.zeros_like(o_ref)
+    def fetch(q):
+        slot = q % 2
+        return pltpu.make_async_copy(w_refs[q], buf.at[slot, pl.ds(0, sizes[q])], sem.at[slot])
 
-    for g in range(group):
-        rows = p_ref[:, g * block_len:(g + 1) * block_len]
-        for k in range(kp):
-            pos = idx_ref[(step * group + g) * kp + k]
-            o_ref[pos] += jnp.dot(rows, w_ref[g, k], preferred_element_type=jnp.float32)
+    copies = [fetch(0)]
+    copies[0].start()
+    base = 0
+    for q in range(n):
+        copies[q].wait()
+        if q + 1 < n:
+            copies.append(fetch(q + 1))
+            copies[q + 1].start()
+        slot = q % 2
+        for g in range(sizes[q]):
+            col = pl.multiple_of((blk_ref[q] + g) * block_len, block_len)
+            rows = p_ref[:, pl.ds(col, block_len)]
+            wide = jnp.concatenate([buf[slot, g, k] for k in range(kp)], axis=1)
+            prod = jnp.dot(rows, wide, preferred_element_type=jnp.float32)
+            for k in range(kp):
+                pos = idx_ref[(base + g) * kp + k]
+                o_ref[pos] += prod[:, k * block_len:(k + 1) * block_len]
+        base += sizes[q]
 
 
-def project(idx, pressure, weights, n_pos, group=8):
-    fb, kp, block_len, _ = weights.shape
+def project(idx, blk, pressure, pieces, n_pos):
+    sizes = tuple(w.shape[0] for w in pieces)
+    _, kp, block_len, _ = pieces[0].shape
     time_len = pressure.shape[0]
-    steps = fb // group
+    face_blocks = sum(sizes)
     return pl.pallas_call(
-        functools.partial(project_kernel, group, kp, block_len),
+        functools.partial(project_kernel, sizes, kp, block_len),
         out_shape=jax.ShapeDtypeStruct((n_pos, time_len, block_len), jnp.float32),
-        grid_spec=pltpu.PrefetchScalarGridSpec(
-            num_scalar_prefetch=1,
-            grid=(steps,),
-            in_specs=[
-                pl.BlockSpec((time_len, group * block_len), lambda c, idx: (0, c)),
-                pl.BlockSpec((group, kp, block_len, block_len), lambda c, idx: (c, 0, 0, 0)),
-            ],
-            out_specs=pl.BlockSpec((n_pos, time_len, block_len), lambda c, idx: (0, 0, 0)),
-        ),
-        compiler_params=pltpu.CompilerParams(dimension_semantics=("arbitrary",)),
+        in_specs=[
+            pl.BlockSpec(memory_space=pltpu.SMEM),
+            pl.BlockSpec(memory_space=pltpu.SMEM),
+            pl.BlockSpec(memory_space=pltpu.VMEM),
+        ]
+        + [pl.BlockSpec(memory_space=pl.ANY)] * len(pieces),
+        out_specs=pl.BlockSpec(memory_space=pltpu.VMEM),
+        scratch_shapes=[
+            pltpu.VMEM((2, max(sizes), kp, block_len, block_len), pieces[0].dtype),
+            pltpu.SemaphoreType.DMA((2,)),
+        ],
         cost_estimate=pl.CostEstimate(
-            flops=2 * fb * kp * time_len * block_len * block_len,
-            bytes_accessed=weights.size * 2 + pressure.size * 2 + n_pos * time_len * block_len * 4,
+            flops=2 * face_blocks * kp * time_len * block_len * block_len,
+            bytes_accessed=face_blocks * kp * block_len * block_len * 2 + pressure.size * 2
+            + n_pos * time_len * block_len * 4,
             transcendentals=0,
         ),
-    )(idx, pressure, weights)
+    )(idx, blk, pressure, *pieces)
 
 
 def collect_kernel(n_rows, dest_ref, r_ref, o_ref, acc_ref):
@@ -113,12 +132,33 @@
     slot_count = max(2, list_len // owner_size)
     n_pos = owner_size * slot_count
 
-    weights = lax.all_gather(proj_weight[0], "tm", axis=0, tiled=True)
+    n_tm = lax.axis_size("tm")
+    t = lax.axis_index("tm")
+    fb_dev = pattern.shape[1]
+    right = [(i, (i + 1) % n_tm) for i in range(n_tm)]
+    left = [(i, (i - 1) % n_tm) for i in range(n_tm)]
+
+    w_r = w_l = proj_weight[0]
+    p_r = p_l = pattern[0]
+    pieces, pats, starts = [w_r], [p_r], [t * fb_dev]
+    for s in range(1, n_tm // 2):
+        w_r, p_r = lax.ppermute((w_r, p_r), "tm", right)
+        w_l, p_l = lax.ppermute((w_l, p_l), "tm", left)
+        pieces += [w_r, w_l]
+        pats += [p_r, p_l]
+        starts += [((t - s) % n_tm) * fb_dev, ((t + s) % n_tm) * fb_dev]
+    half = fb_dev // 2
+    far = (t + n_tm // 2) % n_tm
+    h_r, q_r = lax.ppermute((w_r[:half], p_r[:half]), "tm", right)
+    h_l, q_l = lax.ppermute((w_l[half:], p_l[half:]), "tm", left)
+    pieces += [h_r, h_l]
+    pats += [q_r, q_l]
+    starts += [far * fb_dev, far * fb_dev + half]
+
     positions = send_positions(panel_list, owner_list, owner_count, own_index, slot_count)
-    local_idx = jnp.take(positions, pattern[0], axis=0)
-    idx = lax.all_gather(local_idx, "tm", axis=0, tiled=True).reshape(-1)
-
-    packed = project(idx, pressure, weights, n_pos)
+    idx = jnp.take(positions, jnp.concatenate(pats, axis=0), axis=0).reshape(-1)
+    blk = jnp.stack(starts).astype(jnp.int32)
+    packed = project(idx, blk, pressure, pieces, n_pos)
     received = lax.all_to_all(packed, "owner", split_axis=0, concat_axis=0, tiled=True)
     dest = receive_slots(panel_list, owner_list, owner_count, own_index, slot_count)
     return collect(dest, received, capacity)

time: 165 us -> 167 us (1.012)
  starting transfers between devices: 7.83 us -> 41.8 us
  blocking collectives: 22 us -> 0 us
  between operations: 13.5 us -> 0.19 us
  waiting for transfers between devices: 96.2 us -> 91.1 us
  local copies, waits for them, and re-layouts: 5.88 us -> 10.3 us
  Pallas kernels: 13 us -> 16.8 us
    all_gather x1 -> x0, waiting for transfers between devices: 72 us -> none  [body(): weights = lax.all_gather(proj_weight[0], 'tm', axis=0, tiled=True)]
    ppermute x0 -> x16, waiting for transfers between devices: none -> 67.7 us  [the longest x6 58.6 us: body(): w_l, p_l = lax.ppermute((w_l, p_l), 'tm', left)]
    ppermute x0 -> x16, starting transfers between devices: none -> 26.5 us  [the longest x6 22.1 us: body(): w_l, p_l = lax.ppermute((w_l, p_l), 'tm', left)]
    all_gather x1 -> x0, blocking collectives: 22 us -> none  [body(): idx = lax.all_gather(local_idx, 'tm', axis=0, tiled=True).reshape(-1)]
    all_to_all x1, starting transfers between devices: 7.83 us -> 15.2 us  [body(): lax.all_to_all(packed, 'owner', split_axis=0, concat_axis=0, tiled=True)]
    pallas_call x1, Pallas kernels: 9.69 us -> 13.5 us  [project(): pl.pallas_call(functools.partial(project_kernel, sizes, kp, block_len), o...]
    slice x0 -> x3, local copies, waits for them, and re-layouts: none -> 1.84 us  [the longest x2 0.96 us: body(): h_l, q_l = lax.ppermute((w_l[half:], p_l[half:]), 'tm', left)]
    concatenate x0 -> x4, local copies, waits for them, and re-layouts: none -> 1.75 us  [body(): idx = jnp.take(positions, jnp.concatenate(pats, axis=0), axis=0).reshape(-1)]
  transfers between devices with their start and end apart: 2 -> 17, of which waited for: 2 -> 10; matrix products, arithmetic and copies ran while one was open for 7% -> 9% of each run, Pallas kernels for 0% -> 0%
where the time goes in v4:
time: 167 us; the launch traced here: 166 us
  waiting for transfers between devices  91.1 us (55%)
  starting transfers between devices  41.8 us (25%)
  Pallas kernels  16.8 us (10%)
  local copies, waits for them, and re-layouts  10.3 us (6%)
  other arithmetic  6.08 us (4%)
    ppermute x6, waiting for transfers between devices, body(): w_l, p_l = lax.ppermute((w_l, p_l), 'tm', left)  58.6 us
    all_to_all x1, waiting for transfers between devices, body(): lax.all_to_all(packed, 'owner', split_axis=0, concat_axis=0, tiled=True)  23.4 us
    ppermute x6, starting transfers between devices, body(): w_l, p_l = lax.ppermute((w_l, p_l), 'tm', left)  22.1 us
    all_to_all x1, starting transfers between devices, body(): lax.all_to_all(packed, 'owner', split_axis=0, concat_axis=0, tiled=True)  15.2 us
    pallas_call x1, Pallas kernels, project(): pl.pallas_call(functools.partial(project_kernel, sizes, kp, block_len), o...  13.5 us
    ppermute x2, waiting for transfers between devices, body(): h_r, q_r = lax.ppermute((w_r[:half], p_r[:half]), 'tm', right)  5.02 us
    ppermute x2, waiting for transfers between devices, body(): h_l, q_l = lax.ppermute((w_l[half:], p_l[half:]), 'tm', left)  4.05 us
  transfers between devices with their start and end apart: 17, of which 10 were waited for; matrix products, arithmetic and copies ran while one was open for 9% of the time, Pallas kernels for 0%

profile of v4, /device:TPU:1, one launch (start us, length us, event | category | flops | bytes accessed | tf_op | source)
XLA Modules:
  0.0 166.2 jit_solution(5111655396334827055)
XLA Ops:
  0.0 6.4 %collective-permute-start.9 = (bf16[8,4,128,128]{3,2,1,0:T(8,128)(2,1)}, bf16[8,4,128,128]{3,2,1,0:T(8,128)(2,1)S(1)}, u32[]{:S(2)}, u32[]{:S(2)}) collective-permute-start(bf16[8,4,128,128]{3,2,1,0:T(8,128)(2,1)} %bitcast.28), channel_id=1, source_target_pairs={{0,224},{32,0},{64,32},{96,64},{128,96},{160,128},{192,160},{224,1... | collective-permute-start | bytes 3145736 | tf_op jit(solution)/shard_map/ppermute | solution.py:146
  6.4 22.2 %collective-permute-done.9.refs_2_ = bf16[8,4,128,128]{3,2,1,0:T(8,128)(2,1)S(1)} collective-permute-done((bf16[8,4,128,128]{3,2,1,0:T(8,128)(2,1)}, bf16[8,4,128,128]{3,2,1,0:T(8,128)(2,1)S(1)}, u32[]{:S(2)}, u32[]{:S(2)}) %collective-permute-start.9) | collective-permute-done | bytes 1048608 | tf_op jit(solution)/shard_map/ppermute | solution.py:146
  28.6 3.3 %collective-permute-start.11 = (bf16[8,4,128,128]{3,2,1,0:T(8,128)(2,1)S(1)}, bf16[8,4,128,128]{3,2,1,0:T(8,128)(2,1)}, u32[]{:S(2)}, u32[]{:S(2)}) collective-permute-start(bf16[8,4,128,128]{3,2,1,0:T(8,128)(2,1)S(1)} %collective-permute-done.9.refs_2_), channel_id=1, source_target_pairs={{0,224},{32,0},{64,32},{96,64},{128,96},{160,128},{192,160},{224,1... | collective-permute-start | bytes 3145736 | tf_op jit(solution)/shard_map/ppermute | solution.py:146
  31.9 21.0 %collective-permute-done.11.refs_4_ = bf16[8,4,128,128]{3,2,1,0:T(8,128)(2,1)} collective-permute-done((bf16[8,4,128,128]{3,2,1,0:T(8,128)(2,1)S(1)}, bf16[8,4,128,128]{3,2,1,0:T(8,128)(2,1)}, u32[]{:S(2)}, u32[]{:S(2)}) %collective-permute-start.11) | collective-permute-done | bytes 1048608 | tf_op jit(solution)/shard_map/ppermute | solution.py:146
  52.9 3.5 %collective-permute-start.13 = (bf16[8,4,128,128]{3,2,1,0:T(8,128)(2,1)}, bf16[8,4,128,128]{3,2,1,0:T(8,128)(2,1)S(1)}, u32[]{:S(2)}, u32[]{:S(2)}) collective-permute-start(bf16[8,4,128,128]{3,2,1,0:T(8,128)(2,1)} %collective-permute-done.11.refs_4_), channel_id=1, source_target_pairs={{0,224},{32,0},{64,32},{96,64},{128,96},{160,128},{192,160},{224,1... | collective-permute-start | bytes 3145736 | tf_op jit(solution)/shard_map/ppermute | solution.py:146
  56.4 2.7 %collective-permute-start.1 = (s32[8,4]{0,1:T(4,128)}, s32[8,4]{0,1:T(4,128)S(1)}, u32[]{:S(2)}, u32[]{:S(2)}) collective-permute-start(s32[8,4]{0,1:T(4,128)} %bitcast.32), channel_id=1, source_target_pairs={{0,224},{32,0},{64,32},{96,64},{128,96},{160,128},{192,160},{224,1... | collective-permute-start | bytes 392 | tf_op jit(solution)/shard_map/ppermute | solution.py:146
  59.1 0.7 dynamic-slice_bitcast_fusion
  59.7 0.7 iota_compare_fusion.1
  60.5 1.4 and_reduce_fusion
  61.9 0.1 select_reduce_fusion.2
  62.0 0.2 convert_reduce_fusion.1
  62.2 0.6 stack.39.blk_ref
  62.8 14.0 %collective-permute-done.1 = s32[8,4]{0,1:T(4,128)S(1)} collective-permute-done((s32[8,4]{0,1:T(4,128)}, s32[8,4]{0,1:T(4,128)S(1)}, u32[]{:S(2)}, u32[]{:S(2)}) %collective-permute-start.1) | collective-permute-done | bytes 160 | tf_op jit(solution)/shard_map/ppermute | solution.py:146
  76.8 3.3 %collective-permute-start.3 = (s32[8,4]{0,1:T(4,128)S(1)}, s32[8,4]{0,1:T(4,128)S(1)}, u32[]{:S(2)}, u32[]{:S(2)}) collective-permute-start(s32[8,4]{0,1:T(4,128)S(1)} %collective-permute-done.1), channel_id=1, source_target_pairs={{0,224},{32,0},{64,32},{96,64},{128,96},{160,128},{192,160},{224,1... | collective-permute-start | bytes 392 | tf_op jit(solution)/shard_map/ppermute | solution.py:146
  80.2 0.7 collective-permute-done.3
  80.9 2.9 %collective-permute-start.5 = (s32[8,4]{0,1:T(4,128)S(1)}, s32[8,4]{0,1:T(4,128)S(1)}, u32[]{:S(2)}, u32[]{:S(2)}) collective-permute-start(s32[8,4]{0,1:T(4,128)S(1)} %collective-permute-done.3), channel_id=1, source_target_pairs={{0,224},{32,0},{64,32},{96,64},{128,96},{160,128},{192,160},{224,1... | collective-permute-start | bytes 392 | tf_op jit(solution)/shard_map/ppermute | solution.py:146
  83.8 0.7 collective-permute-done.5
  84.6 2.9 %collective-permute-start.7 = (s32[4,4]{0,1:T(4,128)S(1)}, s32[4,4]{0,1:T(4,128)S(1)}, u32[]{:S(2)}, u32[]{:S(2)}) collective-permute-start(s32[4,4]{0,1:T(4,128)S(1)} %slice.13), channel_id=1, source_target_pairs={{0,224},{32,0},{64,32},{96,64},{128,96},{160,128},{192,160},{224,1... | collective-permute-start | bytes 200 | tf_op jit(solution)/shard_map/ppermute | solution.py:153
  87.5 0.7 collective-permute-done.7
  88.3 2.9 %collective-permute-done.6 = s32[4,4]{0,1:T(4,128)S(1)} collective-permute-done((s32[4,4]{0,1:T(4,128)S(1)}, s32[4,4]{0,1:T(4,128)S(1)}, u32[]{:S(2)}, u32[]{:S(2)}) %collective-permute-start.6) | collective-permute-done | bytes 96 | tf_op jit(solution)/shard_map/ppermute | solution.py:152
  91.2 0.8 concatenate.49
  92.0 0.1 copy.18
  92.1 0.1 concatenate.50
  92.2 0.8 concatenate.60
  92.9 0.9 slice.19
  93.8 0.9 slice.18
  94.7 1.5 collective-permute-start.14
  96.2 0.1 copy.23
  96.3 0.1 reshape.432
  96.4 1.9 %gather_fusion = s32[256]{0:T(256)S(1)} fusion(s32[32]{0:T(128)S(1)} %multiply_add_fusion, s32[1024]{0:T(1024)S(1)} %pad_clamp_fusion), kind=kCustom, calls=%fused_computation | custom fusion | bytes 3072 | tf_op jit(solution)/shard_map/jit(_take)/gather | solution.py:159
  98.3 0.5 and_select_fusion.idx_ref
  98.9 3.3 %collective-permute-done.15.refs_8_ = bf16[4,4,128,128]{3,2,1,0:T(8,128)(2,1)} collective-permute-done((bf16[4,4,128,128]{3,2,1,0:T(8,128)(2,1)}, bf16[4,4,128,128]{3,2,1,0:T(8,128)(2,1)}, u32[]{:S(2)}, u32[]{:S(2)}) %collective-permute-start.15) | collective-permute-done | bytes 524320 | tf_op jit(solution)/shard_map/ppermute | solution.py:153
  102.2 2.1 %collective-permute-done.14.refs_7_ = bf16[4,4,128,128]{3,2,1,0:T(8,128)(2,1)} collective-permute-done((bf16[4,4,128,128]{3,2,1,0:T(8,128)(2,1)}, bf16[4,4,128,128]{3,2,1,0:T(8,128)(2,1)}, u32[]{:S(2)}, u32[]{:S(2)}) %collective-permute-start.14) | collective-permute-done | bytes 524320 | tf_op jit(solution)/shard_map/ppermute | solution.py:152
  104.3 13.5 %shard_map.64 = f32[64,64,128]{2,1,0:T(8,128)} custom-call(s32[256]{0:T(256)} %and_select_fusion.idx_ref, s32[9]{0:T(128)} %stack.39.blk_ref, bf16[64,8192]{1,0:T(8,128)(2,1)} %p_ref.1, bf16[8,4,128,128]{3,2,1,0:T(8,128)(2,1)} %bitcast.30, bf16[8,4,128,128]{3,2,1,0:T(8,128)(2,1)} %copy-done.4, bf16[8,4,128,128]{3,2,1,0:T(8,128)(2,1)} %copy-done.3, ...), custom_call_target="tpu_custom_call" | custom-call | flops 536870912 | bytes 11534336 | tf_op jit(solution)/shard_map/pallas_call | solution.py:78
  117.8 15.2 %all-to-all-start = ((f32[64,64,128]{2,1,0:T(8,128)}), f32[64,64,128]{2,1,0:T(8,128)S(1)}, u32[]{:S(2)}, u32[]{:S(2)}) async-start(f32[64,64,128]{2,1,0:T(8,128)} %shard_map.64), calls=%async_computation | async-start | bytes 4194304 | tf_op jit(solution)/shard_map/all_to_all | solution.py:162
  133.0 0.6 dynamic_slice.10
  133.6 0.7 dynamic-slice_bitcast_fusion.1
  134.3 0.6 iota_compare_fusion.3
  135.0 0.8 fusion
  135.8 0.6 convert_reduce_fusion
  136.4 0.1 fusion.2
  136.5 0.8 select_reduce_fusion
  137.3 0.1 select_reduce_fusion.1
  137.5 0.1 copy.17
  137.6 0.6 select_n.82.dest_ref
  138.2 23.4 %all-to-all-done.r_ref = f32[64,64,128]{2,1,0:T(8,128)S(1)} async-done(((f32[64,64,128]{2,1,0:T(8,128)}), f32[64,64,128]{2,1,0:T(8,128)S(1)}, u32[]{:S(2)}, u32[]{:S(2)}) %all-to-all-start) | async-done | bytes 2097184 | tf_op jit(solution)/shard_map/all_to_all | solution.py:162
  161.6 1.3 copy-done
  163.0 3.3 %shard_map.65 = f32[36,64,128]{2,1,0:T(8,128)} custom-call(s32[64]{0:T(128)} %select_n.82.dest_ref, f32[64,64,128]{2,1,0:T(8,128)} %copy-done), custom_call_target="tpu_custom_call" | custom-call | tf_op jit(solution)/shard_map/pallas_call | solution.py:115
  (34 shorter events, 0.2 us)
Async XLA Ops:
  0.0 28.6 %collective-permute-start.9 = (bf16[8,4,128,128]{3,2,1,0:T(8,128)(2,1)}, bf16[8,4,128,128]{3,2,1,0:T(8,128)(2,1)S(1)}, u32[]{:S(2)}, u32[]{:S(2)}) collective-permute-start(bf16[8,4,128,128]{3,2,1,0:T(8,128)(2,1)} %bitcast.28), channel_id=1, source_target_pairs={{0,224},{32,0},{64,32},{96,64},{128,96},{160,128},{192,160},{224,1... | collective-permute-start | bytes 3145736 | tf_op jit(solution)/shard_map/ppermute | solution.py:146
  6.4 25.5 %collective-permute-start.8 = (bf16[8,4,128,128]{3,2,1,0:T(8,128)(2,1)}, bf16[8,4,128,128]{3,2,1,0:T(8,128)(2,1)S(1)}, u32[]{:S(2)}, u32[]{:S(2)}) collective-permute-start(bf16[8,4,128,128]{3,2,1,0:T(8,128)(2,1)} %bitcast.29), channel_id=1, source_target_pairs={{0,32},{32,64},{64,96},{96,128},{128,160},{160,192},{192,224},{224... | collective-permute-start | bytes 3145736 | tf_op jit(solution)/shard_map/ppermute | solution.py:145
  28.6 69.7 %copy-start.3 = (bf16[8,4,128,128]{3,2,1,0:T(8,128)(2,1)}, bf16[8,4,128,128]{3,2,1,0:T(8,128)(2,1)S(1)}, u32[]{:S(2)}) copy-start(bf16[8,4,128,128]{3,2,1,0:T(8,128)(2,1)S(1)} %collective-permute-done.9.refs_2_) | copy-start | bytes 3145732
  28.6 24.3 %collective-permute-start.11 = (bf16[8,4,128,128]{3,2,1,0:T(8,128)(2,1)S(1)}, bf16[8,4,128,128]{3,2,1,0:T(8,128)(2,1)}, u32[]{:S(2)}, u32[]{:S(2)}) collective-permute-start(bf16[8,4,128,128]{3,2,1,0:T(8,128)(2,1)S(1)} %collective-permute-done.9.refs_2_), channel_id=1, source_target_pairs={{0,224},{32,0},{64,32},{96,64},{128,96},{160,128},{192,160},{224,1... | collective-permute-start | bytes 3145736 | tf_op jit(solution)/shard_map/ppermute | solution.py:146
  31.9 24.5 %copy-start.4 = (bf16[8,4,128,128]{3,2,1,0:T(8,128)(2,1)}, bf16[8,4,128,128]{3,2,1,0:T(8,128)(2,1)S(1)}, u32[]{:S(2)}) copy-start(bf16[8,4,128,128]{3,2,1,0:T(8,128)(2,1)S(1)} %collective-permute-done.8.refs_1_) | copy-start | bytes 3145732
  31.9 24.5 %collective-permute-start.10 = (bf16[8,4,128,128]{3,2,1,0:T(8,128)(2,1)S(1)}, bf16[8,4,128,128]{3,2,1,0:T(8,128)(2,1)}, u32[]{:S(2)}, u32[]{:S(2)}) collective-permute-start(bf16[8,4,128,128]{3,2,1,0:T(8,128)(2,1)S(1)} %collective-permute-done.8.refs_1_), channel_id=1, source_target_pairs={{0,32},{32,64},{64,96},{96,128},{128,160},{160,192},{192,224},{224... | collective-permute-start | bytes 3145736 | tf_op jit(solution)/shard_map/ppermute | solution.py:145
  52.9 40.1 %collective-permute-start.13 = (bf16[8,4,128,128]{3,2,1,0:T(8,128)(2,1)}, bf16[8,4,128,128]{3,2,1,0:T(8,128)(2,1)S(1)}, u32[]{:S(2)}, u32[]{:S(2)}) collective-permute-start(bf16[8,4,128,128]{3,2,1,0:T(8,128)(2,1)} %collective-permute-done.11.refs_4_), channel_id=1, source_target_pairs={{0,224},{32,0},{64,32},{96,64},{128,96},{160,128},{192,160},{224,1... | collective-permute-start | bytes 3145736 | tf_op jit(solution)/shard_map/ppermute | solution.py:146
  56.4 37.5 %collective-permute-start.12 = (bf16[8,4,128,128]{3,2,1,0:T(8,128)(2,1)}, bf16[8,4,128,128]{3,2,1,0:T(8,128)(2,1)S(1)}, u32[]{:S(2)}, u32[]{:S(2)}) collective-permute-start(bf16[8,4,128,128]{3,2,1,0:T(8,128)(2,1)} %collective-permute-done.10.refs_3_), channel_id=1, source_target_pairs={{0,32},{32,64},{64,96},{96,128},{128,160},{160,192},{192,224},{224... | collective-permute-start | bytes 3145736 | tf_op jit(solution)/shard_map/ppermute | solution.py:145
  56.4 20.4 %collective-permute-start.1 = (s32[8,4]{0,1:T(4,128)}, s32[8,4]{0,1:T(4,128)S(1)}, u32[]{:S(2)}, u32[]{:S(2)}) collective-permute-start(s32[8,4]{0,1:T(4,128)} %bitcast.32), channel_id=1, source_target_pairs={{0,224},{32,0},{64,32},{96,64},{128,96},{160,128},{192,160},{224,1... | collective-permute-start | bytes 392 | tf_op jit(solution)/shard_map/ppermute | solution.py:146
  59.1 21.1 %collective-permute-start = (s32[8,4]{0,1:T(4,128)}, s32[8,4]{0,1:T(4,128)S(1)}, u32[]{:S(2)}, u32[]{:S(2)}) collective-permute-start(s32[8,4]{0,1:T(4,128)} %bitcast.33), channel_id=1, source_target_pairs={{0,32},{32,64},{64,96},{96,128},{128,160},{160,192},{192,224},{224... | collective-permute-start | bytes 392 | tf_op jit(solution)/shard_map/ppermute | solution.py:145
  76.8 4.1 %collective-permute-start.3 = (s32[8,4]{0,1:T(4,128)S(1)}, s32[8,4]{0,1:T(4,128)S(1)}, u32[]{:S(2)}, u32[]{:S(2)}) collective-permute-start(s32[8,4]{0,1:T(4,128)S(1)} %collective-permute-done.1), channel_id=1, source_target_pairs={{0,224},{32,0},{64,32},{96,64},{128,96},{160,128},{192,160},{224,1... | collective-permute-start | bytes 392 | tf_op jit(solution)/shard_map/ppermute | solution.py:146
  80.2 3.6 %collective-permute-start.2 = (s32[8,4]{0,1:T(4,128)S(1)}, s32[8,4]{0,1:T(4,128)S(1)}, u32[]{:S(2)}, u32[]{:S(2)}) collective-permute-start(s32[8,4]{0,1:T(4,128)S(1)} %collective-permute-done), channel_id=1, source_target_pairs={{0,32},{32,64},{64,96},{96,128},{128,160},{160,192},{192,224},{224... | collective-permute-start | bytes 392 | tf_op jit(solution)/shard_map/ppermute | solution.py:145
  80.9 3.6 %collective-permute-start.5 = (s32[8,4]{0,1:T(4,128)S(1)}, s32[8,4]{0,1:T(4,128)S(1)}, u32[]{:S(2)}, u32[]{:S(2)}) collective-permute-start(s32[8,4]{0,1:T(4,128)S(1)} %collective-permute-done.3), channel_id=1, source_target_pairs={{0,224},{32,0},{64,32},{96,64},{128,96},{160,128},{192,160},{224,1... | collective-permute-start | bytes 392 | tf_op jit(solution)/shard_map/ppermute | solution.py:146
  83.8 3.7 %collective-permute-start.4 = (s32[8,4]{0,1:T(4,128)S(1)}, s32[8,4]{0,1:T(4,128)S(1)}, u32[]{:S(2)}, u32[]{:S(2)}) collective-permute-start(s32[8,4]{0,1:T(4,128)S(1)} %collective-permute-done.2), channel_id=1, source_target_pairs={{0,32},{32,64},{64,96},{96,128},{128,160},{160,192},{192,224},{224... | collective-permute-start | bytes 392 | tf_op jit(solution)/shard_map/ppermute | solution.py:145
  84.6 3.6 %collective-permute-start.7 = (s32[4,4]{0,1:T(4,128)S(1)}, s32[4,4]{0,1:T(4,128)S(1)}, u32[]{:S(2)}, u32[]{:S(2)}) collective-permute-start(s32[4,4]{0,1:T(4,128)S(1)} %slice.13), channel_id=1, source_target_pairs={{0,224},{32,0},{64,32},{96,64},{128,96},{160,128},{192,160},{224,1... | collective-permute-start | bytes 200 | tf_op jit(solution)/shard_map/ppermute | solution.py:153
  87.5 3.6 %collective-permute-start.6 = (s32[4,4]{0,1:T(4,128)S(1)}, s32[4,4]{0,1:T(4,128)S(1)}, u32[]{:S(2)}, u32[]{:S(2)}) collective-permute-start(s32[4,4]{0,1:T(4,128)S(1)} %bitcast.40), channel_id=1, source_target_pairs={{0,32},{32,64},{64,96},{96,128},{128,160},{160,192},{192,224},{224... | collective-permute-start | bytes 200 | tf_op jit(solution)/shard_map/ppermute | solution.py:152
  92.9 5.4 %copy-start.1 = (bf16[8,4,128,128]{3,2,1,0:T(8,128)(2,1)}, bf16[8,4,128,128]{3,2,1,0:T(8,128)(2,1)S(1)}, u32[]{:S(2)}) copy-start(bf16[8,4,128,128]{3,2,1,0:T(8,128)(2,1)S(1)} %collective-permute-done.13.refs_6_) | copy-start | bytes 3145732
  93.8 8.3 %collective-permute-start.15 = (bf16[4,4,128,128]{3,2,1,0:T(8,128)(2,1)}, bf16[4,4,128,128]{3,2,1,0:T(8,128)(2,1)}, u32[]{:S(2)}, u32[]{:S(2)}) collective-permute-start(bf16[4,4,128,128]{3,2,1,0:T(8,128)(2,1)} %slice.19), channel_id=1, source_target_pairs={{0,224},{32,0},{64,32},{96,64},{128,96},{160,128},{192,160},{224,1... | collective-permute-start | bytes 1572872 | tf_op jit(solution)/shard_map/ppermute | solution.py:153
  93.8 4.5 %copy-start.2 = (bf16[8,4,128,128]{3,2,1,0:T(8,128)(2,1)}, bf16[8,4,128,128]{3,2,1,0:T(8,128)(2,1)S(1)}, u32[]{:S(2)}) copy-start(bf16[8,4,128,128]{3,2,1,0:T(8,128)(2,1)S(1)} %collective-permute-done.12.refs_5_) | copy-start | bytes 3145732
  94.7 9.6 %collective-permute-start.14 = (bf16[4,4,128,128]{3,2,1,0:T(8,128)(2,1)}, bf16[4,4,128,128]{3,2,1,0:T(8,128)(2,1)}, u32[]{:S(2)}, u32[]{:S(2)}) collective-permute-start(bf16[4,4,128,128]{3,2,1,0:T(8,128)(2,1)} %slice.18), channel_id=1, source_target_pairs={{0,32},{32,64},{64,96},{96,128},{128,160},{160,192},{192,224},{224... | collective-permute-start | bytes 1572872 | tf_op jit(solution)/shard_map/ppermute | solution.py:152
  117.8 15.3 %copy-start.6 = (s32[32]{0:T(128)S(1)}, s32[32]{0:T(128)}, u32[]{:S(2)}) copy-start(s32[32]{0:T(128)} %param.11) | copy-start | bytes 388
  117.8 17.2 %copy-start.5 = (s32[32,32]{1,0:T(8,128)S(1)}, s32[32,32]{1,0:T(8,128)}, u32[]{:S(2)}) copy-start(s32[32,32]{1,0:T(8,128)} %param.9) | copy-start | bytes 12292
  117.8 43.8 %all-to-all-start = ((f32[64,64,128]{2,1,0:T(8,128)}), f32[64,64,128]{2,1,0:T(8,128)S(1)}, u32[]{:S(2)}, u32[]{:S(2)}) async-start(f32[64,64,128]{2,1,0:T(8,128)} %shard_map.64), calls=%async_computation | async-start | bytes 4194304 | tf_op jit(solution)/shard_map/all_to_all | solution.py:162
  161.6 1.3 copy-start

commit v5 on v4

--- a/solution.py
+++ b/solution.py
@@ -40,7 +40,7 @@
     return jnp.where(found, dest, capacity).reshape(-1)
 
 
-def project_kernel(sizes, kp, block_len, idx_ref, blk_ref, p_ref, *refs):
+def project_kernel(sizes, kp, block_len, idx_ref, p_ref, *refs):
     n = len(sizes)
     w_refs = refs[:n]
     o_ref, buf, sem = refs[n:]
@@ -48,7 +48,10 @@
 
     def fetch(q):
         slot = q % 2
-        return pltpu.make_async_copy(w_refs[q], buf.at[slot, pl.ds(0, sizes[q])], sem.at[slot])
+        rows = sizes[q] * kp * block_len
+        return pltpu.make_async_copy(
+            w_refs[q].at[pl.ds(0, rows)], buf.at[slot, pl.ds(0, rows)], sem.at[slot]
+        )
 
     copies = [fetch(0)]
     copies[0].start()
@@ -60,33 +63,33 @@
             copies[q + 1].start()
         slot = q % 2
         for g in range(sizes[q]):
-            col = pl.multiple_of((blk_ref[q] + g) * block_len, block_len)
-            rows = p_ref[:, pl.ds(col, block_len)]
-            wide = jnp.concatenate([buf[slot, g, k] for k in range(kp)], axis=1)
+            face = base + g
+            rows = p_ref[:, face * block_len:(face + 1) * block_len]
+            wide = jnp.concatenate(
+                [buf[slot, (g * kp + k) * block_len:(g * kp + k + 1) * block_len, :] for k in range(kp)],
+                axis=1,
+            )
             prod = jnp.dot(rows, wide, preferred_element_type=jnp.float32)
             for k in range(kp):
-                pos = idx_ref[(base + g) * kp + k]
+                pos = idx_ref[face * kp + k]
                 o_ref[pos] += prod[:, k * block_len:(k + 1) * block_len]
         base += sizes[q]
 
 
-def project(idx, blk, pressure, pieces, n_pos):
-    sizes = tuple(w.shape[0] for w in pieces)
-    _, kp, block_len, _ = pieces[0].shape
-    time_len = pressure.shape[0]
+def project(idx, pressure, pieces, sizes, kp, n_pos):
+    time_len, block_len = pressure.shape[0], pieces[0].shape[1]
     face_blocks = sum(sizes)
     return pl.pallas_call(
-        functools.partial(project_kernel, sizes, kp, block_len),
+        functools.partial(project_kernel, tuple(sizes), kp, block_len),
         out_shape=jax.ShapeDtypeStruct((n_pos, time_len, block_len), jnp.float32),
         in_specs=[
-            pl.BlockSpec(memory_space=pltpu.SMEM),
             pl.BlockSpec(memory_space=pltpu.SMEM),
             pl.BlockSpec(memory_space=pltpu.VMEM),
         ]
         + [pl.BlockSpec(memory_space=pl.ANY)] * len(pieces),
         out_specs=pl.BlockSpec(memory_space=pltpu.VMEM),
         scratch_shapes=[
-            pltpu.VMEM((2, max(sizes), kp, block_len, block_len), pieces[0].dtype),
+            pltpu.VMEM((2, max(sizes) * kp * block_len, block_len), pieces[0].dtype),
             pltpu.SemaphoreType.DMA((2,)),
         ],
         cost_estimate=pl.CostEstimate(
@@ -95,7 +98,7 @@
             + n_pos * time_len * block_len * 4,
             transcendentals=0,
         ),
-    )(idx, blk, pressure, *pieces)
+    )(idx, pressure, *pieces)
 
 
 def collect_kernel(n_rows, dest_ref, r_ref, o_ref, acc_ref):
@@ -134,31 +137,41 @@
 
     n_tm = lax.axis_size("tm")
     t = lax.axis_index("tm")
-    fb_dev = pattern.shape[1]
+    fb_dev, kp, block_len = proj_weight.shape[1], proj_weight.shape[2], proj_weight.shape[3]
+    half = fb_dev // 2
+    w_rows = fb_dev * kp * block_len
     right = [(i, (i + 1) % n_tm) for i in range(n_tm)]
     left = [(i, (i - 1) % n_tm) for i in range(n_tm)]
 
-    w_r = w_l = proj_weight[0]
-    p_r = p_l = pattern[0]
-    pieces, pats, starts = [w_r], [p_r], [t * fb_dev]
+    pat_row = jnp.zeros((1, block_len), proj_weight.dtype)
+    pat_row = pat_row.at[0, : fb_dev * kp].set(pattern[0].reshape(-1).astype(proj_weight.dtype))
+    own = jnp.concatenate([proj_weight[0].reshape(w_rows, block_len), pat_row], axis=0)
+
+    x_r = x_l = own
+    pieces, sizes, lane_at, order = [own], [fb_dev], [0], [t]
     for s in range(1, n_tm // 2):
-        w_r, p_r = lax.ppermute((w_r, p_r), "tm", right)
-        w_l, p_l = lax.ppermute((w_l, p_l), "tm", left)
-        pieces += [w_r, w_l]
-        pats += [p_r, p_l]
-        starts += [((t - s) % n_tm) * fb_dev, ((t + s) % n_tm) * fb_dev]
-    half = fb_dev // 2
-    far = (t + n_tm // 2) % n_tm
-    h_r, q_r = lax.ppermute((w_r[:half], p_r[:half]), "tm", right)
-    h_l, q_l = lax.ppermute((w_l[half:], p_l[half:]), "tm", left)
+        x_r = lax.ppermute(x_r, "tm", right)
+        x_l = lax.ppermute(x_l, "tm", left)
+        pieces += [x_r, x_l]
+        sizes += [fb_dev, fb_dev]
+        lane_at += [0, 0]
+        order += [(t - s) % n_tm, (t + s) % n_tm]
+    h_rows = half * kp * block_len
+    h_r = lax.ppermute(jnp.concatenate([x_r[:h_rows], x_r[w_rows:]], axis=0), "tm", right)
+    h_l = lax.ppermute(x_l[h_rows:], "tm", left)
     pieces += [h_r, h_l]
-    pats += [q_r, q_l]
-    starts += [far * fb_dev, far * fb_dev + half]
+    sizes += [half, half]
+    lane_at += [0, half * kp]
+    order += [(t + n_tm // 2) % n_tm]
 
     positions = send_positions(panel_list, owner_list, owner_count, own_index, slot_count)
-    idx = jnp.take(positions, jnp.concatenate(pats, axis=0), axis=0).reshape(-1)
-    blk = jnp.stack(starts).astype(jnp.int32)
-    packed = project(idx, blk, pressure, pieces, n_pos)
+    pats = [x[-1, a:a + n * kp] for x, n, a in zip(pieces, sizes, lane_at)]
+    pat_all = jnp.concatenate(pats).astype(jnp.int32)
+    idx = jnp.take(positions, pat_all, axis=0)
+    time_len = pressure.shape[0]
+    blocks = pressure.reshape(time_len, n_tm, fb_dev * block_len)
+    ordered = jnp.take(blocks, jnp.stack(order), axis=1).reshape(time_len, -1)
+    packed = project(idx, ordered, pieces, sizes, kp, n_pos)
     received = lax.all_to_all(packed, "owner", split_axis=0, concat_axis=0, tiled=True)
     dest = receive_slots(panel_list, owner_list, owner_count, own_index, slot_count)
     return collect(dest, received, capacity)

time: 167 us -> 175 us (1.048)
  other arithmetic: 6.08 us -> 29.5 us
  starting transfers between devices: 41.8 us -> 28.3 us
    select_n x2 -> x3, other arithmetic: 0.54 us -> 17.3 us  [the longest x1 16.2 us: body(): idx = jnp.take(positions, pat_all, axis=0)]
    ppermute x16 -> x8, starting transfers between devices: 26.5 us -> 16.9 us  [the longest x3 13.3 us: body(): x_l = lax.ppermute(x_l, 'tm', left)]
    gather x1 -> x3, other arithmetic: 0.01 us -> 4.61 us  [the longest x2 4.6 us: body(): idx = jnp.take(positions, pat_all, axis=0)]
    all_to_all x1, starting transfers between devices: 15.2 us -> 11.5 us  [body(): lax.all_to_all(packed, 'owner', split_axis=0, concat_axis=0, tiled=True)]
    ppermute x16 -> x8, waiting for transfers between devices: 67.7 us -> 65.3 us  [the longest x3 55.7 us: body(): x_l = lax.ppermute(x_l, 'tm', left)]
    unnamed x14 -> x24, local copies, waits for them, and re-layouts: 1.37 us -> 3.64 us
    slice x3, local copies, waits for them, and re-layouts: 1.84 us -> 0.07 us  [the longest x1 0.04 us: body(): h_l = lax.ppermute(x_l[h_rows:], 'tm', left)]
  transfers between devices with their start and end apart: 17 -> 9, of which waited for: 10 -> 6; matrix products, arithmetic and copies ran while one was open for 9% -> 7% of each run, Pallas kernels for 0% -> 0%
where the time goes in v5:
time: 175 us; the launch traced here: 174 us
  waiting for transfers between devices  89.4 us (51%)
  other arithmetic  29.5 us (17%)
  starting transfers between devices  28.3 us (16%)
  Pallas kernels  16.8 us (10%)
  local copies, waits for them, and re-layouts  10.1 us (6%)
    ppermute x3, waiting for transfers between devices, body(): x_l = lax.ppermute(x_l, 'tm', left)  55.7 us
    all_to_all x1, waiting for transfers between devices, body(): lax.all_to_all(packed, 'owner', split_axis=0, concat_axis=0, tiled=True)  24.1 us
    select_n x1, other arithmetic, body(): idx = jnp.take(positions, pat_all, axis=0)  16.2 us
    pallas_call x1, Pallas kernels, project(): pl.pallas_call(functools.partial(project_kernel, tuple(sizes), kp, block_...  13.5 us
    ppermute x3, starting transfers between devices, body(): x_l = lax.ppermute(x_l, 'tm', left)  13.3 us
    all_to_all x1, starting transfers between devices, body(): lax.all_to_all(packed, 'owner', split_axis=0, concat_axis=0, tiled=True)  11.5 us
    ppermute x1, waiting for transfers between devices, body(): h_l = lax.ppermute(x_l[h_rows:], 'tm', left)  7.08 us
    gather x2, other arithmetic, body(): idx = jnp.take(positions, pat_all, axis=0)  4.6 us
  transfers between devices with their start and end apart: 9, of which 6 were waited for; matrix products, arithmetic and copies ran while one was open for 7% of the time, Pallas kernels for 0%

profile of v5, /device:TPU:1, one launch (start us, length us, event | category | flops | bytes accessed | tf_op | source)
XLA Modules:
  0.0 174.4 jit_solution(14491896212256838476)
XLA Ops:
  0.0 0.6 compare_reduce_fusion.25
  0.6 1.3 convert_select_fusion
  2.0 0.1 copy.20
  2.1 0.1 squeeze.21
  2.2 1.4 fusion.1.refs_0_
  3.6 6.5 %collective-permute-start.1 = (bf16[4097,128]{1,0:T(8,128)(2,1)S(1)}, bf16[4097,128]{1,0:T(8,128)(2,1)}, u32[]{:S(2)}, u32[]{:S(2)}) collective-permute-start(bf16[4097,128]{1,0:T(8,128)(2,1)S(1)} %fusion.1.refs_0_), channel_id=1, source_target_pairs={{0,224},{32,0},{64,32},{96,64},{128,96},{160,128},{192,160},{224,1... | collective-permute-start | bytes 3146504 | tf_op jit(solution)/shard_map/ppermute | solution.py:154
  10.2 0.1 stack.62
  10.5 0.6 gather_fusion
  11.2 0.6 copy-done.8
  11.9 0.7 and_reduce_fusion
  12.6 0.1 select_reduce_fusion.2
  12.7 0.2 convert_reduce_fusion.1
  12.9 19.0 %collective-permute-done.1.refs_2_ = bf16[4097,128]{1,0:T(8,128)(2,1)} collective-permute-done((bf16[4097,128]{1,0:T(8,128)(2,1)S(1)}, bf16[4097,128]{1,0:T(8,128)(2,1)}, u32[]{:S(2)}, u32[]{:S(2)}) %collective-permute-start.1) | collective-permute-done | bytes 1048864 | tf_op jit(solution)/shard_map/ppermute | solution.py:154
  31.9 3.5 %collective-permute-start.3 = (bf16[4097,128]{1,0:T(8,128)(2,1)}, bf16[4097,128]{1,0:T(8,128)(2,1)S(1)}, u32[]{:S(2)}, u32[]{:S(2)}) collective-permute-start(bf16[4097,128]{1,0:T(8,128)(2,1)} %collective-permute-done.1.refs_2_), channel_id=1, source_target_pairs={{0,224},{32,0},{64,32},{96,64},{128,96},{160,128},{192,160},{224,1... | collective-permute-start | bytes 3146504 | tf_op jit(solution)/shard_map/ppermute | solution.py:154
  35.4 1.2 broadcast_select_fusion.p_ref
  36.6 20.2 %collective-permute-done.3.refs_4_ = bf16[4097,128]{1,0:T(8,128)(2,1)S(1)} collective-permute-done((bf16[4097,128]{1,0:T(8,128)(2,1)}, bf16[4097,128]{1,0:T(8,128)(2,1)S(1)}, u32[]{:S(2)}, u32[]{:S(2)}) %collective-permute-start.3) | collective-permute-done | bytes 1048864 | tf_op jit(solution)/shard_map/ppermute | solution.py:154
  56.8 3.3 %collective-permute-start.5 = (bf16[4097,128]{1,0:T(8,128)(2,1)S(1)}, bf16[4097,128]{1,0:T(8,128)(2,1)S(1)}, u32[]{:S(2)}, u32[]{:S(2)}) collective-permute-start(bf16[4097,128]{1,0:T(8,128)(2,1)S(1)} %collective-permute-done.3.refs_4_), channel_id=1, source_target_pairs={{0,224},{32,0},{64,32},{96,64},{128,96},{160,128},{192,160},{224,1... | collective-permute-start | bytes 3146504 | tf_op jit(solution)/shard_map/ppermute | solution.py:154
  60.1 0.7 fusion.7
  60.8 0.1 concatenate.88
  61.0 0.7 fusion.6
  61.7 0.7 slice_bitcast_fusion.13
  62.4 0.7 slice_bitcast_fusion.15
  63.1 0.7 slice_bitcast_fusion.11
  63.7 16.5 %collective-permute-done.5.refs_6_ = bf16[4097,128]{1,0:T(8,128)(2,1)S(1)} collective-permute-done((bf16[4097,128]{1,0:T(8,128)(2,1)S(1)}, bf16[4097,128]{1,0:T(8,128)(2,1)S(1)}, u32[]{:S(2)}, u32[]{:S(2)}) %collective-permute-start.5) | collective-permute-done | bytes 1048864 | tf_op jit(solution)/shard_map/ppermute | solution.py:154
  80.3 3.5 %collective-permute-start.7 = (bf16[2049,128]{1,0:T(8,128)(2,1)S(1)}, bf16[2049,128]{1,0:T(8,128)(2,1)S(1)}, u32[]{:S(2)}, u32[]{:S(2)}) collective-permute-start(bf16[2049,128]{1,0:T(8,128)(2,1)S(1)} %slice.105), channel_id=1, source_target_pairs={{0,224},{32,0},{64,32},{96,64},{128,96},{160,128},{192,160},{224,1... | collective-permute-start | bytes 1573640 | tf_op jit(solution)/shard_map/ppermute | solution.py:161
  84.0 0.8 copy-done.3
  84.8 7.1 %collective-permute-done.7.refs_8_ = bf16[2049,128]{1,0:T(8,128)(2,1)S(1)} collective-permute-done((bf16[2049,128]{1,0:T(8,128)(2,1)S(1)}, bf16[2049,128]{1,0:T(8,128)(2,1)S(1)}, u32[]{:S(2)}, u32[]{:S(2)}) %collective-permute-start.7) | collective-permute-done | bytes 524576 | tf_op jit(solution)/shard_map/ppermute | solution.py:161
  91.9 0.8 copy-done.6
  92.7 2.5 %collective-permute-done.6.refs_7_ = bf16[2049,128]{1,0:T(8,128)(2,1)S(1)} collective-permute-done((bf16[2049,128]{1,0:T(8,128)(2,1)S(1)}, bf16[2049,128]{1,0:T(8,128)(2,1)S(1)}, u32[]{:S(2)}, u32[]{:S(2)}) %collective-permute-start.6) | collective-permute-done | bytes 524576 | tf_op jit(solution)/shard_map/ppermute | solution.py:160
  95.2 0.1 concatenate.97
  95.3 4.5 %compare_select_fusion.1 = (s32[256,1]{0,1:T(1,128)S(1)}, s32[256,1]{0,1:T(1,128)S(1)}) fusion(s32[]{:T(128)} %bitcast.45, s32[]{:T(128)} %bitcast.46, s32[]{:T(128)} %bitcast.47, s32[]{:T(128)} %bitcast.48, s32[]{:T(128)} %bitcast.49, s32[]{:T(128)} %bitcast.51, s32[]{:T(128)} %bitcast.50, bf16[256,1]{0,1:T(2,128)(2,1)S(1)} %concatenate.97), kind=kLoop, calls=%fused_computation.49 | loop fusion | flops 4096 | bytes 2588 | tf_op jit(solution)/shard_map/jit(_take)/gather | solution.py:170
  99.8 0.1 compare_reduce_fusion.24
  99.9 0.1 concatenate.87
  100.0 16.2 %and_select_fusion.idx_ref = s32[256]{0:T(256)} fusion(pred[256]{0:T(512)(128)(4,1)S(1)} %get-tuple-element.41, pred[256]{0:T(512)(128)(4,1)S(1)} %get-tuple-element.40, pred[256]{0:T(512)(128)(4,1)S(1)} %get-tuple-element.39, pred[256]{0:T(512)(128)(4,1)S(1)} %get-tuple-element.38, pred[256]{0:T(512)(128)(4,1)S(1)} %get-tuple-element.37, ...), kind=kLoop, calls=%fused_computation.59 | loop fusion | flops 8448 | bytes 9060 | tf_op jit(solution)/shard_map/jit(_take)/select_n | solution.py:170
  116.2 13.5 %shard_map.64 = f32[64,64,128]{2,1,0:T(8,128)} custom-call(s32[256]{0:T(256)} %and_select_fusion.idx_ref, bf16[64,8192]{1,0:T(8,128)(2,1)} %broadcast_select_fusion.p_ref, bf16[4097,128]{1,0:T(8,128)(2,1)} %copy-done.1, bf16[4097,128]{1,0:T(8,128)(2,1)} %collective-permute-done.refs_1_, bf16[4097,128]{1,0:T(8,128)(2,1)} %collective-permute-done.1.refs_2_, ...), custom_call_target="tpu_custom_call" | custom-call | flops 536870912 | bytes 11534336 | tf_op jit(solution)/shard_map/pallas_call | solution.py:82
  129.7 11.5 %all-to-all-start = ((f32[64,64,128]{2,1,0:T(8,128)}), f32[64,64,128]{2,1,0:T(8,128)S(1)}, u32[]{:S(2)}, u32[]{:S(2)}) async-start(f32[64,64,128]{2,1,0:T(8,128)} %shard_map.64), calls=%async_computation | async-start | bytes 4194304 | tf_op jit(solution)/shard_map/all_to_all | solution.py:175
  141.2 0.6 dynamic_slice.10
  141.8 0.6 iota_compare_fusion.4
  142.4 0.8 fusion.2
  143.2 0.6 convert_reduce_fusion
  143.9 0.1 fusion.4
  144.0 0.8 select_reduce_fusion
  144.8 0.1 select_reduce_fusion.1
  144.9 0.1 copy.19
  145.0 0.6 select_n.101.dest_ref
  145.6 24.1 %all-to-all-done.r_ref = f32[64,64,128]{2,1,0:T(8,128)S(1)} async-done(((f32[64,64,128]{2,1,0:T(8,128)}), f32[64,64,128]{2,1,0:T(8,128)S(1)}, u32[]{:S(2)}, u32[]{:S(2)}) %all-to-all-start) | async-done | bytes 2097184 | tf_op jit(solution)/shard_map/all_to_all | solution.py:175
  169.8 1.3 copy-done
  171.1 3.3 %shard_map.65 = f32[36,64,128]{2,1,0:T(8,128)} custom-call(s32[64]{0:T(128)} %select_n.101.dest_ref, f32[64,64,128]{2,1,0:T(8,128)} %copy-done), custom_call_target="tpu_custom_call" | custom-call | tf_op jit(solution)/shard_map/pallas_call | solution.py:118
  (49 shorter events, 0.9 us)
Async XLA Ops:
  2.2 8.2 %copy-start.5 = (bf16[64,8192]{1,0:T(8,128)(2,1)S(1)}, bf16[64,8192]{1,0:T(8,128)(2,1)}, u32[]{:S(2)}) copy-start(bf16[64,8192]{1,0:T(8,128)(2,1)} %param.8) | copy-start | bytes 3145732
  3.5 6.9 %copy-start.1 = (bf16[4097,128]{1,0:T(8,128)(2,1)}, bf16[4097,128]{1,0:T(8,128)(2,1)S(1)}, u32[]{:S(2)}) copy-start(bf16[4097,128]{1,0:T(8,128)(2,1)S(1)} %fusion.1.refs_0_) | copy-start | bytes 3146500
  3.6 28.4 %collective-permute-start.1 = (bf16[4097,128]{1,0:T(8,128)(2,1)S(1)}, bf16[4097,128]{1,0:T(8,128)(2,1)}, u32[]{:S(2)}, u32[]{:S(2)}) collective-permute-start(bf16[4097,128]{1,0:T(8,128)(2,1)S(1)} %fusion.1.refs_0_), channel_id=1, source_target_pairs={{0,224},{32,0},{64,32},{96,64},{128,96},{160,128},{192,160},{224,1... | collective-permute-start | bytes 3146504 | tf_op jit(solution)/shard_map/ppermute | solution.py:154
  10.0 25.4 %collective-permute-start = (bf16[4097,128]{1,0:T(8,128)(2,1)S(1)}, bf16[4097,128]{1,0:T(8,128)(2,1)}, u32[]{:S(2)}, u32[]{:S(2)}) collective-permute-start(bf16[4097,128]{1,0:T(8,128)(2,1)S(1)} %fusion.1.refs_0_), channel_id=1, source_target_pairs={{0,32},{32,64},{64,96},{96,128},{128,160},{160,192},{192,224},{224... | collective-permute-start | bytes 3146504 | tf_op jit(solution)/shard_map/ppermute | solution.py:153
  11.1 0.7 copy-start.8
  11.1 0.7 copy-start.10
  11.1 0.8 copy-start.9
  31.9 24.9 %collective-permute-start.3 = (bf16[4097,128]{1,0:T(8,128)(2,1)}, bf16[4097,128]{1,0:T(8,128)(2,1)S(1)}, u32[]{:S(2)}, u32[]{:S(2)}) collective-permute-start(bf16[4097,128]{1,0:T(8,128)(2,1)} %collective-permute-done.1.refs_2_), channel_id=1, source_target_pairs={{0,224},{32,0},{64,32},{96,64},{128,96},{160,128},{192,160},{224,1... | collective-permute-start | bytes 3146504 | tf_op jit(solution)/shard_map/ppermute | solution.py:154
  35.4 24.7 %collective-permute-start.2 = (bf16[4097,128]{1,0:T(8,128)(2,1)}, bf16[4097,128]{1,0:T(8,128)(2,1)}, u32[]{:S(2)}, u32[]{:S(2)}) collective-permute-start(bf16[4097,128]{1,0:T(8,128)(2,1)} %collective-permute-done.refs_1_), channel_id=1, source_target_pairs={{0,32},{32,64},{64,96},{96,128},{128,160},{160,192},{192,224},{224... | collective-permute-start | bytes 3146504 | tf_op jit(solution)/shard_map/ppermute | solution.py:153
  56.8 27.1 %copy-start.4 = (bf16[4097,128]{1,0:T(8,128)(2,1)}, bf16[4097,128]{1,0:T(8,128)(2,1)S(1)}, u32[]{:S(2)}) copy-start(bf16[4097,128]{1,0:T(8,128)(2,1)S(1)} %collective-permute-done.3.refs_4_) | copy-start | bytes 3146500
  56.8 23.5 %collective-permute-start.5 = (bf16[4097,128]{1,0:T(8,128)(2,1)S(1)}, bf16[4097,128]{1,0:T(8,128)(2,1)S(1)}, u32[]{:S(2)}, u32[]{:S(2)}) collective-permute-start(bf16[4097,128]{1,0:T(8,128)(2,1)S(1)} %collective-permute-done.3.refs_4_), channel_id=1, source_target_pairs={{0,224},{32,0},{64,32},{96,64},{128,96},{160,128},{192,160},{224,1... | collective-permute-start | bytes 3146504 | tf_op jit(solution)/shard_map/ppermute | solution.py:154
  60.1 23.7 %collective-permute-start.4 = (bf16[4097,128]{1,0:T(8,128)(2,1)}, bf16[4097,128]{1,0:T(8,128)(2,1)S(1)}, u32[]{:S(2)}, u32[]{:S(2)}) collective-permute-start(bf16[4097,128]{1,0:T(8,128)(2,1)} %collective-permute-done.2.refs_3_), channel_id=1, source_target_pairs={{0,32},{32,64},{64,96},{96,128},{128,160},{160,192},{192,224},{224... | collective-permute-start | bytes 3146504 | tf_op jit(solution)/shard_map/ppermute | solution.py:153
  80.3 3.7 %copy-start.2 = (bf16[4097,128]{1,0:T(8,128)(2,1)}, bf16[4097,128]{1,0:T(8,128)(2,1)S(1)}, u32[]{:S(2)}) copy-start(bf16[4097,128]{1,0:T(8,128)(2,1)S(1)} %collective-permute-done.5.refs_6_) | copy-start | bytes 3146500
  80.3 11.6 %collective-permute-start.7 = (bf16[2049,128]{1,0:T(8,128)(2,1)S(1)}, bf16[2049,128]{1,0:T(8,128)(2,1)S(1)}, u32[]{:S(2)}, u32[]{:S(2)}) collective-permute-start(bf16[2049,128]{1,0:T(8,128)(2,1)S(1)} %slice.105), channel_id=1, source_target_pairs={{0,224},{32,0},{64,32},{96,64},{128,96},{160,128},{192,160},{224,1... | collective-permute-start | bytes 1573640 | tf_op jit(solution)/shard_map/ppermute | solution.py:161
  83.8 1.0 copy-start.3
  83.9 11.3 %collective-permute-start.6 = (bf16[2049,128]{1,0:T(8,128)(2,1)S(1)}, bf16[2049,128]{1,0:T(8,128)(2,1)S(1)}, u32[]{:S(2)}, u32[]{:S(2)}) collective-permute-start(bf16[2049,128]{1,0:T(8,128)(2,1)S(1)} %pad_maximum_fusion), channel_id=1, source_target_pairs={{0,32},{32,64},{64,96},{96,128},{128,160},{160,192},{192,224},{224... | collective-permute-start | bytes 1573640 | tf_op jit(solution)/shard_map/ppermute | solution.py:160
  91.9 0.8 copy-start.6
  95.2 21.0 %copy-start.7 = (bf16[2049,128]{1,0:T(8,128)(2,1)}, bf16[2049,128]{1,0:T(8,128)(2,1)S(1)}, u32[]{:S(2)}) copy-start(bf16[2049,128]{1,0:T(8,128)(2,1)S(1)} %collective-permute-done.6.refs_7_) | copy-start | bytes 1573636
  129.7 40.1 %all-to-all-start = ((f32[64,64,128]{2,1,0:T(8,128)}), f32[64,64,128]{2,1,0:T(8,128)S(1)}, u32[]{:S(2)}, u32[]{:S(2)}) async-start(f32[64,64,128]{2,1,0:T(8,128)} %shard_map.64), calls=%async_computation | async-start | bytes 4194304 | tf_op jit(solution)/shard_map/all_to_all | solution.py:175
  169.8 1.4 copy-start

commit v6 on v5

--- a/solution.py
+++ b/solution.py
@@ -40,11 +40,15 @@
     return jnp.where(found, dest, capacity).reshape(-1)
 
 
-def project_kernel(sizes, kp, block_len, idx_ref, p_ref, *refs):
+def project_kernel(sizes, kp, block_len, face_base, has_acc, pos_ref, pat_ref, p_ref, *refs):
     n = len(sizes)
     w_refs = refs[:n]
-    o_ref, buf, sem = refs[n:]
-    o_ref[...] = jnp.zeros_like(o_ref)
+    if has_acc:
+        acc_ref, o_ref, buf, sem = refs[n:]
+        o_ref[...] = acc_ref[...]
+    else:
+        o_ref, buf, sem = refs[n:]
+        o_ref[...] = jnp.zeros_like(o_ref)
 
     def fetch(q):
         slot = q % 2
@@ -64,29 +68,34 @@
         slot = q % 2
         for g in range(sizes[q]):
             face = base + g
-            rows = p_ref[:, face * block_len:(face + 1) * block_len]
+            col = face_base + face
+            rows = p_ref[:, col * block_len:(col + 1) * block_len]
             wide = jnp.concatenate(
                 [buf[slot, (g * kp + k) * block_len:(g * kp + k + 1) * block_len, :] for k in range(kp)],
                 axis=1,
             )
             prod = jnp.dot(rows, wide, preferred_element_type=jnp.float32)
             for k in range(kp):
-                pos = idx_ref[face * kp + k]
+                pos = pos_ref[pat_ref[face * kp + k]]
                 o_ref[pos] += prod[:, k * block_len:(k + 1) * block_len]
         base += sizes[q]
 
 
-def project(idx, pressure, pieces, sizes, kp, n_pos):
+def project(positions, pat, pressure, pieces, sizes, kp, n_pos, face_base, acc):
     time_len, block_len = pressure.shape[0], pieces[0].shape[1]
     face_blocks = sum(sizes)
+    has_acc = acc is not None
+    extra = [acc] if has_acc else []
     return pl.pallas_call(
-        functools.partial(project_kernel, tuple(sizes), kp, block_len),
+        functools.partial(project_kernel, tuple(sizes), kp, block_len, face_base, has_acc),
         out_shape=jax.ShapeDtypeStruct((n_pos, time_len, block_len), jnp.float32),
         in_specs=[
             pl.BlockSpec(memory_space=pltpu.SMEM),
+            pl.BlockSpec(memory_space=pltpu.SMEM),
             pl.BlockSpec(memory_space=pltpu.VMEM),
         ]
-        + [pl.BlockSpec(memory_space=pl.ANY)] * len(pieces),
+        + [pl.BlockSpec(memory_space=pl.ANY)] * len(pieces)
+        + [pl.BlockSpec(memory_space=pltpu.VMEM)] * len(extra),
         out_specs=pl.BlockSpec(memory_space=pltpu.VMEM),
         scratch_shapes=[
             pltpu.VMEM((2, max(sizes) * kp * block_len, block_len), pieces[0].dtype),
@@ -95,10 +104,10 @@
         cost_estimate=pl.CostEstimate(
             flops=2 * face_blocks * kp * time_len * block_len * block_len,
             bytes_accessed=face_blocks * kp * block_len * block_len * 2 + pressure.size * 2
-            + n_pos * time_len * block_len * 4,
+            + (1 + len(extra)) * n_pos * time_len * block_len * 4,
             transcendentals=0,
         ),
-    )(idx, pressure, *pieces)
+    )(positions, pat, pressure, *pieces, *extra)
 
 
 def collect_kernel(n_rows, dest_ref, r_ref, o_ref, acc_ref):
@@ -165,13 +174,20 @@
     order += [(t + n_tm // 2) % n_tm]
 
     positions = send_positions(panel_list, owner_list, owner_count, own_index, slot_count)
-    pats = [x[-1, a:a + n * kp] for x, n, a in zip(pieces, sizes, lane_at)]
-    pat_all = jnp.concatenate(pats).astype(jnp.int32)
-    idx = jnp.take(positions, pat_all, axis=0)
     time_len = pressure.shape[0]
     blocks = pressure.reshape(time_len, n_tm, fb_dev * block_len)
     ordered = jnp.take(blocks, jnp.stack(order), axis=1).reshape(time_len, -1)
-    packed = project(idx, ordered, pieces, sizes, kp, n_pos)
+
+    def pattern_of(group):
+        rows = [pieces[i][-1, lane_at[i]:lane_at[i] + sizes[i] * kp] for i in group]
+        return jnp.concatenate(rows).astype(jnp.int32)
+
+    full = list(range(len(pieces) - 2))
+    tail = [len(pieces) - 2, len(pieces) - 1]
+    packed = project(positions, pattern_of(full), ordered, [pieces[i] for i in full],
+                     [sizes[i] for i in full], kp, n_pos, 0, None)
+    packed = project(positions, pattern_of(tail), ordered, [pieces[i] for i in tail],
+                     [sizes[i] for i in tail], kp, n_pos, sum(sizes[i] for i in full), packed)
     received = lax.all_to_all(packed, "owner", split_axis=0, concat_axis=0, tiled=True)
     dest = receive_slots(panel_list, owner_list, owner_count, own_index, slot_count)
     return collect(dest, received, capacity)

time: 175 us -> 150 us (0.86)
  other arithmetic: 29.5 us -> 11.4 us
  waiting for transfers between devices: 89.4 us -> 84.4 us
  Pallas kernels: 16.8 us -> 20.3 us
  local copies, waits for them, and re-layouts: 10.1 us -> 7.05 us
  starting transfers between devices: 28.3 us -> 25.3 us
    ppermute x3, waiting for transfers between devices: 0.01 us -> 60.3 us  [body(): x_r = lax.ppermute(x_r, 'tm', right)]
    ppermute x3, waiting for transfers between devices: 55.7 us -> 0.01 us  [body(): x_l = lax.ppermute(x_l, 'tm', left)]
    select_n x1 -> x0, other arithmetic: 16.2 us -> none  [body(): idx = jnp.take(positions, pat_all, axis=0)]
    ppermute x1, waiting for transfers between devices: 7.08 us -> 0.01 us  [body(): h_l = lax.ppermute(x_l[h_rows:], 'tm', left)]
    gather x2 -> x0, other arithmetic: 4.6 us -> none  [body(): idx = jnp.take(positions, pat_all, axis=0)]
    ppermute x3, starting transfers between devices: 13.3 us -> 9.38 us  [body(): x_l = lax.ppermute(x_l, 'tm', left)]
    pallas_call x1 -> x2, Pallas kernels: 13.5 us -> 17.1 us  [project(): pl.pallas_call(functools.partial(project_kernel, tuple(sizes), kp, block_...]
    squeeze x3 -> x11, local copies, waits for them, and re-layouts: 0.27 us -> 3.02 us  [pattern_of(): rows = [pieces[i][-1, lane_at[i]:lane_at[i] + sizes[i] * kp] for i in group]]
  transfers between devices with their start and end apart: 9 -> 9, of which waited for: 6 -> 4; matrix products, arithmetic and copies ran while one was open for 7% -> 9% of each run, Pallas kernels for 0% -> 8%
where the time goes in v6:
time: 150 us; the launch traced here: 149 us
  waiting for transfers between devices  84.4 us (56%)
  starting transfers between devices  25.3 us (17%)
  Pallas kernels  20.3 us (14%)
  other arithmetic  11.4 us (8%)
  local copies, waits for them, and re-layouts  7.05 us (5%)
    ppermute x3, waiting for transfers between devices, body(): x_r = lax.ppermute(x_r, 'tm', right)  60.3 us
    all_to_all x1, waiting for transfers between devices, body(): lax.all_to_all(packed, 'owner', split_axis=0, concat_axis=0, tiled=True)  24.1 us
    pallas_call x2, Pallas kernels, project(): pl.pallas_call(functools.partial(project_kernel, tuple(sizes), kp, block_...  17.1 us
    all_to_all x1, starting transfers between devices, body(): lax.all_to_all(packed, 'owner', split_axis=0, concat_axis=0, tiled=True)  10.6 us
    ppermute x3, starting transfers between devices, body(): x_l = lax.ppermute(x_l, 'tm', left)  9.38 us
    pallas_call x1, Pallas kernels, collect(): pl.pallas_call(functools.partial(collect_kernel, n_rows), out_shape=jax.S...  3.27 us
    squeeze x11, local copies, waits for them, and re-layouts, pattern_of(): rows = [pieces[i][-1, lane_at[i]:lane_at[i] + sizes[i] * kp] for i in group]  3.02 us
  transfers between devices with their start and end apart: 9, of which 4 were waited for; matrix products, arithmetic and copies ran while one was open for 9% of the time, Pallas kernels for 8%

profile of v6, /device:TPU:1, one launch (start us, length us, event | category | flops | bytes accessed | tf_op | source)
XLA Modules:
  0.0 148.8 jit_solution(8144967783298731553)
XLA Ops:
  0.0 0.6 compare_reduce_fusion
  0.6 1.3 convert_select_fusion
  2.0 0.1 copy.17
  2.1 0.1 squeeze.36
  2.2 1.4 fusion.1.refs_0_
  3.6 2.5 %collective-permute-start = (bf16[4097,128]{1,0:T(8,128)(2,1)S(1)}, bf16[4097,128]{1,0:T(8,128)(2,1)}, u32[]{:S(2)}, u32[]{:S(2)}) collective-permute-start(bf16[4097,128]{1,0:T(8,128)(2,1)S(1)} %fusion.1.refs_0_), channel_id=1, source_target_pairs={{0,32},{32,64},{64,96},{96,128},{128,160},{160,192},{192,224},{224... | collective-permute-start | bytes 3146504 | tf_op jit(solution)/shard_map/ppermute | solution.py:162
  6.1 4.0 %collective-permute-start.4 = (bf16[4097,128]{1,0:T(8,128)(2,1)S(1)}, bf16[4097,128]{1,0:T(8,128)(2,1)}, u32[]{:S(2)}, u32[]{:S(2)}) collective-permute-start(bf16[4097,128]{1,0:T(8,128)(2,1)S(1)} %fusion.1.refs_0_), channel_id=1, source_target_pairs={{0,224},{32,0},{64,32},{96,64},{128,96},{160,128},{192,160},{224,1... | collective-permute-start | bytes 3146504 | tf_op jit(solution)/shard_map/ppermute | solution.py:163
  10.1 0.1 copy.26
  10.3 0.1 stack.62
  10.4 0.6 gather_fusion
  11.0 0.1 copy.22
  11.1 0.1 stack.53
  11.3 21.7 %collective-permute-done.refs_1_ = bf16[4097,128]{1,0:T(8,128)(2,1)} collective-permute-done((bf16[4097,128]{1,0:T(8,128)(2,1)S(1)}, bf16[4097,128]{1,0:T(8,128)(2,1)}, u32[]{:S(2)}, u32[]{:S(2)}) %collective-permute-start) | collective-permute-done | bytes 1048864 | tf_op jit(solution)/shard_map/ppermute | solution.py:162
  33.1 2.7 %collective-permute-start.5 = (bf16[4097,128]{1,0:T(8,128)(2,1)}, bf16[4097,128]{1,0:T(8,128)(2,1)}, u32[]{:S(2)}, u32[]{:S(2)}) collective-permute-start(bf16[4097,128]{1,0:T(8,128)(2,1)} %collective-permute-done.4.refs_2_), channel_id=1, source_target_pairs={{0,224},{32,0},{64,32},{96,64},{128,96},{160,128},{192,160},{224,1... | collective-permute-start | bytes 3146504 | tf_op jit(solution)/shard_map/ppermute | solution.py:163
  35.7 1.2 broadcast_select_fusion.p_ref
  37.0 0.7 and_reduce_fusion
  37.7 20.3 %collective-permute-done.1.refs_3_ = bf16[4097,128]{1,0:T(8,128)(2,1)S(1)} collective-permute-done((bf16[4097,128]{1,0:T(8,128)(2,1)}, bf16[4097,128]{1,0:T(8,128)(2,1)S(1)}, u32[]{:S(2)}, u32[]{:S(2)}) %collective-permute-start.1) | collective-permute-done | bytes 1048864 | tf_op jit(solution)/shard_map/ppermute | solution.py:162
  58.0 0.1 select_reduce_fusion.2
  58.1 0.1 squeeze.39
  58.2 0.2 convert_reduce_fusion.1
  58.4 0.5 multiply_add_fusion.pos_ref
  58.9 2.7 %collective-permute-start.6 = (bf16[4097,128]{1,0:T(8,128)(2,1)}, bf16[4097,128]{1,0:T(8,128)(2,1)S(1)}, u32[]{:S(2)}, u32[]{:S(2)}) collective-permute-start(bf16[4097,128]{1,0:T(8,128)(2,1)} %collective-permute-done.5.refs_4_), channel_id=1, source_target_pairs={{0,224},{32,0},{64,32},{96,64},{128,96},{160,128},{192,160},{224,1... | collective-permute-start | bytes 3146504 | tf_op jit(solution)/shard_map/ppermute | solution.py:163
  61.6 0.7 slice_bitcast_fusion.4
  62.2 0.7 slice_bitcast_fusion.5
  62.9 0.7 slice_bitcast_fusion.2
  63.6 18.3 %collective-permute-done.2.refs_5_ = bf16[4097,128]{1,0:T(8,128)(2,1)S(1)} collective-permute-done((bf16[4097,128]{1,0:T(8,128)(2,1)S(1)}, bf16[4097,128]{1,0:T(8,128)(2,1)S(1)}, u32[]{:S(2)}, u32[]{:S(2)}) %collective-permute-start.2) | collective-permute-done | bytes 1048864 | tf_op jit(solution)/shard_map/ppermute | solution.py:162
  81.9 0.9 pad_maximum_fusion
  82.9 2.7 %collective-permute-start.7 = (bf16[2049,128]{1,0:T(8,128)(2,1)S(1)}, bf16[2049,128]{1,0:T(8,128)(2,1)S(1)}, u32[]{:S(2)}, u32[]{:S(2)}) collective-permute-start(bf16[2049,128]{1,0:T(8,128)(2,1)S(1)} %slice.66), channel_id=1, source_target_pairs={{0,224},{32,0},{64,32},{96,64},{128,96},{160,128},{192,160},{224,1... | collective-permute-start | bytes 1573640 | tf_op jit(solution)/shard_map/ppermute | solution.py:170
  85.6 0.1 concatenate.38
  85.7 0.6 convert_element_type.26.pat_ref
  86.3 11.5 %shard_map.64.refs_2_ = f32[64,64,128]{2,1,0:T(8,128)} custom-call(s32[32]{0:T(128)} %multiply_add_fusion.pos_ref, s32[224]{0:T(256)} %convert_element_type.26.pat_ref, bf16[64,8192]{1,0:T(8,128)(2,1)} %broadcast_select_fusion.p_ref, bf16[4097,128]{1,0:T(8,128)(2,1)} %copy-done.1, bf16[4097,128]{1,0:T(8,128)(2,1)} %collective-permute-done.refs_1_, ...), custom_call_target="tpu_custom_call" | custom-call | flops 469762048 | bytes 10485760 | tf_op jit(solution)/shard_map/pallas_call | solution.py:89
  97.9 0.7 slice_bitcast_fusion.7
  98.6 0.6 maximum_convert_fusion.pat_ref
  99.3 0.1 copy-done.6
  99.3 5.6 %shard_map.65 = f32[64,64,128]{2,1,0:T(8,128)} custom-call(s32[32]{0:T(128)} %multiply_add_fusion.pos_ref, s32[32]{0:T(128)} %maximum_convert_fusion.pat_ref, bf16[64,8192]{1,0:T(8,128)(2,1)} %broadcast_select_fusion.p_ref, bf16[2049,128]{1,0:T(8,128)(2,1)} %collective-permute-done.3.refs_0_, bf16[2049,128]{1,0:T(8,128)(2,1)} %copy-done.6, ...), custom_call_target="tpu_custom_call" | custom-call | flops 67108864 | bytes 6291456 | tf_op jit(solution)/shard_map/pallas_call | solution.py:89
  104.9 10.6 %all-to-all-start = ((f32[64,64,128]{2,1,0:T(8,128)}), f32[64,64,128]{2,1,0:T(8,128)S(1)}, u32[]{:S(2)}, u32[]{:S(2)}) async-start(f32[64,64,128]{2,1,0:T(8,128)} %shard_map.65), calls=%async_computation | async-start | bytes 4194304 | tf_op jit(solution)/shard_map/all_to_all | solution.py:191
  115.5 0.6 dynamic_slice.10
  116.1 0.6 iota_compare_fusion.4
  116.8 0.8 fusion.2
  117.6 0.6 convert_reduce_fusion
  118.2 0.1 fusion.4
  118.3 0.8 select_reduce_fusion
  119.1 0.1 select_reduce_fusion.1
  119.3 0.1 copy.16
  119.4 0.6 select_n.81.dest_ref
  120.0 24.1 %all-to-all-done.r_ref = f32[64,64,128]{2,1,0:T(8,128)S(1)} async-done(((f32[64,64,128]{2,1,0:T(8,128)}), f32[64,64,128]{2,1,0:T(8,128)S(1)}, u32[]{:S(2)}, u32[]{:S(2)}) %all-to-all-start) | async-done | bytes 2097184 | tf_op jit(solution)/shard_map/all_to_all | solution.py:191
  144.1 1.3 copy-done
  145.5 3.3 %shard_map.66 = f32[36,64,128]{2,1,0:T(8,128)} custom-call(s32[64]{0:T(128)} %select_n.81.dest_ref, f32[64,64,128]{2,1,0:T(8,128)} %copy-done), custom_call_target="tpu_custom_call" | custom-call | tf_op jit(solution)/shard_map/pallas_call | solution.py:127
  (43 shorter events, 0.4 us)
Async XLA Ops:
  2.2 8.0 %copy-start.5 = (bf16[64,8192]{1,0:T(8,128)(2,1)S(1)}, bf16[64,8192]{1,0:T(8,128)(2,1)}, u32[]{:S(2)}) copy-start(bf16[64,8192]{1,0:T(8,128)(2,1)} %param.8) | copy-start | bytes 3145732
  3.5 6.7 %copy-start.1 = (bf16[4097,128]{1,0:T(8,128)(2,1)}, bf16[4097,128]{1,0:T(8,128)(2,1)S(1)}, u32[]{:S(2)}) copy-start(bf16[4097,128]{1,0:T(8,128)(2,1)S(1)} %fusion.1.refs_0_) | copy-start | bytes 3146500
  3.6 29.5 %collective-permute-start = (bf16[4097,128]{1,0:T(8,128)(2,1)S(1)}, bf16[4097,128]{1,0:T(8,128)(2,1)}, u32[]{:S(2)}, u32[]{:S(2)}) collective-permute-start(bf16[4097,128]{1,0:T(8,128)(2,1)S(1)} %fusion.1.refs_0_), channel_id=1, source_target_pairs={{0,32},{32,64},{64,96},{96,128},{128,160},{160,192},{192,224},{224... | collective-permute-start | bytes 3146504 | tf_op jit(solution)/shard_map/ppermute | solution.py:162
  6.1 27.0 %collective-permute-start.4 = (bf16[4097,128]{1,0:T(8,128)(2,1)S(1)}, bf16[4097,128]{1,0:T(8,128)(2,1)}, u32[]{:S(2)}, u32[]{:S(2)}) collective-permute-start(bf16[4097,128]{1,0:T(8,128)(2,1)S(1)} %fusion.1.refs_0_), channel_id=1, source_target_pairs={{0,224},{32,0},{64,32},{96,64},{128,96},{160,128},{192,160},{224,1... | collective-permute-start | bytes 3146504 | tf_op jit(solution)/shard_map/ppermute | solution.py:163
  33.0 24.9 %collective-permute-start.1 = (bf16[4097,128]{1,0:T(8,128)(2,1)}, bf16[4097,128]{1,0:T(8,128)(2,1)S(1)}, u32[]{:S(2)}, u32[]{:S(2)}) collective-permute-start(bf16[4097,128]{1,0:T(8,128)(2,1)} %collective-permute-done.refs_1_), channel_id=1, source_target_pairs={{0,32},{32,64},{64,96},{96,128},{128,160},{160,192},{192,224},{224... | collective-permute-start | bytes 3146504 | tf_op jit(solution)/shard_map/ppermute | solution.py:162
  33.1 25.9 %collective-permute-start.5 = (bf16[4097,128]{1,0:T(8,128)(2,1)}, bf16[4097,128]{1,0:T(8,128)(2,1)}, u32[]{:S(2)}, u32[]{:S(2)}) collective-permute-start(bf16[4097,128]{1,0:T(8,128)(2,1)} %collective-permute-done.4.refs_2_), channel_id=1, source_target_pairs={{0,224},{32,0},{64,32},{96,64},{128,96},{160,128},{192,160},{224,1... | collective-permute-start | bytes 3146504 | tf_op jit(solution)/shard_map/ppermute | solution.py:163
  35.7 1.2 copy-start.7
  35.7 1.2 copy-start.9
  35.7 1.3 copy-start.8
  58.0 24.9 %copy-start.4 = (bf16[4097,128]{1,0:T(8,128)(2,1)}, bf16[4097,128]{1,0:T(8,128)(2,1)S(1)}, u32[]{:S(2)}) copy-start(bf16[4097,128]{1,0:T(8,128)(2,1)S(1)} %collective-permute-done.1.refs_3_) | copy-start | bytes 3146500
  58.0 23.9 %collective-permute-start.2 = (bf16[4097,128]{1,0:T(8,128)(2,1)S(1)}, bf16[4097,128]{1,0:T(8,128)(2,1)S(1)}, u32[]{:S(2)}, u32[]{:S(2)}) collective-permute-start(bf16[4097,128]{1,0:T(8,128)(2,1)S(1)} %collective-permute-done.1.refs_3_), channel_id=1, source_target_pairs={{0,32},{32,64},{64,96},{96,128},{128,160},{160,192},{192,224},{224... | collective-permute-start | bytes 3146504 | tf_op jit(solution)/shard_map/ppermute | solution.py:162
  58.9 23.9 %collective-permute-start.6 = (bf16[4097,128]{1,0:T(8,128)(2,1)}, bf16[4097,128]{1,0:T(8,128)(2,1)S(1)}, u32[]{:S(2)}, u32[]{:S(2)}) collective-permute-start(bf16[4097,128]{1,0:T(8,128)(2,1)} %collective-permute-done.5.refs_4_), channel_id=1, source_target_pairs={{0,224},{32,0},{64,32},{96,64},{128,96},{160,128},{192,160},{224,1... | collective-permute-start | bytes 3146504 | tf_op jit(solution)/shard_map/ppermute | solution.py:163
  81.8 3.8 %copy-start.3 = (bf16[4097,128]{1,0:T(8,128)(2,1)}, bf16[4097,128]{1,0:T(8,128)(2,1)S(1)}, u32[]{:S(2)}) copy-start(bf16[4097,128]{1,0:T(8,128)(2,1)S(1)} %collective-permute-done.2.refs_5_) | copy-start | bytes 3146500
  82.8 15.0 %collective-permute-start.3 = (bf16[2049,128]{1,0:T(8,128)(2,1)}, bf16[2049,128]{1,0:T(8,128)(2,1)}, u32[]{:S(2)}, u32[]{:S(2)}) collective-permute-start(bf16[2049,128]{1,0:T(8,128)(2,1)} %pad_maximum_fusion), channel_id=1, source_target_pairs={{0,32},{32,64},{64,96},{96,128},{128,160},{160,192},{192,224},{224... | collective-permute-start | bytes 1573640 | tf_op jit(solution)/shard_map/ppermute | solution.py:169
  82.8 3.5 %copy-start.2 = (bf16[4097,128]{1,0:T(8,128)(2,1)}, bf16[4097,128]{1,0:T(8,128)(2,1)S(1)}, u32[]{:S(2)}) copy-start(bf16[4097,128]{1,0:T(8,128)(2,1)S(1)} %collective-permute-done.6.refs_6_) | copy-start | bytes 3146500
  82.9 15.7 %collective-permute-start.7 = (bf16[2049,128]{1,0:T(8,128)(2,1)S(1)}, bf16[2049,128]{1,0:T(8,128)(2,1)S(1)}, u32[]{:S(2)}, u32[]{:S(2)}) collective-permute-start(bf16[2049,128]{1,0:T(8,128)(2,1)S(1)} %slice.66), channel_id=1, source_target_pairs={{0,224},{32,0},{64,32},{96,64},{128,96},{160,128},{192,160},{224,1... | collective-permute-start | bytes 1573640 | tf_op jit(solution)/shard_map/ppermute | solution.py:170
  98.5 0.8 copy-start.6
  104.9 39.2 %all-to-all-start = ((f32[64,64,128]{2,1,0:T(8,128)}), f32[64,64,128]{2,1,0:T(8,128)S(1)}, u32[]{:S(2)}, u32[]{:S(2)}) async-start(f32[64,64,128]{2,1,0:T(8,128)} %shard_map.65), calls=%async_computation | async-start | bytes 4194304 | tf_op jit(solution)/shard_map/all_to_all | solution.py:191
  144.1 1.4 copy-start

commit v7 on v6

--- a/solution.py
+++ b/solution.py
@@ -110,16 +110,20 @@
     )(positions, pat, pressure, *pieces, *extra)
 
 
-def collect_kernel(n_rows, dest_ref, r_ref, o_ref, acc_ref):
-    acc_ref[...] = jnp.zeros_like(acc_ref)
+def collect_kernel(n_rows, dest_ref, r_ref, o_ref):
+    o_ref[...] = jnp.zeros_like(o_ref)
+    capacity = o_ref.shape[0]
 
     def add_row(e, carry):
         d = dest_ref[e]
-        acc_ref[d] += r_ref[e]
+
+        @pl.when(d < capacity)
+        def _():
+            o_ref[d] += r_ref[e]
+
         return carry
 
     lax.fori_loop(0, n_rows, add_row, 0)
-    o_ref[...] = acc_ref[: o_ref.shape[0]]
 
 
 def collect(dest, received, capacity):
@@ -132,7 +136,6 @@
             pl.BlockSpec(memory_space=pltpu.VMEM),
         ],
         out_specs=pl.BlockSpec(memory_space=pltpu.VMEM),
-        scratch_shapes=[pltpu.VMEM((capacity + 1, time_len, block_len), jnp.float32)],
     )(dest, received)
 
 
@@ -184,10 +187,11 @@
 
     full = list(range(len(pieces) - 2))
     tail = [len(pieces) - 2, len(pieces) - 1]
-    packed = project(positions, pattern_of(full), ordered, [pieces[i] for i in full],
+    split = sum(sizes[i] for i in full) * block_len
+    packed = project(positions, pattern_of(full), ordered[:, :split], [pieces[i] for i in full],
                      [sizes[i] for i in full], kp, n_pos, 0, None)
-    packed = project(positions, pattern_of(tail), ordered, [pieces[i] for i in tail],
-                     [sizes[i] for i in tail], kp, n_pos, sum(sizes[i] for i in full), packed)
+    packed = project(positions, pattern_of(tail), ordered[:, split:], [pieces[i] for i in tail],
+                     [sizes[i] for i in tail], kp, n_pos, 0, packed)
     received = lax.all_to_all(packed, "owner", split_axis=0, concat_axis=0, tiled=True)
     dest = receive_slots(panel_list, owner_list, owner_count, own_index, slot_count)
     return collect(dest, received, capacity)

time: 150 us -> 150 us (level)
  waiting for transfers between devices: 84.4 us -> 80.8 us
  local copies, waits for them, and re-layouts: 7.05 us -> 9.75 us
  starting transfers between devices: 25.3 us -> 27.3 us
    ppermute x3, waiting for transfers between devices: 60.3 us -> 0.01 us  [body(): x_r = lax.ppermute(x_r, 'tm', right)]
    ppermute x3, waiting for transfers between devices: 0.01 us -> 56.7 us  [body(): x_l = lax.ppermute(x_l, 'tm', left)]
    ppermute x3, starting transfers between devices: 9.38 us -> 13.3 us  [body(): x_l = lax.ppermute(x_l, 'tm', left)]
    ppermute x3, starting transfers between devices: 2.54 us -> 0.01 us  [body(): x_r = lax.ppermute(x_r, 'tm', right)]
    slice x0 -> x2, local copies, waits for them, and re-layouts: none -> 1.72 us  [the longest x1 1.06 us: body(): ordered[:, :split]]
  transfers between devices with their start and end apart: 9 -> 9, of which waited for: 4 -> 4; matrix products, arithmetic and copies ran while one was open for 9% -> 10% of each run, Pallas kernels for 8% -> 8%
where the time goes in v7:
time: 150 us; the launch traced here: 149 us
  waiting for transfers between devices  80.8 us (54%)
  starting transfers between devices  27.3 us (18%)
  Pallas kernels  20.4 us (14%)
  other arithmetic  10.5 us (7%)
  local copies, waits for them, and re-layouts  9.75 us (6%)
    ppermute x3, waiting for transfers between devices, body(): x_l = lax.ppermute(x_l, 'tm', left)  56.7 us
    all_to_all x1, waiting for transfers between devices, body(): lax.all_to_all(packed, 'owner', split_axis=0, concat_axis=0, tiled=True)  24.1 us
    pallas_call x2, Pallas kernels, project(): pl.pallas_call(functools.partial(project_kernel, tuple(sizes), kp, block_...  16.8 us
    ppermute x3, starting transfers between devices, body(): x_l = lax.ppermute(x_l, 'tm', left)  13.3 us
    all_to_all x1, starting transfers between devices, body(): lax.all_to_all(packed, 'owner', split_axis=0, concat_axis=0, tiled=True)  10.6 us
    pallas_call x1, Pallas kernels, collect(): pl.pallas_call(functools.partial(collect_kernel, n_rows), out_shape=jax.S...  3.65 us
    ppermute x1, starting transfers between devices, body(): h_l = lax.ppermute(x_l[h_rows:], 'tm', left)  3.41 us
    squeeze x11, local copies, waits for them, and re-layouts, pattern_of(): rows = [pieces[i][-1, lane_at[i]:lane_at[i] + sizes[i] * kp] for i in group]  3.03 us
  transfers between devices with their start and end apart: 9, of which 4 were waited for; matrix products, arithmetic and copies ran while one was open for 10% of the time, Pallas kernels for 8%

profile of v7, /device:TPU:1, one launch (start us, length us, event | category | flops | bytes accessed | tf_op | source)
XLA Modules:
  0.0 149.0 jit_solution(11449920034519732721)
XLA Ops:
  0.0 0.6 compare_reduce_fusion
  0.6 1.3 convert_select_fusion
  2.0 0.1 copy.17
  2.1 0.1 squeeze.36
  2.2 1.4 fusion.1.refs_0_
  3.6 6.5 %collective-permute-start.4 = (bf16[4097,128]{1,0:T(8,128)(2,1)S(1)}, bf16[4097,128]{1,0:T(8,128)(2,1)}, u32[]{:S(2)}, u32[]{:S(2)}) collective-permute-start(bf16[4097,128]{1,0:T(8,128)(2,1)S(1)} %fusion.1.refs_0_), channel_id=1, source_target_pairs={{0,224},{32,0},{64,32},{96,64},{128,96},{160,128},{192,160},{224,1... | collective-permute-start | bytes 3146504 | tf_op jit(solution)/shard_map/ppermute | solution.py:166
  10.2 0.1 copy.26
  10.3 0.1 stack.62
  10.5 0.6 gather_fusion
  11.2 20.7 %collective-permute-done.4.refs_2_ = bf16[4097,128]{1,0:T(8,128)(2,1)} collective-permute-done((bf16[4097,128]{1,0:T(8,128)(2,1)S(1)}, bf16[4097,128]{1,0:T(8,128)(2,1)}, u32[]{:S(2)}, u32[]{:S(2)}) %collective-permute-start.4) | collective-permute-done | bytes 1048864 | tf_op jit(solution)/shard_map/ppermute | solution.py:166
  31.9 3.5 %collective-permute-start.5 = (bf16[4097,128]{1,0:T(8,128)(2,1)}, bf16[4097,128]{1,0:T(8,128)(2,1)S(1)}, u32[]{:S(2)}, u32[]{:S(2)}) collective-permute-start(bf16[4097,128]{1,0:T(8,128)(2,1)} %collective-permute-done.4.refs_2_), channel_id=1, source_target_pairs={{0,224},{32,0},{64,32},{96,64},{128,96},{160,128},{192,160},{224,1... | collective-permute-start | bytes 3146504 | tf_op jit(solution)/shard_map/ppermute | solution.py:166
  35.4 0.1 broadcast_select_fusion
  35.6 0.1 squeeze.39
  35.7 0.7 slice.76.p_ref
  36.3 1.1 slice.83.p_ref
  37.5 0.7 and_reduce_fusion
  38.2 0.1 select_reduce_fusion.2
  38.3 0.2 convert_reduce_fusion.1
  38.5 18.3 %collective-permute-done.5.refs_4_ = bf16[4097,128]{1,0:T(8,128)(2,1)S(1)} collective-permute-done((bf16[4097,128]{1,0:T(8,128)(2,1)}, bf16[4097,128]{1,0:T(8,128)(2,1)S(1)}, u32[]{:S(2)}, u32[]{:S(2)}) %collective-permute-start.5) | collective-permute-done | bytes 1048864 | tf_op jit(solution)/shard_map/ppermute | solution.py:166
  56.8 3.3 %collective-permute-start.6 = (bf16[4097,128]{1,0:T(8,128)(2,1)S(1)}, bf16[4097,128]{1,0:T(8,128)(2,1)S(1)}, u32[]{:S(2)}, u32[]{:S(2)}) collective-permute-start(bf16[4097,128]{1,0:T(8,128)(2,1)S(1)} %collective-permute-done.5.refs_4_), channel_id=1, source_target_pairs={{0,224},{32,0},{64,32},{96,64},{128,96},{160,128},{192,160},{224,1... | collective-permute-start | bytes 3146504 | tf_op jit(solution)/shard_map/ppermute | solution.py:166
  60.1 0.5 multiply_add_fusion.pos_ref
  60.6 0.7 slice_bitcast_fusion.4
  61.3 0.7 slice_bitcast_fusion.5
  62.0 0.7 slice_bitcast_fusion.3
  62.6 17.6 %collective-permute-done.6.refs_6_ = bf16[4097,128]{1,0:T(8,128)(2,1)S(1)} collective-permute-done((bf16[4097,128]{1,0:T(8,128)(2,1)S(1)}, bf16[4097,128]{1,0:T(8,128)(2,1)S(1)}, u32[]{:S(2)}, u32[]{:S(2)}) %collective-permute-start.6) | collective-permute-done | bytes 1048864 | tf_op jit(solution)/shard_map/ppermute | solution.py:166
  80.3 0.9 slice.74
  81.2 3.4 %collective-permute-start.7 = (bf16[2049,128]{1,0:T(8,128)(2,1)}, bf16[2049,128]{1,0:T(8,128)(2,1)}, u32[]{:S(2)}, u32[]{:S(2)}) collective-permute-start(bf16[2049,128]{1,0:T(8,128)(2,1)} %slice.74), channel_id=1, source_target_pairs={{0,224},{32,0},{64,32},{96,64},{128,96},{160,128},{192,160},{224,1... | collective-permute-start | bytes 1573640 | tf_op jit(solution)/shard_map/ppermute | solution.py:173
  84.6 1.0 pad_maximum_fusion
  85.6 0.2 copy-done.3
  85.8 0.1 concatenate.38
  85.9 0.6 convert_element_type.26.pat_ref
  86.4 11.5 %shard_map.64.refs_2_ = f32[64,64,128]{2,1,0:T(8,128)} custom-call(s32[32]{0:T(128)} %multiply_add_fusion.pos_ref, s32[224]{0:T(256)} %convert_element_type.26.pat_ref, bf16[64,7168]{1,0:T(8,128)(2,1)} %slice.83.p_ref, bf16[4097,128]{1,0:T(8,128)(2,1)} %copy-done.1, bf16[4097,128]{1,0:T(8,128)(2,1)} %collective-permute-done.refs_1_, ...), custom_call_target="tpu_custom_call" | custom-call | flops 469762048 | bytes 10354688 | tf_op jit(solution)/shard_map/pallas_call | solution.py:89
  97.9 0.7 slice_bitcast_fusion.6
  98.7 0.8 maximum_convert_fusion.pat_ref
  99.5 5.3 %shard_map.65 = f32[64,64,128]{2,1,0:T(8,128)} custom-call(s32[32]{0:T(128)} %multiply_add_fusion.pos_ref, s32[32]{0:T(128)} %maximum_convert_fusion.pat_ref, bf16[64,1024]{1,0:T(8,128)(2,1)} %slice.76.p_ref, bf16[2049,128]{1,0:T(8,128)(2,1)} %copy-done.6, bf16[2049,128]{1,0:T(8,128)(2,1)} %collective-permute-done.7.refs_1_, f32[64,64,128]{2,1,0:T(8,128)} %shard_map.64.refs_2_), custom_call_target="tpu_custom_call" | custom-call | flops 67108864 | bytes 5373952 | tf_op jit(solution)/shard_map/pallas_call | solution.py:89
  104.8 10.6 %all-to-all-start = ((f32[64,64,128]{2,1,0:T(8,128)}), f32[64,64,128]{2,1,0:T(8,128)S(1)}, u32[]{:S(2)}, u32[]{:S(2)}) async-start(f32[64,64,128]{2,1,0:T(8,128)} %shard_map.65), calls=%async_computation | async-start | bytes 4194304 | tf_op jit(solution)/shard_map/all_to_all | solution.py:195
  115.4 0.6 dynamic_slice.10
  116.0 0.6 iota_compare_fusion.4
  116.7 0.8 fusion.2
  117.5 0.6 convert_reduce_fusion
  118.1 0.1 fusion.4
  118.2 0.8 select_reduce_fusion
  119.0 0.1 select_reduce_fusion.1
  119.1 0.1 copy.16
  119.2 0.6 select_n.81.dest_ref
  119.9 24.1 %all-to-all-done.r_ref = f32[64,64,128]{2,1,0:T(8,128)S(1)} async-done(((f32[64,64,128]{2,1,0:T(8,128)}), f32[64,64,128]{2,1,0:T(8,128)S(1)}, u32[]{:S(2)}, u32[]{:S(2)}) %all-to-all-start) | async-done | bytes 2097184 | tf_op jit(solution)/shard_map/all_to_all | solution.py:195
  144.0 1.3 copy-done
  145.4 3.7 %shard_map.66 = f32[36,64,128]{2,1,0:T(8,128)} custom-call(s32[64]{0:T(128)} %select_n.81.dest_ref, f32[64,64,128]{2,1,0:T(8,128)} %copy-done), custom_call_target="tpu_custom_call" | custom-call | tf_op jit(solution)/shard_map/pallas_call | solution.py:131
  (45 shorter events, 0.5 us)
Async XLA Ops:
  2.2 8.1 %copy-start.5 = (bf16[64,8192]{1,0:T(8,128)(2,1)S(1)}, bf16[64,8192]{1,0:T(8,128)(2,1)}, u32[]{:S(2)}) copy-start(bf16[64,8192]{1,0:T(8,128)(2,1)} %param.8) | copy-start | bytes 3145732
  3.5 6.8 %copy-start.1 = (bf16[4097,128]{1,0:T(8,128)(2,1)}, bf16[4097,128]{1,0:T(8,128)(2,1)S(1)}, u32[]{:S(2)}) copy-start(bf16[4097,128]{1,0:T(8,128)(2,1)S(1)} %fusion.1.refs_0_) | copy-start | bytes 3146500
  3.6 28.4 %collective-permute-start.4 = (bf16[4097,128]{1,0:T(8,128)(2,1)S(1)}, bf16[4097,128]{1,0:T(8,128)(2,1)}, u32[]{:S(2)}, u32[]{:S(2)}) collective-permute-start(bf16[4097,128]{1,0:T(8,128)(2,1)S(1)} %fusion.1.refs_0_), channel_id=1, source_target_pairs={{0,224},{32,0},{64,32},{96,64},{128,96},{160,128},{192,160},{224,1... | collective-permute-start | bytes 3146504 | tf_op jit(solution)/shard_map/ppermute | solution.py:166
  10.0 25.4 %collective-permute-start = (bf16[4097,128]{1,0:T(8,128)(2,1)S(1)}, bf16[4097,128]{1,0:T(8,128)(2,1)}, u32[]{:S(2)}, u32[]{:S(2)}) collective-permute-start(bf16[4097,128]{1,0:T(8,128)(2,1)S(1)} %fusion.1.refs_0_), channel_id=1, source_target_pairs={{0,32},{32,64},{64,96},{96,128},{128,160},{160,192},{192,224},{224... | collective-permute-start | bytes 3146504 | tf_op jit(solution)/shard_map/ppermute | solution.py:165
  31.9 24.9 %collective-permute-start.5 = (bf16[4097,128]{1,0:T(8,128)(2,1)}, bf16[4097,128]{1,0:T(8,128)(2,1)S(1)}, u32[]{:S(2)}, u32[]{:S(2)}) collective-permute-start(bf16[4097,128]{1,0:T(8,128)(2,1)} %collective-permute-done.4.refs_2_), channel_id=1, source_target_pairs={{0,224},{32,0},{64,32},{96,64},{128,96},{160,128},{192,160},{224,1... | collective-permute-start | bytes 3146504 | tf_op jit(solution)/shard_map/ppermute | solution.py:166
  35.4 24.7 %collective-permute-start.1 = (bf16[4097,128]{1,0:T(8,128)(2,1)}, bf16[4097,128]{1,0:T(8,128)(2,1)}, u32[]{:S(2)}, u32[]{:S(2)}) collective-permute-start(bf16[4097,128]{1,0:T(8,128)(2,1)} %collective-permute-done.refs_1_), channel_id=1, source_target_pairs={{0,32},{32,64},{64,96},{96,128},{128,160},{160,192},{192,224},{224... | collective-permute-start | bytes 3146504 | tf_op jit(solution)/shard_map/ppermute | solution.py:165
  35.7 1.7 %copy-start.7 = (s32[32,32]{1,0:T(8,128)S(1)}, s32[32,32]{1,0:T(8,128)}, u32[]{:S(2)}) copy-start(s32[32,32]{1,0:T(8,128)} %param.11) | copy-start | bytes 12292
  35.7 1.8 %copy-start.9 = (s32[32]{0:T(128)S(1)}, s32[32]{0:T(128)}, u32[]{:S(2)}) copy-start(s32[32]{0:T(128)} %param.13) | copy-start | bytes 388
  35.7 1.8 %copy-start.8 = (s32[32,36]{1,0:T(8,128)S(1)}, s32[32,36]{1,0:T(8,128)}, u32[]{:S(2)}) copy-start(s32[32,36]{1,0:T(8,128)} %param.12) | copy-start | bytes 13828
  56.8 27.8 %copy-start.4 = (bf16[4097,128]{1,0:T(8,128)(2,1)}, bf16[4097,128]{1,0:T(8,128)(2,1)S(1)}, u32[]{:S(2)}) copy-start(bf16[4097,128]{1,0:T(8,128)(2,1)S(1)} %collective-permute-done.5.refs_4_) | copy-start | bytes 3146500
  56.8 23.5 %collective-permute-start.6 = (bf16[4097,128]{1,0:T(8,128)(2,1)S(1)}, bf16[4097,128]{1,0:T(8,128)(2,1)S(1)}, u32[]{:S(2)}, u32[]{:S(2)}) collective-permute-start(bf16[4097,128]{1,0:T(8,128)(2,1)S(1)} %collective-permute-done.5.refs_4_), channel_id=1, source_target_pairs={{0,224},{32,0},{64,32},{96,64},{128,96},{160,128},{192,160},{224,1... | collective-permute-start | bytes 3146504 | tf_op jit(solution)/shard_map/ppermute | solution.py:166
  60.1 24.5 %collective-permute-start.2 = (bf16[4097,128]{1,0:T(8,128)(2,1)}, bf16[4097,128]{1,0:T(8,128)(2,1)S(1)}, u32[]{:S(2)}, u32[]{:S(2)}) collective-permute-start(bf16[4097,128]{1,0:T(8,128)(2,1)} %collective-permute-done.1.refs_3_), channel_id=1, source_target_pairs={{0,32},{32,64},{64,96},{96,128},{128,160},{160,192},{192,224},{224... | collective-permute-start | bytes 3146504 | tf_op jit(solution)/shard_map/ppermute | solution.py:165
  80.3 5.3 %copy-start.2 = (bf16[4097,128]{1,0:T(8,128)(2,1)}, bf16[4097,128]{1,0:T(8,128)(2,1)S(1)}, u32[]{:S(2)}) copy-start(bf16[4097,128]{1,0:T(8,128)(2,1)S(1)} %collective-permute-done.6.refs_6_) | copy-start | bytes 3146500
  81.2 16.8 %collective-permute-start.7 = (bf16[2049,128]{1,0:T(8,128)(2,1)}, bf16[2049,128]{1,0:T(8,128)(2,1)}, u32[]{:S(2)}, u32[]{:S(2)}) collective-permute-start(bf16[2049,128]{1,0:T(8,128)(2,1)} %slice.74), channel_id=1, source_target_pairs={{0,224},{32,0},{64,32},{96,64},{128,96},{160,128},{192,160},{224,1... | collective-permute-start | bytes 1573640 | tf_op jit(solution)/shard_map/ppermute | solution.py:173
  84.6 1.2 copy-start.3
  85.6 13.1 %collective-permute-start.3 = (bf16[2049,128]{1,0:T(8,128)(2,1)}, bf16[2049,128]{1,0:T(8,128)(2,1)S(1)}, u32[]{:S(2)}, u32[]{:S(2)}) collective-permute-start(bf16[2049,128]{1,0:T(8,128)(2,1)} %pad_maximum_fusion), channel_id=1, source_target_pairs={{0,32},{32,64},{64,96},{96,128},{128,160},{160,192},{192,224},{224... | collective-permute-start | bytes 1573640 | tf_op jit(solution)/shard_map/ppermute | solution.py:172
  98.7 0.8 copy-start.6
  104.8 39.2 %all-to-all-start = ((f32[64,64,128]{2,1,0:T(8,128)}), f32[64,64,128]{2,1,0:T(8,128)S(1)}, u32[]{:S(2)}, u32[]{:S(2)}) async-start(f32[64,64,128]{2,1,0:T(8,128)} %shard_map.65), calls=%async_computation | async-start | bytes 4194304 | tf_op jit(solution)/shard_map/all_to_all | solution.py:195
  144.0 1.4 copy-start

commit v8 on v7

--- a/solution.py
+++ b/solution.py
@@ -52,10 +52,7 @@
 
     def fetch(q):
         slot = q % 2
-        rows = sizes[q] * kp * block_len
-        return pltpu.make_async_copy(
-            w_refs[q].at[pl.ds(0, rows)], buf.at[slot, pl.ds(0, rows)], sem.at[slot]
-        )
+        return pltpu.make_async_copy(w_refs[q], buf.at[slot, pl.ds(0, sizes[q])], sem.at[slot])
 
     copies = [fetch(0)]
     copies[0].start()
@@ -70,10 +67,7 @@
             face = base + g
             col = face_base + face
             rows = p_ref[:, col * block_len:(col + 1) * block_len]
-            wide = jnp.concatenate(
-                [buf[slot, (g * kp + k) * block_len:(g * kp + k + 1) * block_len, :] for k in range(kp)],
-                axis=1,
-            )
+            wide = jnp.concatenate([buf[slot, g, k] for k in range(kp)], axis=1)
             prod = jnp.dot(rows, wide, preferred_element_type=jnp.float32)
             for k in range(kp):
                 pos = pos_ref[pat_ref[face * kp + k]]
@@ -82,7 +76,7 @@
 
 
 def project(positions, pat, pressure, pieces, sizes, kp, n_pos, face_base, acc):
-    time_len, block_len = pressure.shape[0], pieces[0].shape[1]
+    time_len, block_len = pressure.shape[0], pieces[0].shape[-1]
     face_blocks = sum(sizes)
     has_acc = acc is not None
     extra = [acc] if has_acc else []
@@ -98,7 +92,7 @@
         + [pl.BlockSpec(memory_space=pltpu.VMEM)] * len(extra),
         out_specs=pl.BlockSpec(memory_space=pltpu.VMEM),
         scratch_shapes=[
-            pltpu.VMEM((2, max(sizes) * kp * block_len, block_len), pieces[0].dtype),
+            pltpu.VMEM((2, max(sizes), kp, block_len, block_len), pieces[0].dtype),
             pltpu.SemaphoreType.DMA((2,)),
         ],
         cost_estimate=pl.CostEstimate(
@@ -151,29 +145,26 @@
     t = lax.axis_index("tm")
     fb_dev, kp, block_len = proj_weight.shape[1], proj_weight.shape[2], proj_weight.shape[3]
     half = fb_dev // 2
-    w_rows = fb_dev * kp * block_len
     right = [(i, (i + 1) % n_tm) for i in range(n_tm)]
     left = [(i, (i - 1) % n_tm) for i in range(n_tm)]
 
-    pat_row = jnp.zeros((1, block_len), proj_weight.dtype)
-    pat_row = pat_row.at[0, : fb_dev * kp].set(pattern[0].reshape(-1).astype(proj_weight.dtype))
-    own = jnp.concatenate([proj_weight[0].reshape(w_rows, block_len), pat_row], axis=0)
-
-    x_r = x_l = own
-    pieces, sizes, lane_at, order = [own], [fb_dev], [0], [t]
+    x_r = x_l = proj_weight[0]
+    p_r = p_l = pattern[0]
+    pieces, pats, sizes, order = [x_r], [p_r], [fb_dev], [t]
     for s in range(1, n_tm // 2):
-        x_r = lax.ppermute(x_r, "tm", right)
-        x_l = lax.ppermute(x_l, "tm", left)
+        x_r, p_r = lax.ppermute((x_r, p_r), "tm", right)
+        x_l, p_l = lax.ppermute((x_l, p_l), "tm", left)
+        x_r, p_r, x_l, p_l = lax.optimization_barrier((x_r, p_r, x_l, p_l))
         pieces += [x_r, x_l]
+        pats += [p_r, p_l]
         sizes += [fb_dev, fb_dev]
-        lane_at += [0, 0]
         order += [(t - s) % n_tm, (t + s) % n_tm]
-    h_rows = half * kp * block_len
-    h_r = lax.ppermute(jnp.concatenate([x_r[:h_rows], x_r[w_rows:]], axis=0), "tm", right)
-    h_l = lax.ppermute(x_l[h_rows:], "tm", left)
+    h_r, q_r = lax.ppermute((x_r[:half], p_r[:half]), "tm", right)
+    h_l, q_l = lax.ppermute((x_l[half:], p_l[half:]), "tm", left)
+    h_r, q_r, h_l, q_l = lax.optimization_barrier((h_r, q_r, h_l, q_l))
     pieces += [h_r, h_l]
+    pats += [q_r, q_l]
     sizes += [half, half]
-    lane_at += [0, half * kp]
     order += [(t + n_tm // 2) % n_tm]
 
     positions = send_positions(panel_list, owner_list, owner_count, own_index, slot_count)
@@ -182,8 +173,7 @@
     ordered = jnp.take(blocks, jnp.stack(order), axis=1).reshape(time_len, -1)
 
     def pattern_of(group):
-        rows = [pieces[i][-1, lane_at[i]:lane_at[i] + sizes[i] * kp] for i in group]
-        return jnp.concatenate(rows).astype(jnp.int32)
+        return jnp.concatenate([pats[i].reshape(-1) for i in group]).astype(jnp.int32)
 
     full = list(range(len(pieces) - 2))
     tail = [len(pieces) - 2, len(pieces) - 1]

time: 150 us -> 155 us (1.033)
  starting transfers between devices: 27.3 us -> 35.9 us
  other arithmetic: 10.5 us -> 5.44 us
    ppermute x8 -> x16, starting transfers between devices: 16.7 us -> 24.2 us  [the longest x6 19.7 us: body(): x_l, p_l = lax.ppermute((x_l, p_l), 'tm', left)]
    squeeze x11 -> x0, local copies, waits for them, and re-layouts: 3.03 us -> none  [pattern_of(): rows = [pieces[i][-1, lane_at[i]:lane_at[i] + sizes[i] * kp] for i in group]]
    concatenate x2 -> x1, other arithmetic: 2.35 us -> 0.59 us  [pattern_of(): jnp.concatenate([pats[i].reshape(-1) for i in group]).astype(jnp.int32)]
    ppermute x8 -> x16, waiting for transfers between devices: 56.7 us -> 57.4 us  [the longest x6 37.9 us: body(): x_r, p_r = lax.ppermute((x_r, p_r), 'tm', right)]
  transfers between devices with their start and end apart: 9 -> 17, of which waited for: 4 -> 5; matrix products, arithmetic and copies ran while one was open for 10% -> 8% of each run, Pallas kernels for 8% -> 7%
where the time goes in v8:
time: 155 us; the launch traced here: 154 us
  waiting for transfers between devices  81.5 us (53%)
  starting transfers between devices  35.9 us (23%)
  Pallas kernels  20.4 us (13%)
  local copies, waits for them, and re-layouts  10.6 us (7%)
  other arithmetic  5.44 us (4%)
    ppermute x6, waiting for transfers between devices, body(): x_r, p_r = lax.ppermute((x_r, p_r), 'tm', right)  37.9 us
    all_to_all x1, waiting for transfers between devices, body(): lax.all_to_all(packed, 'owner', split_axis=0, concat_axis=0, tiled=True)  24.2 us
    ppermute x6, starting transfers between devices, body(): x_l, p_l = lax.ppermute((x_l, p_l), 'tm', left)  19.7 us
    ppermute x6, waiting for transfers between devices, body(): x_l, p_l = lax.ppermute((x_l, p_l), 'tm', left)  19.5 us
    pallas_call x2, Pallas kernels, project(): pl.pallas_call(functools.partial(project_kernel, tuple(sizes), kp, block_...  16.8 us
    all_to_all x1, starting transfers between devices, body(): lax.all_to_all(packed, 'owner', split_axis=0, concat_axis=0, tiled=True)  11.7 us
    ppermute x2, starting transfers between devices, body(): h_l, q_l = lax.ppermute((x_l[half:], p_l[half:]), 'tm', left)  3.83 us
    pallas_call x1, Pallas kernels, collect(): pl.pallas_call(functools.partial(collect_kernel, n_rows), out_shape=jax.S...  3.64 us
  transfers between devices with their start and end apart: 17, of which 5 were waited for; matrix products, arithmetic and copies ran while one was open for 8% of the time, Pallas kernels for 7%

profile of v8, /device:TPU:1, one launch (start us, length us, event | category | flops | bytes accessed | tf_op | source)
XLA Modules:
  0.0 154.1 jit_solution(13275987744298815171)
XLA Ops:
  0.0 6.4 %collective-permute-start.2 = (bf16[8,4,128,128]{3,2,1,0:T(8,128)(2,1)}, bf16[8,4,128,128]{3,2,1,0:T(8,128)(2,1)S(1)}, u32[]{:S(2)}, u32[]{:S(2)}) collective-permute-start(bf16[8,4,128,128]{3,2,1,0:T(8,128)(2,1)} %bitcast.42), channel_id=1, source_target_pairs={{0,224},{32,0},{64,32},{96,64},{128,96},{160,128},{192,160},{224,1... | collective-permute-start | bytes 3145736 | tf_op jit(solution)/shard_map/ppermute | solution.py:156
  6.4 2.7 %collective-permute-start.3 = (s32[8,4]{0,1:T(4,128)}, s32[8,4]{0,1:T(4,128)S(1)}, u32[]{:S(2)}, u32[]{:S(2)}) collective-permute-start(s32[8,4]{0,1:T(4,128)} %bitcast.46), channel_id=1, source_target_pairs={{0,224},{32,0},{64,32},{96,64},{128,96},{160,128},{192,160},{224,1... | collective-permute-start | bytes 392 | tf_op jit(solution)/shard_map/ppermute | solution.py:156
  9.1 19.5 %collective-permute-done.3 = s32[8,4]{0,1:T(4,128)S(1)} collective-permute-done((s32[8,4]{0,1:T(4,128)}, s32[8,4]{0,1:T(4,128)S(1)}, u32[]{:S(2)}, u32[]{:S(2)}) %collective-permute-start.3) | collective-permute-done | bytes 160 | tf_op jit(solution)/shard_map/ppermute | solution.py:156
  28.6 3.2 %collective-permute-done.1 = s32[8,4]{0,1:T(4,128)S(1)} collective-permute-done((s32[8,4]{0,1:T(4,128)}, s32[8,4]{0,1:T(4,128)S(1)}, u32[]{:S(2)}, u32[]{:S(2)}) %collective-permute-start.1) | collective-permute-done | bytes 160 | tf_op jit(solution)/shard_map/ppermute | solution.py:155
  31.7 0.1 collective-permute-start.4
  31.8 2.7 %collective-permute-start.6 = (bf16[8,4,128,128]{3,2,1,0:T(8,128)(2,1)S(1)}, bf16[8,4,128,128]{3,2,1,0:T(8,128)(2,1)}, u32[]{:S(2)}, u32[]{:S(2)}) collective-permute-start(bf16[8,4,128,128]{3,2,1,0:T(8,128)(2,1)S(1)} %collective-permute-done.2.refs_2_), channel_id=1, source_target_pairs={{0,224},{32,0},{64,32},{96,64},{128,96},{160,128},{192,160},{224,1... | collective-permute-start | bytes 3145736 | tf_op jit(solution)/shard_map/ppermute | solution.py:156
  34.5 0.1 stack.53
  34.7 1.3 copy.54
  36.0 0.1 stack.62
  36.1 0.6 gather_fusion
  36.8 2.7 %collective-permute-start.7 = (s32[8,4]{0,1:T(4,128)S(1)}, s32[8,4]{0,1:T(4,128)S(1)}, u32[]{:S(2)}, u32[]{:S(2)}) collective-permute-start(s32[8,4]{0,1:T(4,128)S(1)} %collective-permute-done.3), channel_id=1, source_target_pairs={{0,224},{32,0},{64,32},{96,64},{128,96},{160,128},{192,160},{224,1... | collective-permute-start | bytes 392 | tf_op jit(solution)/shard_map/ppermute | solution.py:156
  39.6 16.7 %collective-permute-done.5 = s32[8,4]{0,1:T(4,128)S(1)} collective-permute-done((s32[8,4]{0,1:T(4,128)S(1)}, s32[8,4]{0,1:T(4,128)S(1)}, u32[]{:S(2)}, u32[]{:S(2)}) %collective-permute-start.5) | collective-permute-done | bytes 160 | tf_op jit(solution)/shard_map/ppermute | solution.py:155
  56.4 2.7 %collective-permute-start.10 = (bf16[8,4,128,128]{3,2,1,0:T(8,128)(2,1)}, bf16[8,4,128,128]{3,2,1,0:T(8,128)(2,1)S(1)}, u32[]{:S(2)}, u32[]{:S(2)}) collective-permute-start(bf16[8,4,128,128]{3,2,1,0:T(8,128)(2,1)} %collective-permute-done.6.refs_4_), channel_id=1, source_target_pairs={{0,224},{32,0},{64,32},{96,64},{128,96},{160,128},{192,160},{224,1... | collective-permute-start | bytes 3145736 | tf_op jit(solution)/shard_map/ppermute | solution.py:156
  59.1 0.1 broadcast_select_fusion
  59.3 2.7 %collective-permute-start.11 = (s32[8,4]{0,1:T(4,128)S(1)}, s32[8,4]{0,1:T(4,128)S(1)}, u32[]{:S(2)}, u32[]{:S(2)}) collective-permute-start(s32[8,4]{0,1:T(4,128)S(1)} %collective-permute-done.7), channel_id=1, source_target_pairs={{0,224},{32,0},{64,32},{96,64},{128,96},{160,128},{192,160},{224,1... | collective-permute-start | bytes 392 | tf_op jit(solution)/shard_map/ppermute | solution.py:156
  62.0 18.0 %collective-permute-done.9 = s32[8,4]{0,1:T(4,128)S(1)} collective-permute-done((s32[8,4]{0,1:T(4,128)S(1)}, s32[8,4]{0,1:T(4,128)S(1)}, u32[]{:S(2)}, u32[]{:S(2)}) %collective-permute-start.9) | collective-permute-done | bytes 160 | tf_op jit(solution)/shard_map/ppermute | solution.py:155
  80.0 1.0 slice.20
  81.0 0.8 slice.18
  81.8 2.7 %collective-permute-start.14 = (bf16[4,4,128,128]{3,2,1,0:T(8,128)(2,1)}, bf16[4,4,128,128]{3,2,1,0:T(8,128)(2,1)}, u32[]{:S(2)}, u32[]{:S(2)}) collective-permute-start(bf16[4,4,128,128]{3,2,1,0:T(8,128)(2,1)} %slice.20), channel_id=1, source_target_pairs={{0,224},{32,0},{64,32},{96,64},{128,96},{160,128},{192,160},{224,1... | collective-permute-start | bytes 1572872 | tf_op jit(solution)/shard_map/ppermute | solution.py:163
  84.5 0.7 and_reduce_fusion
  85.3 0.7 slice.26.p_ref
  86.0 1.0 slice.27.p_ref
  87.0 0.1 select_reduce_fusion.2
  87.1 0.2 convert_reduce_fusion.1
  87.3 0.5 multiply_add_fusion.pos_ref
  88.9 1.2 collective-permute-start.15
  90.1 0.3 collective-permute-start.13
  90.4 0.7 concatenate.28.pat_ref
  91.1 11.5 %shard_map.64.refs_2_ = f32[64,64,128]{2,1,0:T(8,128)} custom-call(s32[32]{0:T(128)} %multiply_add_fusion.pos_ref, s32[224]{0:T(256)} %concatenate.28.pat_ref, bf16[64,7168]{1,0:T(8,128)(2,1)} %slice.27.p_ref, bf16[8,4,128,128]{3,2,1,0:T(8,128)(2,1)} %bitcast.44, bf16[8,4,128,128]{3,2,1,0:T(8,128)(2,1)} %collective-permute-done.refs_1_, ...), custom_call_target="tpu_custom_call" | custom-call | flops 469762048 | bytes 10354688 | tf_op jit(solution)/shard_map/pallas_call | solution.py:83
  102.6 0.1 copy.38
  102.7 0.1 reshape.431
  102.8 0.1 copy.39
  102.9 0.1 reshape.432
  102.9 0.6 pad_add_fusion.pat_ref
  103.5 5.3 %shard_map.65 = f32[64,64,128]{2,1,0:T(8,128)} custom-call(s32[32]{0:T(128)} %multiply_add_fusion.pos_ref, s32[32]{0:T(128)} %pad_add_fusion.pat_ref, bf16[64,1024]{1,0:T(8,128)(2,1)} %slice.26.p_ref, bf16[4,4,128,128]{3,2,1,0:T(8,128)(2,1)} %collective-permute-done.12.refs_0_, bf16[4,4,128,128]{3,2,1,0:T(8,128)(2,1)} %collective-permute-done.14.refs_1_, ...), custom_call_target="tpu_custom_call" | custom-call | flops 67108864 | bytes 5373952 | tf_op jit(solution)/shard_map/pallas_call | solution.py:83
  108.9 11.7 %all-to-all-start = ((f32[64,64,128]{2,1,0:T(8,128)}), f32[64,64,128]{2,1,0:T(8,128)S(1)}, u32[]{:S(2)}, u32[]{:S(2)}) async-start(f32[64,64,128]{2,1,0:T(8,128)} %shard_map.65), calls=%async_computation | async-start | bytes 4194304 | tf_op jit(solution)/shard_map/all_to_all | solution.py:185
  120.6 0.6 dynamic_slice.10
  121.2 0.6 iota_compare_fusion.3
  121.8 0.8 fusion
  122.6 0.6 convert_reduce_fusion
  123.3 0.1 fusion.2
  123.4 0.8 select_reduce_fusion
  124.2 0.1 select_reduce_fusion.1
  124.3 0.1 copy.37
  124.4 0.6 select_n.81.dest_ref
  125.0 24.2 %all-to-all-done.r_ref = f32[64,64,128]{2,1,0:T(8,128)S(1)} async-done(((f32[64,64,128]{2,1,0:T(8,128)}), f32[64,64,128]{2,1,0:T(8,128)S(1)}, u32[]{:S(2)}, u32[]{:S(2)}) %all-to-all-start) | async-done | bytes 2097184 | tf_op jit(solution)/shard_map/all_to_all | solution.py:185
  149.2 1.3 copy-done
  150.5 3.6 %shard_map.66 = f32[36,64,128]{2,1,0:T(8,128)} custom-call(s32[64]{0:T(128)} %select_n.81.dest_ref, f32[64,64,128]{2,1,0:T(8,128)} %copy-done), custom_call_target="tpu_custom_call" | custom-call | tf_op jit(solution)/shard_map/pallas_call | solution.py:125
  (59 shorter events, 1.7 us)
Async XLA Ops:
  0.0 31.7 %collective-permute-start.2 = (bf16[8,4,128,128]{3,2,1,0:T(8,128)(2,1)}, bf16[8,4,128,128]{3,2,1,0:T(8,128)(2,1)S(1)}, u32[]{:S(2)}, u32[]{:S(2)}) collective-permute-start(bf16[8,4,128,128]{3,2,1,0:T(8,128)(2,1)} %bitcast.42), channel_id=1, source_target_pairs={{0,224},{32,0},{64,32},{96,64},{128,96},{160,128},{192,160},{224,1... | collective-permute-start | bytes 3145736 | tf_op jit(solution)/shard_map/ppermute | solution.py:156
  6.4 25.3 %collective-permute-start = (bf16[8,4,128,128]{3,2,1,0:T(8,128)(2,1)}, bf16[8,4,128,128]{3,2,1,0:T(8,128)(2,1)}, u32[]{:S(2)}, u32[]{:S(2)}) collective-permute-start(bf16[8,4,128,128]{3,2,1,0:T(8,128)(2,1)} %bitcast.43), channel_id=1, source_target_pairs={{0,32},{32,64},{64,96},{96,128},{128,160},{160,192},{192,224},{224... | collective-permute-start | bytes 3145736 | tf_op jit(solution)/shard_map/ppermute | solution.py:155
  6.4 22.2 %collective-permute-start.3 = (s32[8,4]{0,1:T(4,128)}, s32[8,4]{0,1:T(4,128)S(1)}, u32[]{:S(2)}, u32[]{:S(2)}) collective-permute-start(s32[8,4]{0,1:T(4,128)} %bitcast.46), channel_id=1, source_target_pairs={{0,224},{32,0},{64,32},{96,64},{128,96},{160,128},{192,160},{224,1... | collective-permute-start | bytes 392 | tf_op jit(solution)/shard_map/ppermute | solution.py:156
  9.1 22.7 %collective-permute-start.1 = (s32[8,4]{0,1:T(4,128)}, s32[8,4]{0,1:T(4,128)S(1)}, u32[]{:S(2)}, u32[]{:S(2)}) collective-permute-start(s32[8,4]{0,1:T(4,128)} %bitcast.47), channel_id=1, source_target_pairs={{0,32},{32,64},{64,96},{96,128},{128,160},{160,192},{192,224},{224... | collective-permute-start | bytes 392 | tf_op jit(solution)/shard_map/ppermute | solution.py:155
  31.7 5.0 %copy-start.3 = (bf16[8,4,128,128]{3,2,1,0:T(8,128)(2,1)}, bf16[8,4,128,128]{3,2,1,0:T(8,128)(2,1)S(1)}, u32[]{:S(2)}) copy-start(bf16[8,4,128,128]{3,2,1,0:T(8,128)(2,1)S(1)} %collective-permute-done.2.refs_2_) | copy-start | bytes 3145732
  31.7 24.6 %collective-permute-start.4 = (bf16[8,4,128,128]{3,2,1,0:T(8,128)(2,1)}, bf16[8,4,128,128]{3,2,1,0:T(8,128)(2,1)}, u32[]{:S(2)}, u32[]{:S(2)}) collective-permute-start(bf16[8,4,128,128]{3,2,1,0:T(8,128)(2,1)} %collective-permute-done.refs_1_), channel_id=1, source_target_pairs={{0,32},{32,64},{64,96},{96,128},{128,160},{160,192},{192,224},{224... | collective-permute-start | bytes 3145736 | tf_op jit(solution)/shard_map/ppermute | solution.py:155
  31.8 24.5 %collective-permute-start.6 = (bf16[8,4,128,128]{3,2,1,0:T(8,128)(2,1)S(1)}, bf16[8,4,128,128]{3,2,1,0:T(8,128)(2,1)}, u32[]{:S(2)}, u32[]{:S(2)}) collective-permute-start(bf16[8,4,128,128]{3,2,1,0:T(8,128)(2,1)S(1)} %collective-permute-done.2.refs_2_), channel_id=1, source_target_pairs={{0,224},{32,0},{64,32},{96,64},{128,96},{160,128},{192,160},{224,1... | collective-permute-start | bytes 3145736 | tf_op jit(solution)/shard_map/ppermute | solution.py:156
  36.8 19.6 %collective-permute-start.5 = (s32[8,4]{0,1:T(4,128)S(1)}, s32[8,4]{0,1:T(4,128)S(1)}, u32[]{:S(2)}, u32[]{:S(2)}) collective-permute-start(s32[8,4]{0,1:T(4,128)S(1)} %collective-permute-done.1), channel_id=1, source_target_pairs={{0,32},{32,64},{64,96},{96,128},{128,160},{160,192},{192,224},{224... | collective-permute-start | bytes 392 | tf_op jit(solution)/shard_map/ppermute | solution.py:155
  36.8 19.5 %collective-permute-start.7 = (s32[8,4]{0,1:T(4,128)S(1)}, s32[8,4]{0,1:T(4,128)S(1)}, u32[]{:S(2)}, u32[]{:S(2)}) collective-permute-start(s32[8,4]{0,1:T(4,128)S(1)} %collective-permute-done.3), channel_id=1, source_target_pairs={{0,224},{32,0},{64,32},{96,64},{128,96},{160,128},{192,160},{224,1... | collective-permute-start | bytes 392 | tf_op jit(solution)/shard_map/ppermute | solution.py:156
  39.5 19.7 %copy-start.7 = (s32[32]{0:T(128)S(1)}, s32[32]{0:T(128)}, u32[]{:S(2)}) copy-start(s32[32]{0:T(128)} %param.11) | copy-start | bytes 388
  39.5 22.5 %copy-start.4 = (s32[32,32]{1,0:T(8,128)S(1)}, s32[32,32]{1,0:T(8,128)}, u32[]{:S(2)}) copy-start(s32[32,32]{1,0:T(8,128)} %param.9) | copy-start | bytes 12292
  56.3 23.6 %collective-permute-start.8 = (bf16[8,4,128,128]{3,2,1,0:T(8,128)(2,1)}, bf16[8,4,128,128]{3,2,1,0:T(8,128)(2,1)S(1)}, u32[]{:S(2)}, u32[]{:S(2)}) collective-permute-start(bf16[8,4,128,128]{3,2,1,0:T(8,128)(2,1)} %collective-permute-done.4.refs_3_), channel_id=1, source_target_pairs={{0,32},{32,64},{64,96},{96,128},{128,160},{160,192},{192,224},{224... | collective-permute-start | bytes 3145736 | tf_op jit(solution)/shard_map/ppermute | solution.py:155
  56.4 23.6 %collective-permute-start.10 = (bf16[8,4,128,128]{3,2,1,0:T(8,128)(2,1)}, bf16[8,4,128,128]{3,2,1,0:T(8,128)(2,1)S(1)}, u32[]{:S(2)}, u32[]{:S(2)}) collective-permute-start(bf16[8,4,128,128]{3,2,1,0:T(8,128)(2,1)} %collective-permute-done.6.refs_4_), channel_id=1, source_target_pairs={{0,224},{32,0},{64,32},{96,64},{128,96},{160,128},{192,160},{224,1... | collective-permute-start | bytes 3145736 | tf_op jit(solution)/shard_map/ppermute | solution.py:156
  59.1 25.4 %copy-start.5 = (s32[32,36]{1,0:T(8,128)S(1)}, s32[32,36]{1,0:T(8,128)}, u32[]{:S(2)}) copy-start(s32[32,36]{1,0:T(8,128)} %param.10) | copy-start | bytes 13828
  59.1 26.1 %copy-start.6 = (s32[1,8,4]{1,2,0:T(4,128)S(1)}, s32[1,8,4]{1,2,0:T(4,128)}, u32[]{:S(2)}) copy-start(s32[1,8,4]{1,2,0:T(4,128)} %param.8) | copy-start | bytes 388
  59.3 20.7 %collective-permute-start.9 = (s32[8,4]{0,1:T(4,128)S(1)}, s32[8,4]{0,1:T(4,128)S(1)}, u32[]{:S(2)}, u32[]{:S(2)}) collective-permute-start(s32[8,4]{0,1:T(4,128)S(1)} %collective-permute-done.5), channel_id=1, source_target_pairs={{0,32},{32,64},{64,96},{96,128},{128,160},{160,192},{192,224},{224... | collective-permute-start | bytes 392 | tf_op jit(solution)/shard_map/ppermute | solution.py:155
  59.3 20.6 %collective-permute-start.11 = (s32[8,4]{0,1:T(4,128)S(1)}, s32[8,4]{0,1:T(4,128)S(1)}, u32[]{:S(2)}, u32[]{:S(2)}) collective-permute-start(s32[8,4]{0,1:T(4,128)S(1)} %collective-permute-done.7), channel_id=1, source_target_pairs={{0,224},{32,0},{64,32},{96,64},{128,96},{160,128},{192,160},{224,1... | collective-permute-start | bytes 392 | tf_op jit(solution)/shard_map/ppermute | solution.py:156
  80.0 7.0 %copy-start.1 = (bf16[8,4,128,128]{3,2,1,0:T(8,128)(2,1)}, bf16[8,4,128,128]{3,2,1,0:T(8,128)(2,1)S(1)}, u32[]{:S(2)}) copy-start(bf16[8,4,128,128]{3,2,1,0:T(8,128)(2,1)S(1)} %collective-permute-done.8.refs_5_) | copy-start | bytes 3145732
  80.0 7.0 %copy-start.2 = (bf16[8,4,128,128]{3,2,1,0:T(8,128)(2,1)}, bf16[8,4,128,128]{3,2,1,0:T(8,128)(2,1)S(1)}, u32[]{:S(2)}) copy-start(bf16[8,4,128,128]{3,2,1,0:T(8,128)(2,1)S(1)} %collective-permute-done.10.refs_6_) | copy-start | bytes 3145732
  81.8 20.7 %collective-permute-start.12 = (bf16[4,4,128,128]{3,2,1,0:T(8,128)(2,1)}, bf16[4,4,128,128]{3,2,1,0:T(8,128)(2,1)}, u32[]{:S(2)}, u32[]{:S(2)}) collective-permute-start(bf16[4,4,128,128]{3,2,1,0:T(8,128)(2,1)} %slice.18), channel_id=1, source_target_pairs={{0,32},{32,64},{64,96},{96,128},{128,160},{160,192},{192,224},{224... | collective-permute-start | bytes 1572872 | tf_op jit(solution)/shard_map/ppermute | solution.py:162
  81.8 20.7 %collective-permute-start.14 = (bf16[4,4,128,128]{3,2,1,0:T(8,128)(2,1)}, bf16[4,4,128,128]{3,2,1,0:T(8,128)(2,1)}, u32[]{:S(2)}, u32[]{:S(2)}) collective-permute-start(bf16[4,4,128,128]{3,2,1,0:T(8,128)(2,1)} %slice.20), channel_id=1, source_target_pairs={{0,224},{32,0},{64,32},{96,64},{128,96},{160,128},{192,160},{224,1... | collective-permute-start | bytes 1572872 | tf_op jit(solution)/shard_map/ppermute | solution.py:163
  88.9 13.6 %collective-permute-start.15 = (s32[4,4]{0,1:T(4,128)S(1)}, s32[4,4]{0,1:T(4,128)S(1)}, u32[]{:S(2)}, u32[]{:S(2)}) collective-permute-start(s32[4,4]{0,1:T(4,128)S(1)} %slice.21), channel_id=1, source_target_pairs={{0,224},{32,0},{64,32},{96,64},{128,96},{160,128},{192,160},{224,1... | collective-permute-start | bytes 200 | tf_op jit(solution)/shard_map/ppermute | solution.py:163
  90.1 12.5 %collective-permute-start.13 = (s32[4,4]{0,1:T(4,128)S(1)}, s32[4,4]{0,1:T(4,128)S(1)}, u32[]{:S(2)}, u32[]{:S(2)}) collective-permute-start(s32[4,4]{0,1:T(4,128)S(1)} %bitcast.48), channel_id=1, source_target_pairs={{0,32},{32,64},{64,96},{96,128},{128,160},{160,192},{192,224},{224... | collective-permute-start | bytes 200 | tf_op jit(solution)/shard_map/ppermute | solution.py:162
  108.9 40.3 %all-to-all-start = ((f32[64,64,128]{2,1,0:T(8,128)}), f32[64,64,128]{2,1,0:T(8,128)S(1)}, u32[]{:S(2)}, u32[]{:S(2)}) async-start(f32[64,64,128]{2,1,0:T(8,128)} %shard_map.65), calls=%async_computation | async-start | bytes 4194304 | tf_op jit(solution)/shard_map/all_to_all | solution.py:185
  149.2 1.3 copy-start

commit v9 on v7

--- a/solution.py
+++ b/solution.py
@@ -45,27 +45,23 @@
     w_refs = refs[:n]
     if has_acc:
         acc_ref, o_ref, buf, sem = refs[n:]
+    else:
+        o_ref, buf, sem = refs[n:]
+    rows_of = [sizes[q] * kp * block_len for q in range(n)]
+    copies = [
+        pltpu.make_async_copy(w_refs[q].at[pl.ds(0, rows_of[q])], buf.at[q, pl.ds(0, rows_of[q])], sem.at[q])
+        for q in range(n)
+    ]
+    for c in copies:
+        c.start()
+    if has_acc:
         o_ref[...] = acc_ref[...]
     else:
-        o_ref, buf, sem = refs[n:]
         o_ref[...] = jnp.zeros_like(o_ref)
-
-    def fetch(q):
-        slot = q % 2
-        rows = sizes[q] * kp * block_len
-        return pltpu.make_async_copy(
-            w_refs[q].at[pl.ds(0, rows)], buf.at[slot, pl.ds(0, rows)], sem.at[slot]
-        )
-
-    copies = [fetch(0)]
-    copies[0].start()
     base = 0
     for q in range(n):
         copies[q].wait()
-        if q + 1 < n:
-            copies.append(fetch(q + 1))
-            copies[q + 1].start()
-        slot = q % 2
+        slot = q
         for g in range(sizes[q]):
             face = base + g
             col = face_base + face
@@ -98,8 +94,8 @@
         + [pl.BlockSpec(memory_space=pltpu.VMEM)] * len(extra),
         out_specs=pl.BlockSpec(memory_space=pltpu.VMEM),
         scratch_shapes=[
-            pltpu.VMEM((2, max(sizes) * kp * block_len, block_len), pieces[0].dtype),
-            pltpu.SemaphoreType.DMA((2,)),
+            pltpu.VMEM((len(pieces), max(sizes) * kp * block_len, block_len), pieces[0].dtype),
+            pltpu.SemaphoreType.DMA((len(pieces),)),
         ],
         cost_estimate=pl.CostEstimate(
             flops=2 * face_blocks * kp * time_len * block_len * block_len,

time: 150 us -> 148 us (0.987)
  Pallas kernels: 20.4 us -> 14.4 us
  waiting for transfers between devices: 80.8 us -> 84.4 us
    pallas_call x2, Pallas kernels: 16.8 us -> 10.8 us  [project(): pl.pallas_call(functools.partial(project_kernel, tuple(sizes), kp, block_...]
    ppermute x1, waiting for transfers between devices: 0.01 us -> 3.3 us  [body(): lax.ppermute(jnp.concatenate([x_r[:h_rows], x_r[w_rows:]], axis=0), 'tm',...]
  transfers between devices with their start and end apart: 9 -> 9, of which waited for: 4 -> 6; matrix products, arithmetic and copies ran while one was open for 10% -> 10% of each run, Pallas kernels for 8% -> 4%
where the time goes in v9:
time: 148 us; the launch traced here: 147 us
  waiting for transfers between devices  84.4 us (57%)
  starting transfers between devices  28.2 us (19%)
  Pallas kernels  14.4 us (10%)
  other arithmetic  10.5 us (7%)
  local copies, waits for them, and re-layouts  9.74 us (7%)
    ppermute x3, waiting for transfers between devices, body(): x_l = lax.ppermute(x_l, 'tm', left)  56.7 us
    all_to_all x1, waiting for transfers between devices, body(): lax.all_to_all(packed, 'owner', split_axis=0, concat_axis=0, tiled=True)  24.1 us
    ppermute x3, starting transfers between devices, body(): x_l = lax.ppermute(x_l, 'tm', left)  13.3 us
    all_to_all x1, starting transfers between devices, body(): lax.all_to_all(packed, 'owner', split_axis=0, concat_axis=0, tiled=True)  11.5 us
    pallas_call x2, Pallas kernels, project(): pl.pallas_call(functools.partial(project_kernel, tuple(sizes), kp, block_...  10.8 us
    pallas_call x1, Pallas kernels, collect(): pl.pallas_call(functools.partial(collect_kernel, n_rows), out_shape=jax.S...  3.65 us
    ppermute x1, starting transfers between devices, body(): h_l = lax.ppermute(x_l[h_rows:], 'tm', left)  3.41 us
    ppermute x1, waiting for transfers between devices, body(): lax.ppermute(jnp.concatenate([x_r[:h_rows], x_r[w_rows:]], axis=0), 'tm',...  3.3 us
  transfers between devices with their start and end apart: 9, of which 6 were waited for; matrix products, arithmetic and copies ran while one was open for 10% of the time, Pallas kernels for 4%

profile of v9, /device:TPU:1, one launch (start us, length us, event | category | flops | bytes accessed | tf_op | source)
XLA Modules:
  0.0 147.4 jit_solution(13483888611470553712)
XLA Ops:
  0.0 0.6 compare_reduce_fusion
  0.6 1.3 convert_select_fusion
  2.0 0.1 copy.17
  2.1 0.1 squeeze.36
  2.2 1.4 fusion.1.refs_0_
  3.6 6.5 %collective-permute-start.4 = (bf16[4097,128]{1,0:T(8,128)(2,1)S(1)}, bf16[4097,128]{1,0:T(8,128)(2,1)}, u32[]{:S(2)}, u32[]{:S(2)}) collective-permute-start(bf16[4097,128]{1,0:T(8,128)(2,1)S(1)} %fusion.1.refs_0_), channel_id=1, source_target_pairs={{0,224},{32,0},{64,32},{96,64},{128,96},{160,128},{192,160},{224,1... | collective-permute-start | bytes 3146504 | tf_op jit(solution)/shard_map/ppermute | solution.py:162
  10.3 0.1 stack.62
  10.5 0.6 gather_fusion
  11.2 20.7 %collective-permute-done.4.refs_2_ = bf16[4097,128]{1,0:T(8,128)(2,1)} collective-permute-done((bf16[4097,128]{1,0:T(8,128)(2,1)S(1)}, bf16[4097,128]{1,0:T(8,128)(2,1)}, u32[]{:S(2)}, u32[]{:S(2)}) %collective-permute-start.4) | collective-permute-done | bytes 1048864 | tf_op jit(solution)/shard_map/ppermute | solution.py:162
  31.9 3.5 %collective-permute-start.5 = (bf16[4097,128]{1,0:T(8,128)(2,1)}, bf16[4097,128]{1,0:T(8,128)(2,1)S(1)}, u32[]{:S(2)}, u32[]{:S(2)}) collective-permute-start(bf16[4097,128]{1,0:T(8,128)(2,1)} %collective-permute-done.4.refs_2_), channel_id=1, source_target_pairs={{0,224},{32,0},{64,32},{96,64},{128,96},{160,128},{192,160},{224,1... | collective-permute-start | bytes 3146504 | tf_op jit(solution)/shard_map/ppermute | solution.py:162
  35.4 0.1 broadcast_select_fusion
  35.7 0.7 slice.76.p_ref
  36.3 1.1 slice.83.p_ref
  37.5 0.7 and_reduce_fusion
  38.2 0.1 select_reduce_fusion.2
  38.3 0.2 convert_reduce_fusion.1
  38.5 18.3 %collective-permute-done.5.refs_4_ = bf16[4097,128]{1,0:T(8,128)(2,1)S(1)} collective-permute-done((bf16[4097,128]{1,0:T(8,128)(2,1)}, bf16[4097,128]{1,0:T(8,128)(2,1)S(1)}, u32[]{:S(2)}, u32[]{:S(2)}) %collective-permute-start.5) | collective-permute-done | bytes 1048864 | tf_op jit(solution)/shard_map/ppermute | solution.py:162
  56.8 3.3 %collective-permute-start.6 = (bf16[4097,128]{1,0:T(8,128)(2,1)S(1)}, bf16[4097,128]{1,0:T(8,128)(2,1)S(1)}, u32[]{:S(2)}, u32[]{:S(2)}) collective-permute-start(bf16[4097,128]{1,0:T(8,128)(2,1)S(1)} %collective-permute-done.5.refs_4_), channel_id=1, source_target_pairs={{0,224},{32,0},{64,32},{96,64},{128,96},{160,128},{192,160},{224,1... | collective-permute-start | bytes 3146504 | tf_op jit(solution)/shard_map/ppermute | solution.py:162
  60.1 0.5 multiply_add_fusion.pos_ref
  60.6 0.7 slice_bitcast_fusion.4
  61.3 0.7 slice_bitcast_fusion.5
  62.0 0.7 slice_bitcast_fusion.3
  62.6 17.6 %collective-permute-done.6.refs_6_ = bf16[4097,128]{1,0:T(8,128)(2,1)S(1)} collective-permute-done((bf16[4097,128]{1,0:T(8,128)(2,1)S(1)}, bf16[4097,128]{1,0:T(8,128)(2,1)S(1)}, u32[]{:S(2)}, u32[]{:S(2)}) %collective-permute-start.6) | collective-permute-done | bytes 1048864 | tf_op jit(solution)/shard_map/ppermute | solution.py:162
  80.3 0.9 slice.74
  81.2 3.4 %collective-permute-start.7 = (bf16[2049,128]{1,0:T(8,128)(2,1)}, bf16[2049,128]{1,0:T(8,128)(2,1)}, u32[]{:S(2)}, u32[]{:S(2)}) collective-permute-start(bf16[2049,128]{1,0:T(8,128)(2,1)} %slice.74), channel_id=1, source_target_pairs={{0,224},{32,0},{64,32},{96,64},{128,96},{160,128},{192,160},{224,1... | collective-permute-start | bytes 1573640 | tf_op jit(solution)/shard_map/ppermute | solution.py:169
  84.6 1.0 pad_maximum_fusion
  85.6 0.2 copy-done.3
  85.8 0.1 concatenate.38
  85.9 0.6 convert_element_type.26.pat_ref
  86.4 6.2 %shard_map.64.refs_2_ = f32[64,64,128]{2,1,0:T(8,128)} custom-call(s32[32]{0:T(128)} %multiply_add_fusion.pos_ref, s32[224]{0:T(256)} %convert_element_type.26.pat_ref, bf16[64,7168]{1,0:T(8,128)(2,1)} %slice.83.p_ref, bf16[4097,128]{1,0:T(8,128)(2,1)} %copy-done.1, bf16[4097,128]{1,0:T(8,128)(2,1)} %collective-permute-done.refs_1_, ...), custom_call_target="tpu_custom_call" | custom-call | flops 469762048 | bytes 10354688 | tf_op jit(solution)/shard_map/pallas_call | solution.py:85
  92.7 0.3 collective-permute-done.7.refs_1_
  93.0 0.7 slice_bitcast_fusion.6
  93.7 3.3 %collective-permute-done.3.refs_0_ = bf16[2049,128]{1,0:T(8,128)(2,1)S(1)} collective-permute-done((bf16[2049,128]{1,0:T(8,128)(2,1)}, bf16[2049,128]{1,0:T(8,128)(2,1)S(1)}, u32[]{:S(2)}, u32[]{:S(2)}) %collective-permute-start.3) | collective-permute-done | bytes 524576 | tf_op jit(solution)/shard_map/ppermute | solution.py:168
  97.0 0.8 maximum_convert_fusion.pat_ref
  97.8 4.5 %shard_map.65 = f32[64,64,128]{2,1,0:T(8,128)} custom-call(s32[32]{0:T(128)} %multiply_add_fusion.pos_ref, s32[32]{0:T(128)} %maximum_convert_fusion.pat_ref, bf16[64,1024]{1,0:T(8,128)(2,1)} %slice.76.p_ref, bf16[2049,128]{1,0:T(8,128)(2,1)} %copy-done.6, bf16[2049,128]{1,0:T(8,128)(2,1)} %collective-permute-done.7.refs_1_, f32[64,64,128]{2,1,0:T(8,128)} %shard_map.64.refs_2_), custom_call_target="tpu_custom_call" | custom-call | flops 67108864 | bytes 5373952 | tf_op jit(solution)/shard_map/pallas_call | solution.py:85
  102.4 11.5 %all-to-all-start = ((f32[64,64,128]{2,1,0:T(8,128)}), f32[64,64,128]{2,1,0:T(8,128)S(1)}, u32[]{:S(2)}, u32[]{:S(2)}) async-start(f32[64,64,128]{2,1,0:T(8,128)} %shard_map.65), calls=%async_computation | async-start | bytes 4194304 | tf_op jit(solution)/shard_map/all_to_all | solution.py:191
  113.8 0.6 dynamic_slice.10
  114.4 0.6 iota_compare_fusion.4
  115.1 0.8 fusion.2
  115.9 0.6 convert_reduce_fusion
  116.5 0.1 fusion.4
  116.6 0.8 select_reduce_fusion
  117.4 0.1 select_reduce_fusion.1
  117.6 0.1 copy.16
  117.6 0.6 select_n.81.dest_ref
  118.3 24.1 %all-to-all-done.r_ref = f32[64,64,128]{2,1,0:T(8,128)S(1)} async-done(((f32[64,64,128]{2,1,0:T(8,128)}), f32[64,64,128]{2,1,0:T(8,128)S(1)}, u32[]{:S(2)}, u32[]{:S(2)}) %all-to-all-start) | async-done | bytes 2097184 | tf_op jit(solution)/shard_map/all_to_all | solution.py:191
  142.4 1.3 copy-done
  143.8 3.6 %shard_map.66 = f32[36,64,128]{2,1,0:T(8,128)} custom-call(s32[64]{0:T(128)} %select_n.81.dest_ref, f32[64,64,128]{2,1,0:T(8,128)} %copy-done), custom_call_target="tpu_custom_call" | custom-call | tf_op jit(solution)/shard_map/pallas_call | solution.py:127
  (45 shorter events, 0.7 us)
Async XLA Ops:
  2.2 8.1 %copy-start.5 = (bf16[64,8192]{1,0:T(8,128)(2,1)S(1)}, bf16[64,8192]{1,0:T(8,128)(2,1)}, u32[]{:S(2)}) copy-start(bf16[64,8192]{1,0:T(8,128)(2,1)} %param.8) | copy-start | bytes 3145732
  3.5 6.8 %copy-start.1 = (bf16[4097,128]{1,0:T(8,128)(2,1)}, bf16[4097,128]{1,0:T(8,128)(2,1)S(1)}, u32[]{:S(2)}) copy-start(bf16[4097,128]{1,0:T(8,128)(2,1)S(1)} %fusion.1.refs_0_) | copy-start | bytes 3146500
  3.6 28.4 %collective-permute-start.4 = (bf16[4097,128]{1,0:T(8,128)(2,1)S(1)}, bf16[4097,128]{1,0:T(8,128)(2,1)}, u32[]{:S(2)}, u32[]{:S(2)}) collective-permute-start(bf16[4097,128]{1,0:T(8,128)(2,1)S(1)} %fusion.1.refs_0_), channel_id=1, source_target_pairs={{0,224},{32,0},{64,32},{96,64},{128,96},{160,128},{192,160},{224,1... | collective-permute-start | bytes 3146504 | tf_op jit(solution)/shard_map/ppermute | solution.py:162
  10.0 25.4 %collective-permute-start = (bf16[4097,128]{1,0:T(8,128)(2,1)S(1)}, bf16[4097,128]{1,0:T(8,128)(2,1)}, u32[]{:S(2)}, u32[]{:S(2)}) collective-permute-start(bf16[4097,128]{1,0:T(8,128)(2,1)S(1)} %fusion.1.refs_0_), channel_id=1, source_target_pairs={{0,32},{32,64},{64,96},{96,128},{128,160},{160,192},{192,224},{224... | collective-permute-start | bytes 3146504 | tf_op jit(solution)/shard_map/ppermute | solution.py:161
  31.9 24.9 %collective-permute-start.5 = (bf16[4097,128]{1,0:T(8,128)(2,1)}, bf16[4097,128]{1,0:T(8,128)(2,1)S(1)}, u32[]{:S(2)}, u32[]{:S(2)}) collective-permute-start(bf16[4097,128]{1,0:T(8,128)(2,1)} %collective-permute-done.4.refs_2_), channel_id=1, source_target_pairs={{0,224},{32,0},{64,32},{96,64},{128,96},{160,128},{192,160},{224,1... | collective-permute-start | bytes 3146504 | tf_op jit(solution)/shard_map/ppermute | solution.py:162
  35.4 24.7 %collective-permute-start.1 = (bf16[4097,128]{1,0:T(8,128)(2,1)}, bf16[4097,128]{1,0:T(8,128)(2,1)}, u32[]{:S(2)}, u32[]{:S(2)}) collective-permute-start(bf16[4097,128]{1,0:T(8,128)(2,1)} %collective-permute-done.refs_1_), channel_id=1, source_target_pairs={{0,32},{32,64},{64,96},{96,128},{128,160},{160,192},{192,224},{224... | collective-permute-start | bytes 3146504 | tf_op jit(solution)/shard_map/ppermute | solution.py:161
  35.7 1.7 %copy-start.7 = (s32[32,32]{1,0:T(8,128)S(1)}, s32[32,32]{1,0:T(8,128)}, u32[]{:S(2)}) copy-start(s32[32,32]{1,0:T(8,128)} %param.11) | copy-start | bytes 12292
  35.7 1.8 %copy-start.9 = (s32[32]{0:T(128)S(1)}, s32[32]{0:T(128)}, u32[]{:S(2)}) copy-start(s32[32]{0:T(128)} %param.13) | copy-start | bytes 388
  35.7 1.8 %copy-start.8 = (s32[32,36]{1,0:T(8,128)S(1)}, s32[32,36]{1,0:T(8,128)}, u32[]{:S(2)}) copy-start(s32[32,36]{1,0:T(8,128)} %param.12) | copy-start | bytes 13828
  56.8 27.8 %copy-start.4 = (bf16[4097,128]{1,0:T(8,128)(2,1)}, bf16[4097,128]{1,0:T(8,128)(2,1)S(1)}, u32[]{:S(2)}) copy-start(bf16[4097,128]{1,0:T(8,128)(2,1)S(1)} %collective-permute-done.5.refs_4_) | copy-start | bytes 3146500
  56.8 23.5 %collective-permute-start.6 = (bf16[4097,128]{1,0:T(8,128)(2,1)S(1)}, bf16[4097,128]{1,0:T(8,128)(2,1)S(1)}, u32[]{:S(2)}, u32[]{:S(2)}) collective-permute-start(bf16[4097,128]{1,0:T(8,128)(2,1)S(1)} %collective-permute-done.5.refs_4_), channel_id=1, source_target_pairs={{0,224},{32,0},{64,32},{96,64},{128,96},{160,128},{192,160},{224,1... | collective-permute-start | bytes 3146504 | tf_op jit(solution)/shard_map/ppermute | solution.py:162
  60.1 24.5 %collective-permute-start.2 = (bf16[4097,128]{1,0:T(8,128)(2,1)}, bf16[4097,128]{1,0:T(8,128)(2,1)S(1)}, u32[]{:S(2)}, u32[]{:S(2)}) collective-permute-start(bf16[4097,128]{1,0:T(8,128)(2,1)} %collective-permute-done.1.refs_3_), channel_id=1, source_target_pairs={{0,32},{32,64},{64,96},{96,128},{128,160},{160,192},{192,224},{224... | collective-permute-start | bytes 3146504 | tf_op jit(solution)/shard_map/ppermute | solution.py:161
  80.3 5.3 %copy-start.2 = (bf16[4097,128]{1,0:T(8,128)(2,1)}, bf16[4097,128]{1,0:T(8,128)(2,1)S(1)}, u32[]{:S(2)}) copy-start(bf16[4097,128]{1,0:T(8,128)(2,1)S(1)} %collective-permute-done.6.refs_6_) | copy-start | bytes 3146500
  81.2 11.8 %collective-permute-start.7 = (bf16[2049,128]{1,0:T(8,128)(2,1)}, bf16[2049,128]{1,0:T(8,128)(2,1)}, u32[]{:S(2)}, u32[]{:S(2)}) collective-permute-start(bf16[2049,128]{1,0:T(8,128)(2,1)} %slice.74), channel_id=1, source_target_pairs={{0,224},{32,0},{64,32},{96,64},{128,96},{160,128},{192,160},{224,1... | collective-permute-start | bytes 1573640 | tf_op jit(solution)/shard_map/ppermute | solution.py:169
  84.6 1.2 copy-start.3
  85.6 11.4 %collective-permute-start.3 = (bf16[2049,128]{1,0:T(8,128)(2,1)}, bf16[2049,128]{1,0:T(8,128)(2,1)S(1)}, u32[]{:S(2)}, u32[]{:S(2)}) collective-permute-start(bf16[2049,128]{1,0:T(8,128)(2,1)} %pad_maximum_fusion), channel_id=1, source_target_pairs={{0,32},{32,64},{64,96},{96,128},{128,160},{160,192},{192,224},{224... | collective-permute-start | bytes 1573640 | tf_op jit(solution)/shard_map/ppermute | solution.py:168
  97.0 0.8 copy-start.6
  102.4 40.1 %all-to-all-start = ((f32[64,64,128]{2,1,0:T(8,128)}), f32[64,64,128]{2,1,0:T(8,128)S(1)}, u32[]{:S(2)}, u32[]{:S(2)}) async-start(f32[64,64,128]{2,1,0:T(8,128)} %shard_map.65), calls=%async_computation | async-start | bytes 4194304 | tf_op jit(solution)/shard_map/all_to_all | solution.py:191
  142.4 1.4 copy-start

commit v10 on v9

--- a/solution.py
+++ b/solution.py
@@ -106,32 +106,45 @@
     )(positions, pat, pressure, *pieces, *extra)
 
 
-def collect_kernel(n_rows, dest_ref, r_ref, o_ref):
+def collect_kernel(n_rows, n_chunks, dest_ref, r_hbm, o_ref, buf, sem):
+    capacity = o_ref.shape[0]
+    rows_per = n_rows // n_chunks
+    copies = [
+        pltpu.make_async_copy(r_hbm.at[pl.ds(c * rows_per, rows_per)], buf.at[c], sem.at[c])
+        for c in range(n_chunks)
+    ]
+    for c in copies:
+        c.start()
     o_ref[...] = jnp.zeros_like(o_ref)
-    capacity = o_ref.shape[0]
-
-    def add_row(e, carry):
-        d = dest_ref[e]
-
-        @pl.when(d < capacity)
-        def _():
-            o_ref[d] += r_ref[e]
-
-        return carry
-
-    lax.fori_loop(0, n_rows, add_row, 0)
-
-
-def collect(dest, received, capacity):
+    for c in range(n_chunks):
+        copies[c].wait()
+
+        def add_row(e, carry):
+            d = dest_ref[c * rows_per + e]
+
+            @pl.when(d < capacity)
+            def _():
+                o_ref[d] += buf[c, e]
+
+            return carry
+
+        lax.fori_loop(0, rows_per, add_row, 0)
+
+
+def collect(dest, received, capacity, n_chunks=4):
     n_rows, time_len, block_len = received.shape
     return pl.pallas_call(
-        functools.partial(collect_kernel, n_rows),
+        functools.partial(collect_kernel, n_rows, n_chunks),
         out_shape=jax.ShapeDtypeStruct((capacity, time_len, block_len), jnp.float32),
         in_specs=[
             pl.BlockSpec(memory_space=pltpu.SMEM),
-            pl.BlockSpec(memory_space=pltpu.VMEM),
+            pl.BlockSpec(memory_space=pl.ANY),
         ],
         out_specs=pl.BlockSpec(memory_space=pltpu.VMEM),
+        scratch_shapes=[
+            pltpu.VMEM((n_chunks, n_rows // n_chunks, time_len, block_len), jnp.float32),
+            pltpu.SemaphoreType.DMA((n_chunks,)),
+        ],
     )(dest, received)
 
 
@@ -151,8 +164,9 @@
     right = [(i, (i + 1) % n_tm) for i in range(n_tm)]
     left = [(i, (i - 1) % n_tm) for i in range(n_tm)]
 
-    pat_row = jnp.zeros((1, block_len), proj_weight.dtype)
-    pat_row = pat_row.at[0, : fb_dev * kp].set(pattern[0].reshape(-1).astype(proj_weight.dtype))
+    pat_row = jnp.pad(
+        pattern[0].reshape(1, fb_dev * kp).astype(proj_weight.dtype), ((0, 0), (0, block_len - fb_dev * kp))
+    )
     own = jnp.concatenate([proj_weight[0].reshape(w_rows, block_len), pat_row], axis=0)
 
     x_r = x_l = own

time: 148 us -> 147 us (level)
    squeeze x11 -> x8, local copies, waits for them, and re-layouts: 3.03 us -> 2.76 us  [pattern_of(): rows = [pieces[i][-1, lane_at[i]:lane_at[i] + sizes[i] * kp] for i in group]]
where the time goes in v10:
time: 147 us; the launch traced here: 146 us
  waiting for transfers between devices  84.4 us (57%)
  starting transfers between devices  28.2 us (19%)
  Pallas kernels  14.4 us (10%)
  local copies, waits for them, and re-layouts  9.74 us (7%)
  other arithmetic  9.2 us (6%)
    ppermute x3, waiting for transfers between devices, body(): x_l = lax.ppermute(x_l, 'tm', left)  56.7 us
    all_to_all x1, waiting for transfers between devices, body(): lax.all_to_all(packed, 'owner', split_axis=0, concat_axis=0, tiled=True)  24.1 us
    ppermute x3, starting transfers between devices, body(): x_l = lax.ppermute(x_l, 'tm', left)  13.3 us
    all_to_all x1, starting transfers between devices, body(): lax.all_to_all(packed, 'owner', split_axis=0, concat_axis=0, tiled=True)  11.5 us
    pallas_call x2, Pallas kernels, project(): pl.pallas_call(functools.partial(project_kernel, tuple(sizes), kp, block_...  10.8 us
    pallas_call x1, Pallas kernels, collect(): pl.pallas_call(functools.partial(collect_kernel, n_rows, n_chunks), out_s...  3.66 us
    ppermute x1, starting transfers between devices, body(): h_l = lax.ppermute(x_l[h_rows:], 'tm', left)  3.41 us
    ppermute x1, waiting for transfers between devices, body(): lax.ppermute(jnp.concatenate([x_r[:h_rows], x_r[w_rows:]], axis=0), 'tm',...  3.3 us
  transfers between devices with their start and end apart: 9, of which 6 were waited for; matrix products, arithmetic and copies ran while one was open for 10% of the time, Pallas kernels for 4%

profile of v10, /device:TPU:1, one launch (start us, length us, event | category | flops | bytes accessed | tf_op | source)
XLA Modules:
  0.0 146.1 jit_solution(8684625775428859329)
XLA Ops:
  0.0 0.7 convert_element_type.34
  0.7 0.1 copy.17
  0.8 0.1 convert_element_type.35
  0.9 1.4 fusion.1.refs_0_
  2.3 6.5 %collective-permute-start.4 = (bf16[4097,128]{1,0:T(8,128)(2,1)S(1)}, bf16[4097,128]{1,0:T(8,128)(2,1)}, u32[]{:S(2)}, u32[]{:S(2)}) collective-permute-start(bf16[4097,128]{1,0:T(8,128)(2,1)S(1)} %fusion.1.refs_0_), channel_id=1, source_target_pairs={{0,224},{32,0},{64,32},{96,64},{128,96},{160,128},{192,160},{224,1... | collective-permute-start | bytes 3146504 | tf_op jit(solution)/shard_map/ppermute | solution.py:176
  9.0 0.1 stack.62
  9.2 0.6 gather_fusion
  9.9 20.7 %collective-permute-done.4.refs_2_ = bf16[4097,128]{1,0:T(8,128)(2,1)} collective-permute-done((bf16[4097,128]{1,0:T(8,128)(2,1)S(1)}, bf16[4097,128]{1,0:T(8,128)(2,1)}, u32[]{:S(2)}, u32[]{:S(2)}) %collective-permute-start.4) | collective-permute-done | bytes 1048864 | tf_op jit(solution)/shard_map/ppermute | solution.py:176
  30.6 3.5 %collective-permute-start.5 = (bf16[4097,128]{1,0:T(8,128)(2,1)}, bf16[4097,128]{1,0:T(8,128)(2,1)S(1)}, u32[]{:S(2)}, u32[]{:S(2)}) collective-permute-start(bf16[4097,128]{1,0:T(8,128)(2,1)} %collective-permute-done.4.refs_2_), channel_id=1, source_target_pairs={{0,224},{32,0},{64,32},{96,64},{128,96},{160,128},{192,160},{224,1... | collective-permute-start | bytes 3146504 | tf_op jit(solution)/shard_map/ppermute | solution.py:176
  34.2 0.1 broadcast_select_fusion
  34.3 0.1 convert_element_type.37
  34.4 0.7 slice.60.p_ref
  35.1 1.1 slice.67.p_ref
  36.2 0.7 and_reduce_fusion
  36.9 0.1 select_reduce_fusion.2
  37.0 0.2 convert_reduce_fusion.1
  37.2 18.3 %collective-permute-done.5.refs_4_ = bf16[4097,128]{1,0:T(8,128)(2,1)S(1)} collective-permute-done((bf16[4097,128]{1,0:T(8,128)(2,1)}, bf16[4097,128]{1,0:T(8,128)(2,1)S(1)}, u32[]{:S(2)}, u32[]{:S(2)}) %collective-permute-start.5) | collective-permute-done | bytes 1048864 | tf_op jit(solution)/shard_map/ppermute | solution.py:176
  55.5 3.3 %collective-permute-start.6 = (bf16[4097,128]{1,0:T(8,128)(2,1)S(1)}, bf16[4097,128]{1,0:T(8,128)(2,1)S(1)}, u32[]{:S(2)}, u32[]{:S(2)}) collective-permute-start(bf16[4097,128]{1,0:T(8,128)(2,1)S(1)} %collective-permute-done.5.refs_4_), channel_id=1, source_target_pairs={{0,224},{32,0},{64,32},{96,64},{128,96},{160,128},{192,160},{224,1... | collective-permute-start | bytes 3146504 | tf_op jit(solution)/shard_map/ppermute | solution.py:176
  58.8 0.5 multiply_add_fusion.pos_ref
  59.3 0.7 slice_bitcast_fusion.4
  60.0 0.7 slice_bitcast_fusion.5
  60.7 0.7 slice_bitcast_fusion.3
  61.3 17.6 %collective-permute-done.6.refs_6_ = bf16[4097,128]{1,0:T(8,128)(2,1)S(1)} collective-permute-done((bf16[4097,128]{1,0:T(8,128)(2,1)S(1)}, bf16[4097,128]{1,0:T(8,128)(2,1)S(1)}, u32[]{:S(2)}, u32[]{:S(2)}) %collective-permute-start.6) | collective-permute-done | bytes 1048864 | tf_op jit(solution)/shard_map/ppermute | solution.py:176
  79.0 0.9 slice.58
  79.9 3.4 %collective-permute-start.7 = (bf16[2049,128]{1,0:T(8,128)(2,1)}, bf16[2049,128]{1,0:T(8,128)(2,1)}, u32[]{:S(2)}, u32[]{:S(2)}) collective-permute-start(bf16[2049,128]{1,0:T(8,128)(2,1)} %slice.58), channel_id=1, source_target_pairs={{0,224},{32,0},{64,32},{96,64},{128,96},{160,128},{192,160},{224,1... | collective-permute-start | bytes 1573640 | tf_op jit(solution)/shard_map/ppermute | solution.py:183
  83.3 1.0 pad_maximum_fusion
  84.3 0.2 copy-done.3
  84.5 0.1 concatenate.36
  84.6 0.6 convert_element_type.38.pat_ref
  85.2 6.3 %shard_map.64.refs_2_ = f32[64,64,128]{2,1,0:T(8,128)} custom-call(s32[32]{0:T(128)} %multiply_add_fusion.pos_ref, s32[224]{0:T(256)} %convert_element_type.38.pat_ref, bf16[64,7168]{1,0:T(8,128)(2,1)} %slice.67.p_ref, bf16[4097,128]{1,0:T(8,128)(2,1)} %copy-done.1, bf16[4097,128]{1,0:T(8,128)(2,1)} %collective-permute-done.refs_1_, ...), custom_call_target="tpu_custom_call" | custom-call | flops 469762048 | bytes 10354688 | tf_op jit(solution)/shard_map/pallas_call | solution.py:85
  91.4 0.3 collective-permute-done.7.refs_1_
  91.7 0.7 slice_bitcast_fusion.6
  92.4 3.3 %collective-permute-done.3.refs_0_ = bf16[2049,128]{1,0:T(8,128)(2,1)S(1)} collective-permute-done((bf16[2049,128]{1,0:T(8,128)(2,1)}, bf16[2049,128]{1,0:T(8,128)(2,1)S(1)}, u32[]{:S(2)}, u32[]{:S(2)}) %collective-permute-start.3) | collective-permute-done | bytes 524576 | tf_op jit(solution)/shard_map/ppermute | solution.py:182
  95.7 0.8 maximum_convert_fusion.pat_ref
  96.5 4.5 %shard_map.65 = f32[64,64,128]{2,1,0:T(8,128)} custom-call(s32[32]{0:T(128)} %multiply_add_fusion.pos_ref, s32[32]{0:T(128)} %maximum_convert_fusion.pat_ref, bf16[64,1024]{1,0:T(8,128)(2,1)} %slice.60.p_ref, bf16[2049,128]{1,0:T(8,128)(2,1)} %copy-done.6, bf16[2049,128]{1,0:T(8,128)(2,1)} %collective-permute-done.7.refs_1_, f32[64,64,128]{2,1,0:T(8,128)} %shard_map.64.refs_2_), custom_call_target="tpu_custom_call" | custom-call | flops 67108864 | bytes 5373952 | tf_op jit(solution)/shard_map/pallas_call | solution.py:85
  101.1 11.5 %all-to-all-start = ((f32[64,64,128]{2,1,0:T(8,128)}), f32[64,64,128]{2,1,0:T(8,128)S(1)}, u32[]{:S(2)}, u32[]{:S(2)}) async-start(f32[64,64,128]{2,1,0:T(8,128)} %shard_map.65), calls=%async_computation | async-start | bytes 4194304 | tf_op jit(solution)/shard_map/all_to_all | solution.py:205
  112.5 0.6 dynamic_slice.10
  113.1 0.6 iota_compare_fusion.4
  113.8 0.8 fusion.2
  114.6 0.6 convert_reduce_fusion
  115.2 0.1 fusion.4
  115.4 0.8 select_reduce_fusion
  116.1 0.1 select_reduce_fusion.1
  116.3 0.1 copy.16
  116.4 0.6 select_n.81.dest_ref
  117.0 24.1 %all-to-all-done.r_hbm = f32[64,64,128]{2,1,0:T(8,128)S(1)} async-done(((f32[64,64,128]{2,1,0:T(8,128)}), f32[64,64,128]{2,1,0:T(8,128)S(1)}, u32[]{:S(2)}, u32[]{:S(2)}) %all-to-all-start) | async-done | bytes 2097184 | tf_op jit(solution)/shard_map/all_to_all | solution.py:205
  141.1 1.3 copy-done
  142.5 3.7 %shard_map.66 = f32[36,64,128]{2,1,0:T(8,128)} custom-call(s32[64]{0:T(128)} %select_n.81.dest_ref, f32[64,64,128]{2,1,0:T(8,128)} %copy-done), custom_call_target="tpu_custom_call" | custom-call | tf_op jit(solution)/shard_map/pallas_call | solution.py:136
  (44 shorter events, 0.6 us)
Async XLA Ops:
  0.9 8.1 %copy-start.5 = (bf16[64,8192]{1,0:T(8,128)(2,1)S(1)}, bf16[64,8192]{1,0:T(8,128)(2,1)}, u32[]{:S(2)}) copy-start(bf16[64,8192]{1,0:T(8,128)(2,1)} %param.6) | copy-start | bytes 3145732
  2.3 6.8 %copy-start.1 = (bf16[4097,128]{1,0:T(8,128)(2,1)}, bf16[4097,128]{1,0:T(8,128)(2,1)S(1)}, u32[]{:S(2)}) copy-start(bf16[4097,128]{1,0:T(8,128)(2,1)S(1)} %fusion.1.refs_0_) | copy-start | bytes 3146500
  2.3 28.4 %collective-permute-start.4 = (bf16[4097,128]{1,0:T(8,128)(2,1)S(1)}, bf16[4097,128]{1,0:T(8,128)(2,1)}, u32[]{:S(2)}, u32[]{:S(2)}) collective-permute-start(bf16[4097,128]{1,0:T(8,128)(2,1)S(1)} %fusion.1.refs_0_), channel_id=1, source_target_pairs={{0,224},{32,0},{64,32},{96,64},{128,96},{160,128},{192,160},{224,1... | collective-permute-start | bytes 3146504 | tf_op jit(solution)/shard_map/ppermute | solution.py:176
  8.7 25.4 %collective-permute-start = (bf16[4097,128]{1,0:T(8,128)(2,1)S(1)}, bf16[4097,128]{1,0:T(8,128)(2,1)}, u32[]{:S(2)}, u32[]{:S(2)}) collective-permute-start(bf16[4097,128]{1,0:T(8,128)(2,1)S(1)} %fusion.1.refs_0_), channel_id=1, source_target_pairs={{0,32},{32,64},{64,96},{96,128},{128,160},{160,192},{192,224},{224... | collective-permute-start | bytes 3146504 | tf_op jit(solution)/shard_map/ppermute | solution.py:175
  30.6 24.9 %collective-permute-start.5 = (bf16[4097,128]{1,0:T(8,128)(2,1)}, bf16[4097,128]{1,0:T(8,128)(2,1)S(1)}, u32[]{:S(2)}, u32[]{:S(2)}) collective-permute-start(bf16[4097,128]{1,0:T(8,128)(2,1)} %collective-permute-done.4.refs_2_), channel_id=1, source_target_pairs={{0,224},{32,0},{64,32},{96,64},{128,96},{160,128},{192,160},{224,1... | collective-permute-start | bytes 3146504 | tf_op jit(solution)/shard_map/ppermute | solution.py:176
  34.2 24.7 %collective-permute-start.1 = (bf16[4097,128]{1,0:T(8,128)(2,1)}, bf16[4097,128]{1,0:T(8,128)(2,1)}, u32[]{:S(2)}, u32[]{:S(2)}) collective-permute-start(bf16[4097,128]{1,0:T(8,128)(2,1)} %collective-permute-done.refs_1_), channel_id=1, source_target_pairs={{0,32},{32,64},{64,96},{96,128},{128,160},{160,192},{192,224},{224... | collective-permute-start | bytes 3146504 | tf_op jit(solution)/shard_map/ppermute | solution.py:175
  34.4 1.7 %copy-start.7 = (s32[32,32]{1,0:T(8,128)S(1)}, s32[32,32]{1,0:T(8,128)}, u32[]{:S(2)}) copy-start(s32[32,32]{1,0:T(8,128)} %param.9) | copy-start | bytes 12292
  34.4 1.8 %copy-start.9 = (s32[32]{0:T(128)S(1)}, s32[32]{0:T(128)}, u32[]{:S(2)}) copy-start(s32[32]{0:T(128)} %param.11) | copy-start | bytes 388
  34.4 1.8 %copy-start.8 = (s32[32,36]{1,0:T(8,128)S(1)}, s32[32,36]{1,0:T(8,128)}, u32[]{:S(2)}) copy-start(s32[32,36]{1,0:T(8,128)} %param.10) | copy-start | bytes 13828
  55.5 27.8 %copy-start.4 = (bf16[4097,128]{1,0:T(8,128)(2,1)}, bf16[4097,128]{1,0:T(8,128)(2,1)S(1)}, u32[]{:S(2)}) copy-start(bf16[4097,128]{1,0:T(8,128)(2,1)S(1)} %collective-permute-done.5.refs_4_) | copy-start | bytes 3146500
  55.5 23.5 %collective-permute-start.6 = (bf16[4097,128]{1,0:T(8,128)(2,1)S(1)}, bf16[4097,128]{1,0:T(8,128)(2,1)S(1)}, u32[]{:S(2)}, u32[]{:S(2)}) collective-permute-start(bf16[4097,128]{1,0:T(8,128)(2,1)S(1)} %collective-permute-done.5.refs_4_), channel_id=1, source_target_pairs={{0,224},{32,0},{64,32},{96,64},{128,96},{160,128},{192,160},{224,1... | collective-permute-start | bytes 3146504 | tf_op jit(solution)/shard_map/ppermute | solution.py:176
  58.8 24.5 %collective-permute-start.2 = (bf16[4097,128]{1,0:T(8,128)(2,1)}, bf16[4097,128]{1,0:T(8,128)(2,1)S(1)}, u32[]{:S(2)}, u32[]{:S(2)}) collective-permute-start(bf16[4097,128]{1,0:T(8,128)(2,1)} %collective-permute-done.1.refs_3_), channel_id=1, source_target_pairs={{0,32},{32,64},{64,96},{96,128},{128,160},{160,192},{192,224},{224... | collective-permute-start | bytes 3146504 | tf_op jit(solution)/shard_map/ppermute | solution.py:175
  79.0 5.3 %copy-start.2 = (bf16[4097,128]{1,0:T(8,128)(2,1)}, bf16[4097,128]{1,0:T(8,128)(2,1)S(1)}, u32[]{:S(2)}) copy-start(bf16[4097,128]{1,0:T(8,128)(2,1)S(1)} %collective-permute-done.6.refs_6_) | copy-start | bytes 3146500
  79.9 11.8 %collective-permute-start.7 = (bf16[2049,128]{1,0:T(8,128)(2,1)}, bf16[2049,128]{1,0:T(8,128)(2,1)}, u32[]{:S(2)}, u32[]{:S(2)}) collective-permute-start(bf16[2049,128]{1,0:T(8,128)(2,1)} %slice.58), channel_id=1, source_target_pairs={{0,224},{32,0},{64,32},{96,64},{128,96},{160,128},{192,160},{224,1... | collective-permute-start | bytes 1573640 | tf_op jit(solution)/shard_map/ppermute | solution.py:183
  83.3 1.2 copy-start.3
  84.3 11.4 %collective-permute-start.3 = (bf16[2049,128]{1,0:T(8,128)(2,1)}, bf16[2049,128]{1,0:T(8,128)(2,1)S(1)}, u32[]{:S(2)}, u32[]{:S(2)}) collective-permute-start(bf16[2049,128]{1,0:T(8,128)(2,1)} %pad_maximum_fusion), channel_id=1, source_target_pairs={{0,32},{32,64},{64,96},{96,128},{128,160},{160,192},{192,224},{224... | collective-permute-start | bytes 1573640 | tf_op jit(solution)/shard_map/ppermute | solution.py:182
  95.7 0.8 copy-start.6
  101.1 40.1 %all-to-all-start = ((f32[64,64,128]{2,1,0:T(8,128)}), f32[64,64,128]{2,1,0:T(8,128)S(1)}, u32[]{:S(2)}, u32[]{:S(2)}) async-start(f32[64,64,128]{2,1,0:T(8,128)} %shard_map.65), calls=%async_computation | async-start | bytes 4194304 | tf_op jit(solution)/shard_map/all_to_all | solution.py:205
  141.1 1.4 copy-start

commit v11 on v10

--- a/solution.py
+++ b/solution.py
@@ -44,7 +44,7 @@
     n = len(sizes)
     w_refs = refs[:n]
     if has_acc:
-        acc_ref, o_ref, buf, sem = refs[n:]
+        acc_hbm, o_ref, buf, sem = refs[n:]
     else:
         o_ref, buf, sem = refs[n:]
     rows_of = [sizes[q] * kp * block_len for q in range(n)]
@@ -52,10 +52,13 @@
         pltpu.make_async_copy(w_refs[q].at[pl.ds(0, rows_of[q])], buf.at[q, pl.ds(0, rows_of[q])], sem.at[q])
         for q in range(n)
     ]
+    if has_acc:
+        acc_copy = pltpu.make_async_copy(acc_hbm, o_ref, sem.at[n])
+        acc_copy.start()
     for c in copies:
         c.start()
     if has_acc:
-        o_ref[...] = acc_ref[...]
+        acc_copy.wait()
     else:
         o_ref[...] = jnp.zeros_like(o_ref)
     base = 0
@@ -91,11 +94,11 @@
             pl.BlockSpec(memory_space=pltpu.VMEM),
         ]
         + [pl.BlockSpec(memory_space=pl.ANY)] * len(pieces)
-        + [pl.BlockSpec(memory_space=pltpu.VMEM)] * len(extra),
+        + [pl.BlockSpec(memory_space=pl.ANY)] * len(extra),
         out_specs=pl.BlockSpec(memory_space=pltpu.VMEM),
         scratch_shapes=[
             pltpu.VMEM((len(pieces), max(sizes) * kp * block_len, block_len), pieces[0].dtype),
-            pltpu.SemaphoreType.DMA((len(pieces),)),
+            pltpu.SemaphoreType.DMA((len(pieces) + 1,)),
         ],
         cost_estimate=pl.CostEstimate(
             flops=2 * face_blocks * kp * time_len * block_len * block_len,
@@ -119,16 +122,12 @@
     for c in range(n_chunks):
         copies[c].wait()
 
-        def add_row(e, carry):
+        for e in range(rows_per):
             d = dest_ref[c * rows_per + e]
 
             @pl.when(d < capacity)
             def _():
                 o_ref[d] += buf[c, e]
-
-            return carry
-
-        lax.fori_loop(0, rows_per, add_row, 0)
 
 
 def collect(dest, received, capacity, n_chunks=4):

time: 147 us -> 146 us (level)
  no operation moved by 1% of the time
where the time goes in v11:
time: 146 us
  waiting for transfers between devices  84.3 us (58%)
  starting transfers between devices  28.2 us (19%)
  Pallas kernels  14 us (10%)
  local copies, waits for them, and re-layouts  9.74 us (7%)
  other arithmetic  9.2 us (6%)
    ppermute x3, waiting for transfers between devices, body(): x_l = lax.ppermute(x_l, 'tm', left)  56.7 us
    all_to_all x1, waiting for transfers between devices, body(): lax.all_to_all(packed, 'owner', split_axis=0, concat_axis=0, tiled=True)  24.1 us
    ppermute x3, starting transfers between devices, body(): x_l = lax.ppermute(x_l, 'tm', left)  13.3 us
    all_to_all x1, starting transfers between devices, body(): lax.all_to_all(packed, 'owner', split_axis=0, concat_axis=0, tiled=True)  11.5 us
    pallas_call x2, Pallas kernels, project(): pl.pallas_call(functools.partial(project_kernel, tuple(sizes), kp, block_...  10.7 us
    ppermute x1, starting transfers between devices, body(): h_l = lax.ppermute(x_l[h_rows:], 'tm', left)  3.41 us
    pallas_call x1, Pallas kernels, collect(): pl.pallas_call(functools.partial(collect_kernel, n_rows, n_chunks), out_s...  3.35 us
    ppermute x1, waiting for transfers between devices, body(): lax.ppermute(jnp.concatenate([x_r[:h_rows], x_r[w_rows:]], axis=0), 'tm',...  3.3 us
  transfers between devices with their start and end apart: 9, of which 6 were waited for; matrix products, arithmetic and copies ran while one was open for 10% of the time, Pallas kernels for 4%

profile of v11, /device:TPU:1, one launch (start us, length us, event | category | flops | bytes accessed | tf_op | source)
XLA Modules:
  0.0 145.8 jit_solution(10104491395842166806)
XLA Ops:
  0.0 0.7 convert_element_type.34
  0.7 0.1 copy.17
  0.8 0.1 convert_element_type.35
  0.9 1.4 fusion.1.refs_0_
  2.3 6.5 %collective-permute-start.4 = (bf16[4097,128]{1,0:T(8,128)(2,1)S(1)}, bf16[4097,128]{1,0:T(8,128)(2,1)}, u32[]{:S(2)}, u32[]{:S(2)}) collective-permute-start(bf16[4097,128]{1,0:T(8,128)(2,1)S(1)} %fusion.1.refs_0_), channel_id=1, source_target_pairs={{0,224},{32,0},{64,32},{96,64},{128,96},{160,128},{192,160},{224,1... | collective-permute-start | bytes 3146504 | tf_op jit(solution)/shard_map/ppermute | solution.py:175
  9.0 0.1 stack.62
  9.2 0.6 gather_fusion
  9.9 20.7 %collective-permute-done.4.refs_2_ = bf16[4097,128]{1,0:T(8,128)(2,1)} collective-permute-done((bf16[4097,128]{1,0:T(8,128)(2,1)S(1)}, bf16[4097,128]{1,0:T(8,128)(2,1)}, u32[]{:S(2)}, u32[]{:S(2)}) %collective-permute-start.4) | collective-permute-done | bytes 1048864 | tf_op jit(solution)/shard_map/ppermute | solution.py:175
  30.6 3.5 %collective-permute-start.5 = (bf16[4097,128]{1,0:T(8,128)(2,1)}, bf16[4097,128]{1,0:T(8,128)(2,1)S(1)}, u32[]{:S(2)}, u32[]{:S(2)}) collective-permute-start(bf16[4097,128]{1,0:T(8,128)(2,1)} %collective-permute-done.4.refs_2_), channel_id=1, source_target_pairs={{0,224},{32,0},{64,32},{96,64},{128,96},{160,128},{192,160},{224,1... | collective-permute-start | bytes 3146504 | tf_op jit(solution)/shard_map/ppermute | solution.py:175
  34.2 0.1 broadcast_select_fusion
  34.3 0.1 convert_element_type.37
  34.4 0.7 slice.60.p_ref
  35.1 1.1 slice.67.p_ref
  36.2 0.7 and_reduce_fusion
  36.9 0.1 select_reduce_fusion.2
  37.0 0.2 convert_reduce_fusion.1
  37.2 18.3 %collective-permute-done.5.refs_4_ = bf16[4097,128]{1,0:T(8,128)(2,1)S(1)} collective-permute-done((bf16[4097,128]{1,0:T(8,128)(2,1)}, bf16[4097,128]{1,0:T(8,128)(2,1)S(1)}, u32[]{:S(2)}, u32[]{:S(2)}) %collective-permute-start.5) | collective-permute-done | bytes 1048864 | tf_op jit(solution)/shard_map/ppermute | solution.py:175
  55.5 3.3 %collective-permute-start.6 = (bf16[4097,128]{1,0:T(8,128)(2,1)S(1)}, bf16[4097,128]{1,0:T(8,128)(2,1)S(1)}, u32[]{:S(2)}, u32[]{:S(2)}) collective-permute-start(bf16[4097,128]{1,0:T(8,128)(2,1)S(1)} %collective-permute-done.5.refs_4_), channel_id=1, source_target_pairs={{0,224},{32,0},{64,32},{96,64},{128,96},{160,128},{192,160},{224,1... | collective-permute-start | bytes 3146504 | tf_op jit(solution)/shard_map/ppermute | solution.py:175
  58.8 0.5 multiply_add_fusion.pos_ref
  59.3 0.7 slice_bitcast_fusion.4
  60.0 0.7 slice_bitcast_fusion.5
  60.7 0.7 slice_bitcast_fusion.3
  61.3 17.6 %collective-permute-done.6.refs_6_ = bf16[4097,128]{1,0:T(8,128)(2,1)S(1)} collective-permute-done((bf16[4097,128]{1,0:T(8,128)(2,1)S(1)}, bf16[4097,128]{1,0:T(8,128)(2,1)S(1)}, u32[]{:S(2)}, u32[]{:S(2)}) %collective-permute-start.6) | collective-permute-done | bytes 1048864 | tf_op jit(solution)/shard_map/ppermute | solution.py:175
  79.0 0.9 slice.58
  79.9 3.4 %collective-permute-start.7 = (bf16[2049,128]{1,0:T(8,128)(2,1)}, bf16[2049,128]{1,0:T(8,128)(2,1)}, u32[]{:S(2)}, u32[]{:S(2)}) collective-permute-start(bf16[2049,128]{1,0:T(8,128)(2,1)} %slice.58), channel_id=1, source_target_pairs={{0,224},{32,0},{64,32},{96,64},{128,96},{160,128},{192,160},{224,1... | collective-permute-start | bytes 1573640 | tf_op jit(solution)/shard_map/ppermute | solution.py:182
  83.3 1.0 pad_maximum_fusion
  84.3 0.2 copy-done.3
  84.5 0.1 concatenate.36
  84.6 0.6 convert_element_type.38.pat_ref
  85.2 6.3 %shard_map.64.refs_2_ = f32[64,64,128]{2,1,0:T(8,128)} custom-call(s32[32]{0:T(128)} %multiply_add_fusion.pos_ref, s32[224]{0:T(256)} %convert_element_type.38.pat_ref, bf16[64,7168]{1,0:T(8,128)(2,1)} %slice.67.p_ref, bf16[4097,128]{1,0:T(8,128)(2,1)} %copy-done.1, bf16[4097,128]{1,0:T(8,128)(2,1)} %collective-permute-done.refs_1_, ...), custom_call_target="tpu_custom_call" | custom-call | flops 469762048 | bytes 10354688 | tf_op jit(solution)/shard_map/pallas_call | solution.py:88
  91.4 0.3 collective-permute-done.7.refs_1_
  91.7 0.7 slice_bitcast_fusion.6
  92.4 3.3 %collective-permute-done.3.refs_0_ = bf16[2049,128]{1,0:T(8,128)(2,1)S(1)} collective-permute-done((bf16[2049,128]{1,0:T(8,128)(2,1)}, bf16[2049,128]{1,0:T(8,128)(2,1)S(1)}, u32[]{:S(2)}, u32[]{:S(2)}) %collective-permute-start.3) | collective-permute-done | bytes 524576 | tf_op jit(solution)/shard_map/ppermute | solution.py:181
  95.7 0.8 maximum_convert_fusion.pat_ref
  96.5 4.4 %shard_map.65 = f32[64,64,128]{2,1,0:T(8,128)} custom-call(s32[32]{0:T(128)} %multiply_add_fusion.pos_ref, s32[32]{0:T(128)} %maximum_convert_fusion.pat_ref, bf16[64,1024]{1,0:T(8,128)(2,1)} %slice.60.p_ref, bf16[2049,128]{1,0:T(8,128)(2,1)} %copy-done.6, bf16[2049,128]{1,0:T(8,128)(2,1)} %collective-permute-done.7.refs_1_, f32[64,64,128]{2,1,0:T(8,128)} %shard_map.64.refs_2_), custom_call_target="tpu_custom_call" | custom-call | flops 67108864 | bytes 5373952 | tf_op jit(solution)/shard_map/pallas_call | solution.py:88
  100.9 11.5 %all-to-all-start = ((f32[64,64,128]{2,1,0:T(8,128)}), f32[64,64,128]{2,1,0:T(8,128)S(1)}, u32[]{:S(2)}, u32[]{:S(2)}) async-start(f32[64,64,128]{2,1,0:T(8,128)} %shard_map.65), calls=%async_computation | async-start | bytes 4194304 | tf_op jit(solution)/shard_map/all_to_all | solution.py:204
  112.4 0.6 dynamic_slice.10
  113.0 0.6 iota_compare_fusion.4
  113.7 0.8 fusion.2
  114.5 0.6 convert_reduce_fusion
  115.1 0.1 fusion.4
  115.2 0.8 select_reduce_fusion
  116.0 0.1 select_reduce_fusion.1
  116.1 0.1 copy.16
  116.2 0.6 select_n.81.dest_ref
  116.9 24.1 %all-to-all-done.r_hbm = f32[64,64,128]{2,1,0:T(8,128)S(1)} async-done(((f32[64,64,128]{2,1,0:T(8,128)}), f32[64,64,128]{2,1,0:T(8,128)S(1)}, u32[]{:S(2)}, u32[]{:S(2)}) %all-to-all-start) | async-done | bytes 2097184 | tf_op jit(solution)/shard_map/all_to_all | solution.py:204
  141.0 1.3 copy-done
  142.3 3.4 %shard_map.66 = f32[36,64,128]{2,1,0:T(8,128)} custom-call(s32[64]{0:T(128)} %select_n.81.dest_ref, f32[64,64,128]{2,1,0:T(8,128)} %copy-done), custom_call_target="tpu_custom_call" | custom-call | tf_op jit(solution)/shard_map/pallas_call | solution.py:135
  (44 shorter events, 0.6 us)
Async XLA Ops:
  0.9 8.1 %copy-start.5 = (bf16[64,8192]{1,0:T(8,128)(2,1)S(1)}, bf16[64,8192]{1,0:T(8,128)(2,1)}, u32[]{:S(2)}) copy-start(bf16[64,8192]{1,0:T(8,128)(2,1)} %param.6) | copy-start | bytes 3145732
  2.3 6.8 %copy-start.1 = (bf16[4097,128]{1,0:T(8,128)(2,1)}, bf16[4097,128]{1,0:T(8,128)(2,1)S(1)}, u32[]{:S(2)}) copy-start(bf16[4097,128]{1,0:T(8,128)(2,1)S(1)} %fusion.1.refs_0_) | copy-start | bytes 3146500
  2.3 28.4 %collective-permute-start.4 = (bf16[4097,128]{1,0:T(8,128)(2,1)S(1)}, bf16[4097,128]{1,0:T(8,128)(2,1)}, u32[]{:S(2)}, u32[]{:S(2)}) collective-permute-start(bf16[4097,128]{1,0:T(8,128)(2,1)S(1)} %fusion.1.refs_0_), channel_id=1, source_target_pairs={{0,224},{32,0},{64,32},{96,64},{128,96},{160,128},{192,160},{224,1... | collective-permute-start | bytes 3146504 | tf_op jit(solution)/shard_map/ppermute | solution.py:175
  8.7 25.4 %collective-permute-start = (bf16[4097,128]{1,0:T(8,128)(2,1)S(1)}, bf16[4097,128]{1,0:T(8,128)(2,1)}, u32[]{:S(2)}, u32[]{:S(2)}) collective-permute-start(bf16[4097,128]{1,0:T(8,128)(2,1)S(1)} %fusion.1.refs_0_), channel_id=1, source_target_pairs={{0,32},{32,64},{64,96},{96,128},{128,160},{160,192},{192,224},{224... | collective-permute-start | bytes 3146504 | tf_op jit(solution)/shard_map/ppermute | solution.py:174
  30.6 24.9 %collective-permute-start.5 = (bf16[4097,128]{1,0:T(8,128)(2,1)}, bf16[4097,128]{1,0:T(8,128)(2,1)S(1)}, u32[]{:S(2)}, u32[]{:S(2)}) collective-permute-start(bf16[4097,128]{1,0:T(8,128)(2,1)} %collective-permute-done.4.refs_2_), channel_id=1, source_target_pairs={{0,224},{32,0},{64,32},{96,64},{128,96},{160,128},{192,160},{224,1... | collective-permute-start | bytes 3146504 | tf_op jit(solution)/shard_map/ppermute | solution.py:175
  34.2 24.7 %collective-permute-start.1 = (bf16[4097,128]{1,0:T(8,128)(2,1)}, bf16[4097,128]{1,0:T(8,128)(2,1)}, u32[]{:S(2)}, u32[]{:S(2)}) collective-permute-start(bf16[4097,128]{1,0:T(8,128)(2,1)} %collective-permute-done.refs_1_), channel_id=1, source_target_pairs={{0,32},{32,64},{64,96},{96,128},{128,160},{160,192},{192,224},{224... | collective-permute-start | bytes 3146504 | tf_op jit(solution)/shard_map/ppermute | solution.py:174
  34.4 1.7 %copy-start.7 = (s32[32,32]{1,0:T(8,128)S(1)}, s32[32,32]{1,0:T(8,128)}, u32[]{:S(2)}) copy-start(s32[32,32]{1,0:T(8,128)} %param.9) | copy-start | bytes 12292
  34.4 1.8 %copy-start.9 = (s32[32]{0:T(128)S(1)}, s32[32]{0:T(128)}, u32[]{:S(2)}) copy-start(s32[32]{0:T(128)} %param.11) | copy-start | bytes 388
  34.4 1.8 %copy-start.8 = (s32[32,36]{1,0:T(8,128)S(1)}, s32[32,36]{1,0:T(8,128)}, u32[]{:S(2)}) copy-start(s32[32,36]{1,0:T(8,128)} %param.10) | copy-start | bytes 13828
  55.5 27.8 %copy-start.4 = (bf16[4097,128]{1,0:T(8,128)(2,1)}, bf16[4097,128]{1,0:T(8,128)(2,1)S(1)}, u32[]{:S(2)}) copy-start(bf16[4097,128]{1,0:T(8,128)(2,1)S(1)} %collective-permute-done.5.refs_4_) | copy-start | bytes 3146500
  55.5 23.5 %collective-permute-start.6 = (bf16[4097,128]{1,0:T(8,128)(2,1)S(1)}, bf16[4097,128]{1,0:T(8,128)(2,1)S(1)}, u32[]{:S(2)}, u32[]{:S(2)}) collective-permute-start(bf16[4097,128]{1,0:T(8,128)(2,1)S(1)} %collective-permute-done.5.refs_4_), channel_id=1, source_target_pairs={{0,224},{32,0},{64,32},{96,64},{128,96},{160,128},{192,160},{224,1... | collective-permute-start | bytes 3146504 | tf_op jit(solution)/shard_map/ppermute | solution.py:175
  58.8 24.5 %collective-permute-start.2 = (bf16[4097,128]{1,0:T(8,128)(2,1)}, bf16[4097,128]{1,0:T(8,128)(2,1)S(1)}, u32[]{:S(2)}, u32[]{:S(2)}) collective-permute-start(bf16[4097,128]{1,0:T(8,128)(2,1)} %collective-permute-done.1.refs_3_), channel_id=1, source_target_pairs={{0,32},{32,64},{64,96},{96,128},{128,160},{160,192},{192,224},{224... | collective-permute-start | bytes 3146504 | tf_op jit(solution)/shard_map/ppermute | solution.py:174
  79.0 5.3 %copy-start.2 = (bf16[4097,128]{1,0:T(8,128)(2,1)}, bf16[4097,128]{1,0:T(8,128)(2,1)S(1)}, u32[]{:S(2)}) copy-start(bf16[4097,128]{1,0:T(8,128)(2,1)S(1)} %collective-permute-done.6.refs_6_) | copy-start | bytes 3146500
  79.9 11.8 %collective-permute-start.7 = (bf16[2049,128]{1,0:T(8,128)(2,1)}, bf16[2049,128]{1,0:T(8,128)(2,1)}, u32[]{:S(2)}, u32[]{:S(2)}) collective-permute-start(bf16[2049,128]{1,0:T(8,128)(2,1)} %slice.58), channel_id=1, source_target_pairs={{0,224},{32,0},{64,32},{96,64},{128,96},{160,128},{192,160},{224,1... | collective-permute-start | bytes 1573640 | tf_op jit(solution)/shard_map/ppermute | solution.py:182
  83.3 1.2 copy-start.3
  84.3 11.4 %collective-permute-start.3 = (bf16[2049,128]{1,0:T(8,128)(2,1)}, bf16[2049,128]{1,0:T(8,128)(2,1)S(1)}, u32[]{:S(2)}, u32[]{:S(2)}) collective-permute-start(bf16[2049,128]{1,0:T(8,128)(2,1)} %pad_maximum_fusion), channel_id=1, source_target_pairs={{0,32},{32,64},{64,96},{96,128},{128,160},{160,192},{192,224},{224... | collective-permute-start | bytes 1573640 | tf_op jit(solution)/shard_map/ppermute | solution.py:181
  95.7 0.8 copy-start.6
  100.9 40.0 %all-to-all-start = ((f32[64,64,128]{2,1,0:T(8,128)}), f32[64,64,128]{2,1,0:T(8,128)S(1)}, u32[]{:S(2)}, u32[]{:S(2)}) async-start(f32[64,64,128]{2,1,0:T(8,128)} %shard_map.65), calls=%async_computation | async-start | bytes 4194304 | tf_op jit(solution)/shard_map/all_to_all | solution.py:204
  141.0 1.4 copy-start

commit v12 on v11

--- a/solution.py
+++ b/solution.py
@@ -203,7 +203,11 @@
                      [sizes[i] for i in tail], kp, n_pos, 0, packed)
     received = lax.all_to_all(packed, "owner", split_axis=0, concat_axis=0, tiled=True)
     dest = receive_slots(panel_list, owner_list, owner_count, own_index, slot_count)
-    return collect(dest, received, capacity)
+    slots = jnp.arange(capacity, dtype=jnp.int32)
+    onehot = (slots[:, None] == dest[None, :]).astype(jnp.float32)
+    return jnp.einsum(
+        "ce,etb->ctb", onehot, received, precision=lax.Precision.HIGHEST, preferred_element_type=jnp.float32
+    )
 
 
 def solution(mesh):

time: 146 us -> 145 us (level)
  Pallas kernels: 14 us -> 10.6 us
  matrix products: 0 us -> 2.18 us
    pallas_call x1 -> x0, Pallas kernels: 3.35 us -> none  [collect(): pl.pallas_call(functools.partial(collect_kernel, n_rows, n_chunks), out_s...]
    dot_general x0 -> x1, matrix products: none -> 2.18 us  [body(): jnp.einsum('ce,etb->ctb', onehot, received, precision=lax.Precision.HIGHE...]
where the time goes in v12:
time: 145 us; the launch traced here: 144 us
  waiting for transfers between devices  84.9 us (59%)
  starting transfers between devices  28.2 us (19%)
  Pallas kernels  10.6 us (7%)
  other arithmetic  9.2 us (6%)
  local copies, waits for them, and re-layouts  9.09 us (6%)
  matrix products  2.18 us (2%)
    ppermute x3, waiting for transfers between devices, body(): x_l = lax.ppermute(x_l, 'tm', left)  56.7 us
    all_to_all x1, waiting for transfers between devices, body(): lax.all_to_all(packed, 'owner', split_axis=0, concat_axis=0, tiled=True)  24.6 us
    ppermute x3, starting transfers between devices, body(): x_l = lax.ppermute(x_l, 'tm', left)  13.3 us
    all_to_all x1, starting transfers between devices, body(): lax.all_to_all(packed, 'owner', split_axis=0, concat_axis=0, tiled=True)  11.5 us
    pallas_call x2, Pallas kernels, project(): pl.pallas_call(functools.partial(project_kernel, tuple(sizes), kp, block_...  10.6 us
    ppermute x1, starting transfers between devices, body(): h_l = lax.ppermute(x_l[h_rows:], 'tm', left)  3.41 us
    ppermute x1, waiting for transfers between devices, body(): lax.ppermute(jnp.concatenate([x_r[:h_rows], x_r[w_rows:]], axis=0), 'tm',...  3.3 us
  transfers between devices with their start and end apart: 9, of which 6 were waited for; matrix products, arithmetic and copies ran while one was open for 10% of the time, Pallas kernels for 4%

profile of v12, /device:TPU:1, one launch (start us, length us, event | category | flops | bytes accessed | tf_op | source)
XLA Modules:
  0.0 144.4 jit_solution(18033097698080868036)
XLA Ops:
  0.0 0.7 convert_element_type.35
  0.7 0.1 copy.23
  0.8 0.1 convert_element_type.36
  0.9 1.4 fusion.3.refs_0_
  2.3 6.5 %collective-permute-start.4 = (bf16[4097,128]{1,0:T(8,128)(2,1)S(1)}, bf16[4097,128]{1,0:T(8,128)(2,1)}, u32[]{:S(2)}, u32[]{:S(2)}) collective-permute-start(bf16[4097,128]{1,0:T(8,128)(2,1)S(1)} %fusion.3.refs_0_), channel_id=1, source_target_pairs={{0,224},{32,0},{64,32},{96,64},{128,96},{160,128},{192,160},{224,1... | collective-permute-start | bytes 3146504 | tf_op jit(solution)/shard_map/ppermute | solution.py:175
  9.0 0.1 stack.62
  9.2 0.6 gather_fusion
  9.9 20.7 %collective-permute-done.4.refs_2_ = bf16[4097,128]{1,0:T(8,128)(2,1)} collective-permute-done((bf16[4097,128]{1,0:T(8,128)(2,1)S(1)}, bf16[4097,128]{1,0:T(8,128)(2,1)}, u32[]{:S(2)}, u32[]{:S(2)}) %collective-permute-start.4) | collective-permute-done | bytes 1048864 | tf_op jit(solution)/shard_map/ppermute | solution.py:175
  30.6 3.5 %collective-permute-start.5 = (bf16[4097,128]{1,0:T(8,128)(2,1)}, bf16[4097,128]{1,0:T(8,128)(2,1)S(1)}, u32[]{:S(2)}, u32[]{:S(2)}) collective-permute-start(bf16[4097,128]{1,0:T(8,128)(2,1)} %collective-permute-done.4.refs_2_), channel_id=1, source_target_pairs={{0,224},{32,0},{64,32},{96,64},{128,96},{160,128},{192,160},{224,1... | collective-permute-start | bytes 3146504 | tf_op jit(solution)/shard_map/ppermute | solution.py:175
  34.2 0.1 broadcast_select_fusion
  34.3 0.1 convert_element_type.38
  34.4 0.7 slice.60.p_ref
  35.1 1.1 slice.67.p_ref
  36.2 0.7 and_reduce_fusion
  36.9 0.1 select_reduce_fusion.2
  37.0 0.2 convert_reduce_fusion.1
  37.2 18.3 %collective-permute-done.5.refs_4_ = bf16[4097,128]{1,0:T(8,128)(2,1)S(1)} collective-permute-done((bf16[4097,128]{1,0:T(8,128)(2,1)}, bf16[4097,128]{1,0:T(8,128)(2,1)S(1)}, u32[]{:S(2)}, u32[]{:S(2)}) %collective-permute-start.5) | collective-permute-done | bytes 1048864 | tf_op jit(solution)/shard_map/ppermute | solution.py:175
  55.5 3.3 %collective-permute-start.6 = (bf16[4097,128]{1,0:T(8,128)(2,1)S(1)}, bf16[4097,128]{1,0:T(8,128)(2,1)S(1)}, u32[]{:S(2)}, u32[]{:S(2)}) collective-permute-start(bf16[4097,128]{1,0:T(8,128)(2,1)S(1)} %collective-permute-done.5.refs_4_), channel_id=1, source_target_pairs={{0,224},{32,0},{64,32},{96,64},{128,96},{160,128},{192,160},{224,1... | collective-permute-start | bytes 3146504 | tf_op jit(solution)/shard_map/ppermute | solution.py:175
  58.8 0.5 multiply_add_fusion.pos_ref
  59.3 0.7 slice_bitcast_fusion.4
  60.0 0.7 slice_bitcast_fusion.5
  60.7 0.7 slice_bitcast_fusion.3
  61.3 17.6 %collective-permute-done.6.refs_6_ = bf16[4097,128]{1,0:T(8,128)(2,1)S(1)} collective-permute-done((bf16[4097,128]{1,0:T(8,128)(2,1)S(1)}, bf16[4097,128]{1,0:T(8,128)(2,1)S(1)}, u32[]{:S(2)}, u32[]{:S(2)}) %collective-permute-start.6) | collective-permute-done | bytes 1048864 | tf_op jit(solution)/shard_map/ppermute | solution.py:175
  79.0 0.9 slice.58
  79.9 3.4 %collective-permute-start.7 = (bf16[2049,128]{1,0:T(8,128)(2,1)}, bf16[2049,128]{1,0:T(8,128)(2,1)}, u32[]{:S(2)}, u32[]{:S(2)}) collective-permute-start(bf16[2049,128]{1,0:T(8,128)(2,1)} %slice.58), channel_id=1, source_target_pairs={{0,224},{32,0},{64,32},{96,64},{128,96},{160,128},{192,160},{224,1... | collective-permute-start | bytes 1573640 | tf_op jit(solution)/shard_map/ppermute | solution.py:182
  83.3 1.0 pad_maximum_fusion
  84.3 0.1 copy-done.2
  84.5 0.1 concatenate.36
  84.6 0.6 convert_element_type.39.pat_ref
  85.2 6.2 %shard_map.64.refs_2_ = f32[64,64,128]{2,1,0:T(8,128)} custom-call(s32[32]{0:T(128)} %multiply_add_fusion.pos_ref, s32[224]{0:T(256)} %convert_element_type.39.pat_ref, bf16[64,7168]{1,0:T(8,128)(2,1)} %slice.67.p_ref, bf16[4097,128]{1,0:T(8,128)(2,1)} %copy-done, bf16[4097,128]{1,0:T(8,128)(2,1)} %collective-permute-done.refs_1_, ...), custom_call_target="tpu_custom_call" | custom-call | flops 469762048 | bytes 10354688 | tf_op jit(solution)/shard_map/pallas_call | solution.py:88
  91.4 0.3 collective-permute-done.7.refs_1_
  91.7 0.7 slice_bitcast_fusion.6
  92.4 3.3 %collective-permute-done.3.refs_0_ = bf16[2049,128]{1,0:T(8,128)(2,1)S(1)} collective-permute-done((bf16[2049,128]{1,0:T(8,128)(2,1)}, bf16[2049,128]{1,0:T(8,128)(2,1)S(1)}, u32[]{:S(2)}, u32[]{:S(2)}) %collective-permute-start.3) | collective-permute-done | bytes 524576 | tf_op jit(solution)/shard_map/ppermute | solution.py:181
  95.7 0.8 maximum_convert_fusion.pat_ref
  96.5 4.4 %shard_map.65 = f32[64,64,128]{2,1,0:T(8,128)} custom-call(s32[32]{0:T(128)} %multiply_add_fusion.pos_ref, s32[32]{0:T(128)} %maximum_convert_fusion.pat_ref, bf16[64,1024]{1,0:T(8,128)(2,1)} %slice.60.p_ref, bf16[2049,128]{1,0:T(8,128)(2,1)} %copy-done.5, bf16[2049,128]{1,0:T(8,128)(2,1)} %collective-permute-done.7.refs_1_, f32[64,64,128]{2,1,0:T(8,128)} %shard_map.64.refs_2_), custom_call_target="tpu_custom_call" | custom-call | flops 67108864 | bytes 5373952 | tf_op jit(solution)/shard_map/pallas_call | solution.py:88
  100.9 11.5 %all-to-all-start = ((f32[64,64,128]{2,1,0:T(8,128)}), f32[64,64,128]{2,1,0:T(8,128)S(1)}, u32[]{:S(2)}, u32[]{:S(2)}) async-start(f32[64,64,128]{2,1,0:T(8,128)} %shard_map.65), calls=%async_computation | async-start | bytes 4194304 | tf_op jit(solution)/shard_map/all_to_all | solution.py:204
  112.4 0.6 dynamic_slice.10
  113.0 0.6 iota_compare_fusion.5
  113.7 0.8 fusion.4
  114.5 0.6 convert_reduce_fusion
  115.1 0.1 fusion.6
  115.2 0.8 select_reduce_fusion
  116.0 0.1 select_reduce_fusion.1
  116.1 0.1 copy.22
  116.2 0.1 select_n.84
  116.3 24.6 %all-to-all-done = f32[64,64,128]{2,1,0:T(8,128)S(1)} async-done(((f32[64,64,128]{2,1,0:T(8,128)}), f32[64,64,128]{2,1,0:T(8,128)S(1)}, u32[]{:S(2)}, u32[]{:S(2)}) %all-to-all-start) | async-done | bytes 2097184 | tf_op jit(solution)/shard_map/all_to_all | solution.py:204
  141.0 2.2 %fusion.1 = f32[36,64,128]{2,0,1:T(8,128)S(1)} fusion(f32[64,64,128]{2,1,0:T(8,128)S(1)} %all-to-all-done, s32[64]{0:T(128)S(1)} %select_n.84), kind=kOutput, calls=%fused_computation.3 | convolution fusion | flops 226494720 | bytes 3277056 | tf_op jit(solution)/shard_map/ce,etb->ctb/dot_general | solution.py:208
  143.1 1.2 copy.28
  (43 shorter events, 0.6 us)
Async XLA Ops:
  0.9 8.1 %copy-start.4 = (bf16[64,8192]{1,0:T(8,128)(2,1)S(1)}, bf16[64,8192]{1,0:T(8,128)(2,1)}, u32[]{:S(2)}) copy-start(bf16[64,8192]{1,0:T(8,128)(2,1)} %param.6) | copy-start | bytes 3145732
  2.3 6.8 %copy-start = (bf16[4097,128]{1,0:T(8,128)(2,1)}, bf16[4097,128]{1,0:T(8,128)(2,1)S(1)}, u32[]{:S(2)}) copy-start(bf16[4097,128]{1,0:T(8,128)(2,1)S(1)} %fusion.3.refs_0_) | copy-start | bytes 3146500
  2.3 28.4 %collective-permute-start.4 = (bf16[4097,128]{1,0:T(8,128)(2,1)S(1)}, bf16[4097,128]{1,0:T(8,128)(2,1)}, u32[]{:S(2)}, u32[]{:S(2)}) collective-permute-start(bf16[4097,128]{1,0:T(8,128)(2,1)S(1)} %fusion.3.refs_0_), channel_id=1, source_target_pairs={{0,224},{32,0},{64,32},{96,64},{128,96},{160,128},{192,160},{224,1... | collective-permute-start | bytes 3146504 | tf_op jit(solution)/shard_map/ppermute | solution.py:175
  8.7 25.4 %collective-permute-start = (bf16[4097,128]{1,0:T(8,128)(2,1)S(1)}, bf16[4097,128]{1,0:T(8,128)(2,1)}, u32[]{:S(2)}, u32[]{:S(2)}) collective-permute-start(bf16[4097,128]{1,0:T(8,128)(2,1)S(1)} %fusion.3.refs_0_), channel_id=1, source_target_pairs={{0,32},{32,64},{64,96},{96,128},{128,160},{160,192},{192,224},{224... | collective-permute-start | bytes 3146504 | tf_op jit(solution)/shard_map/ppermute | solution.py:174
  30.6 24.9 %collective-permute-start.5 = (bf16[4097,128]{1,0:T(8,128)(2,1)}, bf16[4097,128]{1,0:T(8,128)(2,1)S(1)}, u32[]{:S(2)}, u32[]{:S(2)}) collective-permute-start(bf16[4097,128]{1,0:T(8,128)(2,1)} %collective-permute-done.4.refs_2_), channel_id=1, source_target_pairs={{0,224},{32,0},{64,32},{96,64},{128,96},{160,128},{192,160},{224,1... | collective-permute-start | bytes 3146504 | tf_op jit(solution)/shard_map/ppermute | solution.py:175
  34.2 24.7 %collective-permute-start.1 = (bf16[4097,128]{1,0:T(8,128)(2,1)}, bf16[4097,128]{1,0:T(8,128)(2,1)}, u32[]{:S(2)}, u32[]{:S(2)}) collective-permute-start(bf16[4097,128]{1,0:T(8,128)(2,1)} %collective-permute-done.refs_1_), channel_id=1, source_target_pairs={{0,32},{32,64},{64,96},{96,128},{128,160},{160,192},{192,224},{224... | collective-permute-start | bytes 3146504 | tf_op jit(solution)/shard_map/ppermute | solution.py:174
  34.4 1.7 %copy-start.6 = (s32[32,32]{1,0:T(8,128)S(1)}, s32[32,32]{1,0:T(8,128)}, u32[]{:S(2)}) copy-start(s32[32,32]{1,0:T(8,128)} %param.9) | copy-start | bytes 12292
  34.4 1.8 %copy-start.8 = (s32[32]{0:T(128)S(1)}, s32[32]{0:T(128)}, u32[]{:S(2)}) copy-start(s32[32]{0:T(128)} %param.11) | copy-start | bytes 388
  34.4 1.8 %copy-start.7 = (s32[32,36]{1,0:T(8,128)S(1)}, s32[32,36]{1,0:T(8,128)}, u32[]{:S(2)}) copy-start(s32[32,36]{1,0:T(8,128)} %param.10) | copy-start | bytes 13828
  55.5 27.8 %copy-start.3 = (bf16[4097,128]{1,0:T(8,128)(2,1)}, bf16[4097,128]{1,0:T(8,128)(2,1)S(1)}, u32[]{:S(2)}) copy-start(bf16[4097,128]{1,0:T(8,128)(2,1)S(1)} %collective-permute-done.5.refs_4_) | copy-start | bytes 3146500
  55.5 23.5 %collective-permute-start.6 = (bf16[4097,128]{1,0:T(8,128)(2,1)S(1)}, bf16[4097,128]{1,0:T(8,128)(2,1)S(1)}, u32[]{:S(2)}, u32[]{:S(2)}) collective-permute-start(bf16[4097,128]{1,0:T(8,128)(2,1)S(1)} %collective-permute-done.5.refs_4_), channel_id=1, source_target_pairs={{0,224},{32,0},{64,32},{96,64},{128,96},{160,128},{192,160},{224,1... | collective-permute-start | bytes 3146504 | tf_op jit(solution)/shard_map/ppermute | solution.py:175
  58.8 24.5 %collective-permute-start.2 = (bf16[4097,128]{1,0:T(8,128)(2,1)}, bf16[4097,128]{1,0:T(8,128)(2,1)S(1)}, u32[]{:S(2)}, u32[]{:S(2)}) collective-permute-start(bf16[4097,128]{1,0:T(8,128)(2,1)} %collective-permute-done.1.refs_3_), channel_id=1, source_target_pairs={{0,32},{32,64},{64,96},{96,128},{128,160},{160,192},{192,224},{224... | collective-permute-start | bytes 3146504 | tf_op jit(solution)/shard_map/ppermute | solution.py:174
  79.0 5.3 %copy-start.1 = (bf16[4097,128]{1,0:T(8,128)(2,1)}, bf16[4097,128]{1,0:T(8,128)(2,1)S(1)}, u32[]{:S(2)}) copy-start(bf16[4097,128]{1,0:T(8,128)(2,1)S(1)} %collective-permute-done.6.refs_6_) | copy-start | bytes 3146500
  79.9 11.8 %collective-permute-start.7 = (bf16[2049,128]{1,0:T(8,128)(2,1)}, bf16[2049,128]{1,0:T(8,128)(2,1)}, u32[]{:S(2)}, u32[]{:S(2)}) collective-permute-start(bf16[2049,128]{1,0:T(8,128)(2,1)} %slice.58), channel_id=1, source_target_pairs={{0,224},{32,0},{64,32},{96,64},{128,96},{160,128},{192,160},{224,1... | collective-permute-start | bytes 1573640 | tf_op jit(solution)/shard_map/ppermute | solution.py:182
  83.3 1.2 copy-start.2
  84.3 11.4 %collective-permute-start.3 = (bf16[2049,128]{1,0:T(8,128)(2,1)}, bf16[2049,128]{1,0:T(8,128)(2,1)S(1)}, u32[]{:S(2)}, u32[]{:S(2)}) collective-permute-start(bf16[2049,128]{1,0:T(8,128)(2,1)} %pad_maximum_fusion), channel_id=1, source_target_pairs={{0,32},{32,64},{64,96},{96,128},{128,160},{160,192},{192,224},{224... | collective-permute-start | bytes 1573640 | tf_op jit(solution)/shard_map/ppermute | solution.py:181
  95.7 0.8 copy-start.5
  100.9 40.0 %all-to-all-start = ((f32[64,64,128]{2,1,0:T(8,128)}), f32[64,64,128]{2,1,0:T(8,128)S(1)}, u32[]{:S(2)}, u32[]{:S(2)}) async-start(f32[64,64,128]{2,1,0:T(8,128)} %shard_map.65), calls=%async_computation | async-start | bytes 4194304 | tf_op jit(solution)/shard_map/all_to_all | solution.py:204

commit v13 on v11

--- a/solution.py
+++ b/solution.py
@@ -203,7 +203,14 @@
                      [sizes[i] for i in tail], kp, n_pos, 0, packed)
     received = lax.all_to_all(packed, "owner", split_axis=0, concat_axis=0, tiled=True)
     dest = receive_slots(panel_list, owner_list, owner_count, own_index, slot_count)
-    return collect(dest, received, capacity)
+    hi = lax.reduce_precision(received, exponent_bits=8, mantissa_bits=7)
+    rest = received - hi
+    mid = lax.reduce_precision(rest, exponent_bits=8, mantissa_bits=7)
+    parts = jnp.concatenate([hi, mid, rest - mid], axis=0).astype(jnp.bfloat16)
+    slots = jnp.arange(capacity, dtype=jnp.int32)
+    onehot = (slots[:, None] == dest[None, :]).astype(jnp.bfloat16)
+    onehot = jnp.concatenate([onehot] * 3, axis=1)
+    return jnp.einsum("ce,etb->ctb", onehot, parts, preferred_element_type=jnp.float32)
 
 
 def solution(mesh):

time: 146 us -> 146 us (level)
  Pallas kernels: 14 us -> 10.7 us
  matrix products: 0 us -> 1.94 us
    pallas_call x1 -> x0, Pallas kernels: 3.35 us -> none  [collect(): pl.pallas_call(functools.partial(collect_kernel, n_rows, n_chunks), out_s...]
    dot_general x0 -> x1, matrix products: none -> 1.94 us  [body(): jnp.einsum('ce,etb->ctb', onehot, parts, preferred_element_type=jnp.float32)]
    unnamed x22 -> x18, local copies, waits for them, and re-layouts: 1.66 us -> 0.13 us
where the time goes in v13:
time: 146 us
  waiting for transfers between devices  85 us (58%)
  starting transfers between devices  28.2 us (19%)
  Pallas kernels  10.7 us (7%)
  other arithmetic  10.3 us (7%)
  local copies, waits for them, and re-layouts  9.66 us (7%)
  matrix products  1.94 us (1%)
    ppermute x3, waiting for transfers between devices, body(): x_l = lax.ppermute(x_l, 'tm', left)  56.6 us
    all_to_all x1, waiting for transfers between devices, body(): lax.all_to_all(packed, 'owner', split_axis=0, concat_axis=0, tiled=True)  24.6 us
    ppermute x3, starting transfers between devices, body(): x_l = lax.ppermute(x_l, 'tm', left)  13.3 us
    all_to_all x1, starting transfers between devices, body(): lax.all_to_all(packed, 'owner', split_axis=0, concat_axis=0, tiled=True)  11.5 us
    pallas_call x2, Pallas kernels, project(): pl.pallas_call(functools.partial(project_kernel, tuple(sizes), kp, block_...  10.7 us
    squeeze x8, local copies, waits for them, and re-layouts, pattern_of(): rows = [pieces[i][-1, lane_at[i]:lane_at[i] + sizes[i] * kp] for i in group]  3.44 us
    ppermute x1, starting transfers between devices, body(): h_l = lax.ppermute(x_l[h_rows:], 'tm', left)  3.41 us
    ppermute x1, waiting for transfers between devices, body(): lax.ppermute(jnp.concatenate([x_r[:h_rows], x_r[w_rows:]], axis=0), 'tm',...  3.35 us
  transfers between devices with their start and end apart: 9, of which 6 were waited for; matrix products, arithmetic and copies ran while one was open for 10% of the time, Pallas kernels for 4%

profile of v13, /device:TPU:1, one launch (start us, length us, event | category | flops | bytes accessed | tf_op | source)
XLA Modules:
  0.0 146.0 jit_solution(17076831999076228368)
XLA Ops:
  0.0 0.8 convert_element_type.36
  0.8 0.1 copy.23
  1.0 1.3 fusion.4.refs_0_
  2.3 6.5 %collective-permute-start.4 = (bf16[4097,128]{1,0:T(8,128)(2,1)S(1)}, bf16[4097,128]{1,0:T(8,128)(2,1)}, u32[]{:S(2)}, u32[]{:S(2)}) collective-permute-start(bf16[4097,128]{1,0:T(8,128)(2,1)S(1)} %fusion.4.refs_0_), channel_id=1, source_target_pairs={{0,224},{32,0},{64,32},{96,64},{128,96},{160,128},{192,160},{224,1... | collective-permute-start | bytes 3146504 | tf_op jit(solution)/shard_map/ppermute | solution.py:175
  9.0 0.1 stack.62
  9.2 0.6 gather_fusion
  9.9 20.7 %collective-permute-done.4.refs_2_ = bf16[4097,128]{1,0:T(8,128)(2,1)} collective-permute-done((bf16[4097,128]{1,0:T(8,128)(2,1)S(1)}, bf16[4097,128]{1,0:T(8,128)(2,1)}, u32[]{:S(2)}, u32[]{:S(2)}) %collective-permute-start.4) | collective-permute-done | bytes 1048864 | tf_op jit(solution)/shard_map/ppermute | solution.py:175
  30.6 3.5 %collective-permute-start.5 = (bf16[4097,128]{1,0:T(8,128)(2,1)}, bf16[4097,128]{1,0:T(8,128)(2,1)S(1)}, u32[]{:S(2)}, u32[]{:S(2)}) collective-permute-start(bf16[4097,128]{1,0:T(8,128)(2,1)} %collective-permute-done.4.refs_2_), channel_id=1, source_target_pairs={{0,224},{32,0},{64,32},{96,64},{128,96},{160,128},{192,160},{224,1... | collective-permute-start | bytes 3146504 | tf_op jit(solution)/shard_map/ppermute | solution.py:175
  34.2 0.1 broadcast_select_fusion
  34.4 0.7 slice.60.p_ref
  35.1 1.1 slice.67.p_ref
  36.2 0.7 and_reduce_fusion
  36.9 0.1 select_reduce_fusion.2
  37.0 0.2 convert_reduce_fusion.1
  37.2 18.3 %collective-permute-done.5.refs_4_ = bf16[4097,128]{1,0:T(8,128)(2,1)S(1)} collective-permute-done((bf16[4097,128]{1,0:T(8,128)(2,1)}, bf16[4097,128]{1,0:T(8,128)(2,1)S(1)}, u32[]{:S(2)}, u32[]{:S(2)}) %collective-permute-start.5) | collective-permute-done | bytes 1048864 | tf_op jit(solution)/shard_map/ppermute | solution.py:175
  55.5 3.3 %collective-permute-start.6 = (bf16[4097,128]{1,0:T(8,128)(2,1)S(1)}, bf16[4097,128]{1,0:T(8,128)(2,1)S(1)}, u32[]{:S(2)}, u32[]{:S(2)}) collective-permute-start(bf16[4097,128]{1,0:T(8,128)(2,1)S(1)} %collective-permute-done.5.refs_4_), channel_id=1, source_target_pairs={{0,224},{32,0},{64,32},{96,64},{128,96},{160,128},{192,160},{224,1... | collective-permute-start | bytes 3146504 | tf_op jit(solution)/shard_map/ppermute | solution.py:175
  58.8 0.6 multiply_add_fusion.pos_ref
  59.4 0.7 slice_bitcast_fusion.4
  60.1 0.7 slice_bitcast_fusion.5
  60.7 0.7 slice_bitcast_fusion.3
  61.4 17.6 %collective-permute-done.6.refs_6_ = bf16[4097,128]{1,0:T(8,128)(2,1)S(1)} collective-permute-done((bf16[4097,128]{1,0:T(8,128)(2,1)S(1)}, bf16[4097,128]{1,0:T(8,128)(2,1)S(1)}, u32[]{:S(2)}, u32[]{:S(2)}) %collective-permute-start.6) | collective-permute-done | bytes 1048864 | tf_op jit(solution)/shard_map/ppermute | solution.py:175
  79.0 1.0 slice.58
  79.9 3.4 %collective-permute-start.7 = (bf16[2049,128]{1,0:T(8,128)(2,1)}, bf16[2049,128]{1,0:T(8,128)(2,1)}, u32[]{:S(2)}, u32[]{:S(2)}) collective-permute-start(bf16[2049,128]{1,0:T(8,128)(2,1)} %slice.58), channel_id=1, source_target_pairs={{0,224},{32,0},{64,32},{96,64},{128,96},{160,128},{192,160},{224,1... | collective-permute-start | bytes 1573640 | tf_op jit(solution)/shard_map/ppermute | solution.py:182
  83.4 0.9 pad_maximum_fusion.1
  84.3 0.1 concatenate.48
  84.4 0.6 convert_element_type.40.pat_ref
  85.0 6.3 %shard_map.64.refs_2_ = f32[64,64,128]{2,1,0:T(8,128)} custom-call(s32[32]{0:T(128)} %multiply_add_fusion.pos_ref, s32[224]{0:T(256)} %convert_element_type.40.pat_ref, bf16[64,7168]{1,0:T(8,128)(2,1)} %slice.67.p_ref, bf16[4097,128]{1,0:T(8,128)(2,1)} %copy-done, bf16[4097,128]{1,0:T(8,128)(2,1)} %collective-permute-done.refs_1_, ...), custom_call_target="tpu_custom_call" | custom-call | flops 469762048 | bytes 10354688 | tf_op jit(solution)/shard_map/pallas_call | solution.py:88
  91.3 0.5 collective-permute-done.7.refs_1_
  91.8 0.7 slice_bitcast_fusion.6
  92.5 3.3 %collective-permute-done.3.refs_0_ = bf16[2049,128]{1,0:T(8,128)(2,1)} collective-permute-done((bf16[2049,128]{1,0:T(8,128)(2,1)}, bf16[2049,128]{1,0:T(8,128)(2,1)}, u32[]{:S(2)}, u32[]{:S(2)}) %collective-permute-start.3) | collective-permute-done | bytes 524576 | tf_op jit(solution)/shard_map/ppermute | solution.py:181
  95.8 0.7 slice_bitcast_fusion.7
  96.5 0.6 maximum_convert_fusion.pat_ref
  97.1 4.4 %shard_map.65 = f32[64,64,128]{2,1,0:T(8,128)} custom-call(s32[32]{0:T(128)} %multiply_add_fusion.pos_ref, s32[32]{0:T(128)} %maximum_convert_fusion.pat_ref, bf16[64,1024]{1,0:T(8,128)(2,1)} %slice.60.p_ref, bf16[2049,128]{1,0:T(8,128)(2,1)} %collective-permute-done.3.refs_0_, bf16[2049,128]{1,0:T(8,128)(2,1)} %collective-permute-done.7.refs_1_, ...), custom_call_target="tpu_custom_call" | custom-call | flops 67108864 | bytes 5373952 | tf_op jit(solution)/shard_map/pallas_call | solution.py:88
  101.5 11.5 %all-to-all-start = ((f32[64,64,128]{2,1,0:T(8,128)}), f32[64,64,128]{2,1,0:T(8,128)S(1)}, u32[]{:S(2)}, u32[]{:S(2)}) async-start(f32[64,64,128]{2,1,0:T(8,128)} %shard_map.65), calls=%async_computation | async-start | bytes 4194304 | tf_op jit(solution)/shard_map/all_to_all | solution.py:204
  113.0 0.6 dynamic_slice.10
  113.6 0.6 iota_compare_fusion.5
  114.3 0.8 fusion.5
  115.1 0.6 convert_reduce_fusion
  115.7 0.1 fusion.11
  115.8 0.8 select_reduce_fusion
  116.6 0.1 select_reduce_fusion.1
  116.7 0.1 copy.22
  116.8 0.1 select_n.84
  116.9 24.6 %all-to-all-done = f32[64,64,128]{2,1,0:T(8,128)S(1)} async-done(((f32[64,64,128]{2,1,0:T(8,128)}), f32[64,64,128]{2,1,0:T(8,128)S(1)}, u32[]{:S(2)}, u32[]{:S(2)}) %all-to-all-start) | async-done | bytes 2097184 | tf_op jit(solution)/shard_map/all_to_all | solution.py:204
  141.5 0.9 reduce-precision_convert_fusion.1
  142.4 0.4 pad_maximum_fusion
  142.8 1.9 %fusion = f32[36,64,128]{2,0,1:T(8,128)S(1)} fusion(bf16[192,64,128]{2,1,0:T(8,128)(2,1)S(1)} %pad_maximum_fusion, pred[36,64]{1,0:T(8,128)(4,1)S(1)} %iota_compare_fusion.2), kind=kOutput, calls=%fused_computation.2 | convolution fusion | flops 113260032 | bytes 4327680 | tf_op jit(solution)/shard_map/ce,etb->ctb/dot_general | solution.py:213
  144.8 1.2 copy.28
  (44 shorter events, 0.8 us)
Async XLA Ops:
  0.0 8.9 %copy-start.4 = (bf16[64,8192]{1,0:T(8,128)(2,1)S(1)}, bf16[64,8192]{1,0:T(8,128)(2,1)}, u32[]{:S(2)}) copy-start(bf16[64,8192]{1,0:T(8,128)(2,1)} %param.6) | copy-start | bytes 3145732
  2.3 7.5 %copy-start = (bf16[4097,128]{1,0:T(8,128)(2,1)}, bf16[4097,128]{1,0:T(8,128)(2,1)S(1)}, u32[]{:S(2)}) copy-start(bf16[4097,128]{1,0:T(8,128)(2,1)S(1)} %fusion.4.refs_0_) | copy-start | bytes 3146500
  2.3 28.4 %collective-permute-start.4 = (bf16[4097,128]{1,0:T(8,128)(2,1)S(1)}, bf16[4097,128]{1,0:T(8,128)(2,1)}, u32[]{:S(2)}, u32[]{:S(2)}) collective-permute-start(bf16[4097,128]{1,0:T(8,128)(2,1)S(1)} %fusion.4.refs_0_), channel_id=1, source_target_pairs={{0,224},{32,0},{64,32},{96,64},{128,96},{160,128},{192,160},{224,1... | collective-permute-start | bytes 3146504 | tf_op jit(solution)/shard_map/ppermute | solution.py:175
  8.7 25.4 %collective-permute-start = (bf16[4097,128]{1,0:T(8,128)(2,1)S(1)}, bf16[4097,128]{1,0:T(8,128)(2,1)}, u32[]{:S(2)}, u32[]{:S(2)}) collective-permute-start(bf16[4097,128]{1,0:T(8,128)(2,1)S(1)} %fusion.4.refs_0_), channel_id=1, source_target_pairs={{0,32},{32,64},{64,96},{96,128},{128,160},{160,192},{192,224},{224... | collective-permute-start | bytes 3146504 | tf_op jit(solution)/shard_map/ppermute | solution.py:174
  30.6 24.9 %collective-permute-start.5 = (bf16[4097,128]{1,0:T(8,128)(2,1)}, bf16[4097,128]{1,0:T(8,128)(2,1)S(1)}, u32[]{:S(2)}, u32[]{:S(2)}) collective-permute-start(bf16[4097,128]{1,0:T(8,128)(2,1)} %collective-permute-done.4.refs_2_), channel_id=1, source_target_pairs={{0,224},{32,0},{64,32},{96,64},{128,96},{160,128},{192,160},{224,1... | collective-permute-start | bytes 3146504 | tf_op jit(solution)/shard_map/ppermute | solution.py:175
  34.2 24.7 %collective-permute-start.1 = (bf16[4097,128]{1,0:T(8,128)(2,1)}, bf16[4097,128]{1,0:T(8,128)(2,1)}, u32[]{:S(2)}, u32[]{:S(2)}) collective-permute-start(bf16[4097,128]{1,0:T(8,128)(2,1)} %collective-permute-done.refs_1_), channel_id=1, source_target_pairs={{0,32},{32,64},{64,96},{96,128},{128,160},{160,192},{192,224},{224... | collective-permute-start | bytes 3146504 | tf_op jit(solution)/shard_map/ppermute | solution.py:174
  34.3 1.8 %copy-start.5 = (s32[32,32]{1,0:T(8,128)S(1)}, s32[32,32]{1,0:T(8,128)}, u32[]{:S(2)}) copy-start(s32[32,32]{1,0:T(8,128)} %param.9) | copy-start | bytes 12292
  34.3 1.8 %copy-start.7 = (s32[32]{0:T(128)S(1)}, s32[32]{0:T(128)}, u32[]{:S(2)}) copy-start(s32[32]{0:T(128)} %param.11) | copy-start | bytes 388
  34.3 1.9 %copy-start.6 = (s32[32,36]{1,0:T(8,128)S(1)}, s32[32,36]{1,0:T(8,128)}, u32[]{:S(2)}) copy-start(s32[32,36]{1,0:T(8,128)} %param.10) | copy-start | bytes 13828
  55.5 28.8 %copy-start.3 = (bf16[4097,128]{1,0:T(8,128)(2,1)}, bf16[4097,128]{1,0:T(8,128)(2,1)S(1)}, u32[]{:S(2)}) copy-start(bf16[4097,128]{1,0:T(8,128)(2,1)S(1)} %collective-permute-done.5.refs_4_) | copy-start | bytes 3146500
  55.5 23.5 %collective-permute-start.6 = (bf16[4097,128]{1,0:T(8,128)(2,1)S(1)}, bf16[4097,128]{1,0:T(8,128)(2,1)S(1)}, u32[]{:S(2)}, u32[]{:S(2)}) collective-permute-start(bf16[4097,128]{1,0:T(8,128)(2,1)S(1)} %collective-permute-done.5.refs_4_), channel_id=1, source_target_pairs={{0,224},{32,0},{64,32},{96,64},{128,96},{160,128},{192,160},{224,1... | collective-permute-start | bytes 3146504 | tf_op jit(solution)/shard_map/ppermute | solution.py:175
  58.8 24.5 %collective-permute-start.2 = (bf16[4097,128]{1,0:T(8,128)(2,1)}, bf16[4097,128]{1,0:T(8,128)(2,1)S(1)}, u32[]{:S(2)}, u32[]{:S(2)}) collective-permute-start(bf16[4097,128]{1,0:T(8,128)(2,1)} %collective-permute-done.1.refs_3_), channel_id=1, source_target_pairs={{0,32},{32,64},{64,96},{96,128},{128,160},{160,192},{192,224},{224... | collective-permute-start | bytes 3146504 | tf_op jit(solution)/shard_map/ppermute | solution.py:174
  79.0 5.3 %copy-start.1 = (bf16[4097,128]{1,0:T(8,128)(2,1)}, bf16[4097,128]{1,0:T(8,128)(2,1)S(1)}, u32[]{:S(2)}) copy-start(bf16[4097,128]{1,0:T(8,128)(2,1)S(1)} %collective-permute-done.6.refs_6_) | copy-start | bytes 3146500
  79.9 11.8 %collective-permute-start.7 = (bf16[2049,128]{1,0:T(8,128)(2,1)}, bf16[2049,128]{1,0:T(8,128)(2,1)}, u32[]{:S(2)}, u32[]{:S(2)}) collective-permute-start(bf16[2049,128]{1,0:T(8,128)(2,1)} %slice.58), channel_id=1, source_target_pairs={{0,224},{32,0},{64,32},{96,64},{128,96},{160,128},{192,160},{224,1... | collective-permute-start | bytes 1573640 | tf_op jit(solution)/shard_map/ppermute | solution.py:182
  83.4 1.6 %copy-start.2 = (bf16[4097,128]{1,0:T(8,128)(2,1)}, bf16[4097,128]{1,0:T(8,128)(2,1)S(1)}, u32[]{:S(2)}) copy-start(bf16[4097,128]{1,0:T(8,128)(2,1)S(1)} %collective-permute-done.2.refs_5_) | copy-start | bytes 3146500
  84.3 11.5 %collective-permute-start.3 = (bf16[2049,128]{1,0:T(8,128)(2,1)}, bf16[2049,128]{1,0:T(8,128)(2,1)}, u32[]{:S(2)}, u32[]{:S(2)}) collective-permute-start(bf16[2049,128]{1,0:T(8,128)(2,1)} %pad_maximum_fusion.1), channel_id=1, source_target_pairs={{0,32},{32,64},{64,96},{96,128},{128,160},{160,192},{192,224},{224... | collective-permute-start | bytes 1573640 | tf_op jit(solution)/shard_map/ppermute | solution.py:181
  101.5 40.0 %all-to-all-start = ((f32[64,64,128]{2,1,0:T(8,128)}), f32[64,64,128]{2,1,0:T(8,128)S(1)}, u32[]{:S(2)}, u32[]{:S(2)}) async-start(f32[64,64,128]{2,1,0:T(8,128)} %shard_map.65), calls=%async_computation | async-start | bytes 4194304 | tf_op jit(solution)/shard_map/all_to_all | solution.py:204

commit v14 on v12

--- a/solution.py
+++ b/solution.py
@@ -57,9 +57,7 @@
         acc_copy.start()
     for c in copies:
         c.start()
-    if has_acc:
-        acc_copy.wait()
-    else:
+    if not has_acc:
         o_ref[...] = jnp.zeros_like(o_ref)
     base = 0
     for q in range(n):
@@ -74,6 +72,8 @@
                 axis=1,
             )
             prod = jnp.dot(rows, wide, preferred_element_type=jnp.float32)
+            if has_acc and face == 0:
+                acc_copy.wait()
             for k in range(kp):
                 pos = pos_ref[pat_ref[face * kp + k]]
                 o_ref[pos] += prod[:, k * block_len:(k + 1) * block_len]

time: 145 us -> 145 us (level)
  no operation moved by 1% of the time
where the time goes in v14:
time: 145 us
  waiting for transfers between devices  84.9 us (59%)
  starting transfers between devices  28.2 us (19%)
  Pallas kernels  10.8 us (7%)
  other arithmetic  9.2 us (6%)
  local copies, waits for them, and re-layouts  9.09 us (6%)
  matrix products  2.18 us (2%)
    ppermute x3, waiting for transfers between devices, body(): x_l = lax.ppermute(x_l, 'tm', left)  56.7 us
    all_to_all x1, waiting for transfers between devices, body(): lax.all_to_all(packed, 'owner', split_axis=0, concat_axis=0, tiled=True)  24.6 us
    ppermute x3, starting transfers between devices, body(): x_l = lax.ppermute(x_l, 'tm', left)  13.3 us
    all_to_all x1, starting transfers between devices, body(): lax.all_to_all(packed, 'owner', split_axis=0, concat_axis=0, tiled=True)  11.5 us
    pallas_call x2, Pallas kernels, project(): pl.pallas_call(functools.partial(project_kernel, tuple(sizes), kp, block_...  10.8 us
    ppermute x1, starting transfers between devices, body(): h_l = lax.ppermute(x_l[h_rows:], 'tm', left)  3.41 us
    ppermute x1, waiting for transfers between devices, body(): lax.ppermute(jnp.concatenate([x_r[:h_rows], x_r[w_rows:]], axis=0), 'tm',...  3.3 us
  transfers between devices with their start and end apart: 9, of which 6 were waited for; matrix products, arithmetic and copies ran while one was open for 10% of the time, Pallas kernels for 4%

profile of v14, /device:TPU:1, one launch (start us, length us, event | category | flops | bytes accessed | tf_op | source)
XLA Modules:
  0.0 144.5 jit_solution(7903615572942811821)
XLA Ops:
  0.0 0.7 convert_element_type.35
  0.7 0.1 copy.23
  0.8 0.1 convert_element_type.36
  0.9 1.4 fusion.3.refs_0_
  2.3 6.5 %collective-permute-start.4 = (bf16[4097,128]{1,0:T(8,128)(2,1)S(1)}, bf16[4097,128]{1,0:T(8,128)(2,1)}, u32[]{:S(2)}, u32[]{:S(2)}) collective-permute-start(bf16[4097,128]{1,0:T(8,128)(2,1)S(1)} %fusion.3.refs_0_), channel_id=1, source_target_pairs={{0,224},{32,0},{64,32},{96,64},{128,96},{160,128},{192,160},{224,1... | collective-permute-start | bytes 3146504 | tf_op jit(solution)/shard_map/ppermute | solution.py:175
  9.0 0.1 stack.62
  9.2 0.6 gather_fusion
  9.9 20.7 %collective-permute-done.4.refs_2_ = bf16[4097,128]{1,0:T(8,128)(2,1)} collective-permute-done((bf16[4097,128]{1,0:T(8,128)(2,1)S(1)}, bf16[4097,128]{1,0:T(8,128)(2,1)}, u32[]{:S(2)}, u32[]{:S(2)}) %collective-permute-start.4) | collective-permute-done | bytes 1048864 | tf_op jit(solution)/shard_map/ppermute | solution.py:175
  30.6 3.5 %collective-permute-start.5 = (bf16[4097,128]{1,0:T(8,128)(2,1)}, bf16[4097,128]{1,0:T(8,128)(2,1)S(1)}, u32[]{:S(2)}, u32[]{:S(2)}) collective-permute-start(bf16[4097,128]{1,0:T(8,128)(2,1)} %collective-permute-done.4.refs_2_), channel_id=1, source_target_pairs={{0,224},{32,0},{64,32},{96,64},{128,96},{160,128},{192,160},{224,1... | collective-permute-start | bytes 3146504 | tf_op jit(solution)/shard_map/ppermute | solution.py:175
  34.2 0.1 broadcast_select_fusion
  34.3 0.1 convert_element_type.38
  34.4 0.7 slice.60.p_ref
  35.1 1.1 slice.67.p_ref
  36.2 0.7 and_reduce_fusion
  36.9 0.1 select_reduce_fusion.2
  37.0 0.2 convert_reduce_fusion.1
  37.2 18.3 %collective-permute-done.5.refs_4_ = bf16[4097,128]{1,0:T(8,128)(2,1)S(1)} collective-permute-done((bf16[4097,128]{1,0:T(8,128)(2,1)}, bf16[4097,128]{1,0:T(8,128)(2,1)S(1)}, u32[]{:S(2)}, u32[]{:S(2)}) %collective-permute-start.5) | collective-permute-done | bytes 1048864 | tf_op jit(solution)/shard_map/ppermute | solution.py:175
  55.5 3.3 %collective-permute-start.6 = (bf16[4097,128]{1,0:T(8,128)(2,1)S(1)}, bf16[4097,128]{1,0:T(8,128)(2,1)S(1)}, u32[]{:S(2)}, u32[]{:S(2)}) collective-permute-start(bf16[4097,128]{1,0:T(8,128)(2,1)S(1)} %collective-permute-done.5.refs_4_), channel_id=1, source_target_pairs={{0,224},{32,0},{64,32},{96,64},{128,96},{160,128},{192,160},{224,1... | collective-permute-start | bytes 3146504 | tf_op jit(solution)/shard_map/ppermute | solution.py:175
  58.8 0.5 multiply_add_fusion.pos_ref
  59.3 0.7 slice_bitcast_fusion.4
  60.0 0.7 slice_bitcast_fusion.5
  60.7 0.7 slice_bitcast_fusion.3
  61.3 17.6 %collective-permute-done.6.refs_6_ = bf16[4097,128]{1,0:T(8,128)(2,1)S(1)} collective-permute-done((bf16[4097,128]{1,0:T(8,128)(2,1)S(1)}, bf16[4097,128]{1,0:T(8,128)(2,1)S(1)}, u32[]{:S(2)}, u32[]{:S(2)}) %collective-permute-start.6) | collective-permute-done | bytes 1048864 | tf_op jit(solution)/shard_map/ppermute | solution.py:175
  79.0 0.9 slice.58
  79.9 3.4 %collective-permute-start.7 = (bf16[2049,128]{1,0:T(8,128)(2,1)}, bf16[2049,128]{1,0:T(8,128)(2,1)}, u32[]{:S(2)}, u32[]{:S(2)}) collective-permute-start(bf16[2049,128]{1,0:T(8,128)(2,1)} %slice.58), channel_id=1, source_target_pairs={{0,224},{32,0},{64,32},{96,64},{128,96},{160,128},{192,160},{224,1... | collective-permute-start | bytes 1573640 | tf_op jit(solution)/shard_map/ppermute | solution.py:182
  83.3 1.0 pad_maximum_fusion
  84.3 0.1 copy-done.2
  84.5 0.1 concatenate.36
  84.6 0.6 convert_element_type.39.pat_ref
  85.2 6.3 %shard_map.64.refs_2_ = f32[64,64,128]{2,1,0:T(8,128)} custom-call(s32[32]{0:T(128)} %multiply_add_fusion.pos_ref, s32[224]{0:T(256)} %convert_element_type.39.pat_ref, bf16[64,7168]{1,0:T(8,128)(2,1)} %slice.67.p_ref, bf16[4097,128]{1,0:T(8,128)(2,1)} %copy-done, bf16[4097,128]{1,0:T(8,128)(2,1)} %collective-permute-done.refs_1_, ...), custom_call_target="tpu_custom_call" | custom-call | flops 469762048 | bytes 10354688 | tf_op jit(solution)/shard_map/pallas_call | solution.py:88
  91.4 0.3 collective-permute-done.7.refs_1_
  91.7 0.7 slice_bitcast_fusion.6
  92.4 3.3 %collective-permute-done.3.refs_0_ = bf16[2049,128]{1,0:T(8,128)(2,1)S(1)} collective-permute-done((bf16[2049,128]{1,0:T(8,128)(2,1)}, bf16[2049,128]{1,0:T(8,128)(2,1)S(1)}, u32[]{:S(2)}, u32[]{:S(2)}) %collective-permute-start.3) | collective-permute-done | bytes 524576 | tf_op jit(solution)/shard_map/ppermute | solution.py:181
  95.7 0.8 maximum_convert_fusion.pat_ref
  96.5 4.5 %shard_map.65 = f32[64,64,128]{2,1,0:T(8,128)} custom-call(s32[32]{0:T(128)} %multiply_add_fusion.pos_ref, s32[32]{0:T(128)} %maximum_convert_fusion.pat_ref, bf16[64,1024]{1,0:T(8,128)(2,1)} %slice.60.p_ref, bf16[2049,128]{1,0:T(8,128)(2,1)} %copy-done.5, bf16[2049,128]{1,0:T(8,128)(2,1)} %collective-permute-done.7.refs_1_, f32[64,64,128]{2,1,0:T(8,128)} %shard_map.64.refs_2_), custom_call_target="tpu_custom_call" | custom-call | flops 67108864 | bytes 5373952 | tf_op jit(solution)/shard_map/pallas_call | solution.py:88
  101.1 11.5 %all-to-all-start = ((f32[64,64,128]{2,1,0:T(8,128)}), f32[64,64,128]{2,1,0:T(8,128)S(1)}, u32[]{:S(2)}, u32[]{:S(2)}) async-start(f32[64,64,128]{2,1,0:T(8,128)} %shard_map.65), calls=%async_computation | async-start | bytes 4194304 | tf_op jit(solution)/shard_map/all_to_all | solution.py:204
  112.6 0.6 dynamic_slice.10
  113.2 0.6 iota_compare_fusion.5
  113.8 0.8 fusion.4
  114.6 0.6 convert_reduce_fusion
  115.3 0.1 fusion.6
  115.4 0.8 select_reduce_fusion
  116.2 0.1 select_reduce_fusion.1
  116.3 0.1 copy.22
  116.4 0.1 select_n.84
  116.5 24.6 %all-to-all-done = f32[64,64,128]{2,1,0:T(8,128)S(1)} async-done(((f32[64,64,128]{2,1,0:T(8,128)}), f32[64,64,128]{2,1,0:T(8,128)S(1)}, u32[]{:S(2)}, u32[]{:S(2)}) %all-to-all-start) | async-done | bytes 2097184 | tf_op jit(solution)/shard_map/all_to_all | solution.py:204
  141.1 2.2 %fusion.1 = f32[36,64,128]{2,0,1:T(8,128)S(1)} fusion(f32[64,64,128]{2,1,0:T(8,128)S(1)} %all-to-all-done, s32[64]{0:T(128)S(1)} %select_n.84), kind=kOutput, calls=%fused_computation.3 | convolution fusion | flops 226494720 | bytes 3277056 | tf_op jit(solution)/shard_map/ce,etb->ctb/dot_general | solution.py:208
  143.3 1.2 copy.28
  (43 shorter events, 0.6 us)
Async XLA Ops:
  0.9 8.1 %copy-start.4 = (bf16[64,8192]{1,0:T(8,128)(2,1)S(1)}, bf16[64,8192]{1,0:T(8,128)(2,1)}, u32[]{:S(2)}) copy-start(bf16[64,8192]{1,0:T(8,128)(2,1)} %param.6) | copy-start | bytes 3145732
  2.3 6.8 %copy-start = (bf16[4097,128]{1,0:T(8,128)(2,1)}, bf16[4097,128]{1,0:T(8,128)(2,1)S(1)}, u32[]{:S(2)}) copy-start(bf16[4097,128]{1,0:T(8,128)(2,1)S(1)} %fusion.3.refs_0_) | copy-start | bytes 3146500
  2.3 28.4 %collective-permute-start.4 = (bf16[4097,128]{1,0:T(8,128)(2,1)S(1)}, bf16[4097,128]{1,0:T(8,128)(2,1)}, u32[]{:S(2)}, u32[]{:S(2)}) collective-permute-start(bf16[4097,128]{1,0:T(8,128)(2,1)S(1)} %fusion.3.refs_0_), channel_id=1, source_target_pairs={{0,224},{32,0},{64,32},{96,64},{128,96},{160,128},{192,160},{224,1... | collective-permute-start | bytes 3146504 | tf_op jit(solution)/shard_map/ppermute | solution.py:175
  8.7 25.4 %collective-permute-start = (bf16[4097,128]{1,0:T(8,128)(2,1)S(1)}, bf16[4097,128]{1,0:T(8,128)(2,1)}, u32[]{:S(2)}, u32[]{:S(2)}) collective-permute-start(bf16[4097,128]{1,0:T(8,128)(2,1)S(1)} %fusion.3.refs_0_), channel_id=1, source_target_pairs={{0,32},{32,64},{64,96},{96,128},{128,160},{160,192},{192,224},{224... | collective-permute-start | bytes 3146504 | tf_op jit(solution)/shard_map/ppermute | solution.py:174
  30.6 24.9 %collective-permute-start.5 = (bf16[4097,128]{1,0:T(8,128)(2,1)}, bf16[4097,128]{1,0:T(8,128)(2,1)S(1)}, u32[]{:S(2)}, u32[]{:S(2)}) collective-permute-start(bf16[4097,128]{1,0:T(8,128)(2,1)} %collective-permute-done.4.refs_2_), channel_id=1, source_target_pairs={{0,224},{32,0},{64,32},{96,64},{128,96},{160,128},{192,160},{224,1... | collective-permute-start | bytes 3146504 | tf_op jit(solution)/shard_map/ppermute | solution.py:175
  34.2 24.7 %collective-permute-start.1 = (bf16[4097,128]{1,0:T(8,128)(2,1)}, bf16[4097,128]{1,0:T(8,128)(2,1)}, u32[]{:S(2)}, u32[]{:S(2)}) collective-permute-start(bf16[4097,128]{1,0:T(8,128)(2,1)} %collective-permute-done.refs_1_), channel_id=1, source_target_pairs={{0,32},{32,64},{64,96},{96,128},{128,160},{160,192},{192,224},{224... | collective-permute-start | bytes 3146504 | tf_op jit(solution)/shard_map/ppermute | solution.py:174
  34.4 1.7 %copy-start.6 = (s32[32,32]{1,0:T(8,128)S(1)}, s32[32,32]{1,0:T(8,128)}, u32[]{:S(2)}) copy-start(s32[32,32]{1,0:T(8,128)} %param.9) | copy-start | bytes 12292
  34.4 1.8 %copy-start.8 = (s32[32]{0:T(128)S(1)}, s32[32]{0:T(128)}, u32[]{:S(2)}) copy-start(s32[32]{0:T(128)} %param.11) | copy-start | bytes 388
  34.4 1.8 %copy-start.7 = (s32[32,36]{1,0:T(8,128)S(1)}, s32[32,36]{1,0:T(8,128)}, u32[]{:S(2)}) copy-start(s32[32,36]{1,0:T(8,128)} %param.10) | copy-start | bytes 13828
  55.5 27.8 %copy-start.3 = (bf16[4097,128]{1,0:T(8,128)(2,1)}, bf16[4097,128]{1,0:T(8,128)(2,1)S(1)}, u32[]{:S(2)}) copy-start(bf16[4097,128]{1,0:T(8,128)(2,1)S(1)} %collective-permute-done.5.refs_4_) | copy-start | bytes 3146500
  55.5 23.5 %collective-permute-start.6 = (bf16[4097,128]{1,0:T(8,128)(2,1)S(1)}, bf16[4097,128]{1,0:T(8,128)(2,1)S(1)}, u32[]{:S(2)}, u32[]{:S(2)}) collective-permute-start(bf16[4097,128]{1,0:T(8,128)(2,1)S(1)} %collective-permute-done.5.refs_4_), channel_id=1, source_target_pairs={{0,224},{32,0},{64,32},{96,64},{128,96},{160,128},{192,160},{224,1... | collective-permute-start | bytes 3146504 | tf_op jit(solution)/shard_map/ppermute | solution.py:175
  58.8 24.5 %collective-permute-start.2 = (bf16[4097,128]{1,0:T(8,128)(2,1)}, bf16[4097,128]{1,0:T(8,128)(2,1)S(1)}, u32[]{:S(2)}, u32[]{:S(2)}) collective-permute-start(bf16[4097,128]{1,0:T(8,128)(2,1)} %collective-permute-done.1.refs_3_), channel_id=1, source_target_pairs={{0,32},{32,64},{64,96},{96,128},{128,160},{160,192},{192,224},{224... | collective-permute-start | bytes 3146504 | tf_op jit(solution)/shard_map/ppermute | solution.py:174
  79.0 5.3 %copy-start.1 = (bf16[4097,128]{1,0:T(8,128)(2,1)}, bf16[4097,128]{1,0:T(8,128)(2,1)S(1)}, u32[]{:S(2)}) copy-start(bf16[4097,128]{1,0:T(8,128)(2,1)S(1)} %collective-permute-done.6.refs_6_) | copy-start | bytes 3146500
  79.9 11.8 %collective-permute-start.7 = (bf16[2049,128]{1,0:T(8,128)(2,1)}, bf16[2049,128]{1,0:T(8,128)(2,1)}, u32[]{:S(2)}, u32[]{:S(2)}) collective-permute-start(bf16[2049,128]{1,0:T(8,128)(2,1)} %slice.58), channel_id=1, source_target_pairs={{0,224},{32,0},{64,32},{96,64},{128,96},{160,128},{192,160},{224,1... | collective-permute-start | bytes 1573640 | tf_op jit(solution)/shard_map/ppermute | solution.py:182
  83.3 1.2 copy-start.2
  84.3 11.4 %collective-permute-start.3 = (bf16[2049,128]{1,0:T(8,128)(2,1)}, bf16[2049,128]{1,0:T(8,128)(2,1)S(1)}, u32[]{:S(2)}, u32[]{:S(2)}) collective-permute-start(bf16[2049,128]{1,0:T(8,128)(2,1)} %pad_maximum_fusion), channel_id=1, source_target_pairs={{0,32},{32,64},{64,96},{96,128},{128,160},{160,192},{192,224},{224... | collective-permute-start | bytes 1573640 | tf_op jit(solution)/shard_map/ppermute | solution.py:181
  95.7 0.8 copy-start.5
  101.1 40.0 %all-to-all-start = ((f32[64,64,128]{2,1,0:T(8,128)}), f32[64,64,128]{2,1,0:T(8,128)S(1)}, u32[]{:S(2)}, u32[]{:S(2)}) async-start(f32[64,64,128]{2,1,0:T(8,128)} %shard_map.65), calls=%async_computation | async-start | bytes 4194304 | tf_op jit(solution)/shard_map/all_to_all | solution.py:204
